TPU v7x, 768 devices: a whole 4x8x12 slice. The times are simulated.
768 devices in a mesh: dp: 24 (over z, y_lo), tm: 16 (over x, y_hi), rows: 2 (over core).
Axes of the slice: x: 4, y: 8 (y_hi: 4, y_lo: 2; y = y_hi * 2 + y_lo), z: 12, core: 2. Of those that a mesh axis runs over, the one named last changes fastest.
Arguments:
- queries: bfloat16 [24, 16, 1, 1, 384, 1536], P('dp', 'tm', None, None, None, 'rows'), may hold values from -44 to 44
- keys_values: bfloat16 [24, 16, 1, 1, 384, 2, 1536], P('dp', 'tm', None, None, None, None, 'rows'), may hold values from -5 to 5
- window_offsets: int32 [24, 16, 1, 1, 3], P('dp', 'tm'), may hold values from 0 to 26, as said below
- out_weight: bfloat16 [1536, 1536], P(('rows', 'dp')), may hold values from -0.15625 to 0.15625
- gate: float32 [24, 1536], P('dp'), may hold values from 3 to 30
Outputs:
- mixed: bfloat16 [24, 16, 1, 1, 384, 1536], P('dp', 'tm', None, None, 'rows')
Inputs may be any that keep to these rules, and one draw needn't show every extreme that they name: `window_offsets`: entry 0 of every row is 13; the other 2 entries are distinct offsets other than 13, which may point outside the grid.
All inputs are finite; a program needn't handle non-finite values.
Results may differ from a plain program's by a relative error of at most 0.015.
Values may be sent and summed in bfloat16 or wider, within the bound.
No kernel may reach another device: no remote copies, remote signals or barrier semaphores. Data moves between devices by JAX's collectives and lax.ppermute only.
A program may use at most 64 MiB of HBM per device.

v0:
```python
import jax
import jax.numpy as jnp
from jax import lax
from jax.sharding import PartitionSpec as P

HD = 128
DOUT = 1536


def with_halo(block, sides, width):
    for axis, dim in sides:
        count = lax.axis_size(axis)
        forward = [(i, i + 1) for i in range(count - 1)]
        backward = [(target, source) for source, target in forward]
        low = lax.ppermute(
            lax.slice_in_dim(block, block.shape[dim] - width, None, axis=dim), axis, forward
        )
        high = lax.ppermute(lax.slice_in_dim(block, 0, width, axis=dim), axis, backward)
        block = jnp.concatenate([low, block, high], axis=dim)
    return block


def local(queries, keys_values, window_offsets, out_weight, gate):
    nht = queries.shape[2]
    wt = queries.shape[3]
    tl = queries.shape[4]
    local_width = queries.shape[5]
    local_heads = local_width // HD
    tiles = nht * wt
    keep = window_offsets.shape[4]
    scale = float(HD) ** (-0.5)
    extended = with_halo(keys_values, (("tm", 1),), 1)
    ext_flat = extended[0].reshape(3 * tiles, tl, 2, local_width)
    offsets = window_offsets[0, 0]
    all_time = lax.axis_size("tm")
    time_now = lax.axis_index("tm")
    row_pos = jnp.arange(nht, dtype=jnp.int32)[:, None, None]
    col_pos = jnp.arange(wt, dtype=jnp.int32)[None, :, None]
    first = offsets // 9
    near_t = time_now + first - 1
    near_h = row_pos + offsets // 3 % 3 - 1
    near_w = col_pos + offsets % 3 - 1
    inside = (
        (near_t >= 0)
        & (near_t < all_time)
        & (near_h >= 0)
        & (near_h < nht)
        & (near_w >= 0)
        & (near_w < wt)
    )
    index = first * tiles + jnp.clip(near_h, 0, nht - 1) * wt + jnp.clip(near_w, 0, wt - 1)
    index = index.reshape(tiles, keep)
    inside = inside.reshape(tiles, keep)
    q_flat = queries[0, 0].reshape(tiles, tl, local_heads, HD)

    def per_tile(items):
        query_tile, index_row, live_row = items
        key_tiles = jnp.take(ext_flat, index_row, axis=0)
        keys = key_tiles[:, :, 0, :].reshape(keep * tl, local_heads, HD)
        values = key_tiles[:, :, 1, :].reshape(keep * tl, local_heads, HD)
        scores = (
            jnp.einsum("qnd,knd->nqk", query_tile, keys, preferred_element_type=jnp.float32) * scale
        )
        mask = jnp.repeat(live_row, tl)[None, None, :]
        top = jnp.max(jnp.where(mask, scores, -jnp.inf), axis=2, keepdims=True)
        prob = jnp.where(mask, jnp.exp(scores - top), 0.0)
        total = jnp.sum(prob, axis=2, keepdims=True)
        weights = (prob / total).astype(jnp.bfloat16)
        acc = jnp.einsum("nqk,knd->qnd", weights, values, preferred_element_type=jnp.float32)
        return acc.astype(jnp.bfloat16).reshape(tl, local_width)

    attended = lax.map(per_tile, (q_flat, index, inside))
    bands = lax.axis_size("rows")
    band = tl // bands
    reordered = (
        attended.reshape(tiles, bands, band, local_width)
        .transpose(1, 0, 2, 3)
        .reshape(tiles * tl, local_width)
    )
    head_rows = lax.all_gather(out_weight, "dp", axis=0, tiled=True)
    projection = lax.psum_scatter(
        jnp.dot(reordered, head_rows, preferred_element_type=jnp.float32),
        "rows",
        scatter_dimension=0,
        tiled=True,
    )
    mixed = (gate[0][None, :] * projection).astype(jnp.bfloat16)
    return mixed.reshape(1, 1, nht, wt, band, DOUT)


def solution(mesh):
    placed = (
        P("dp", "tm", None, None, None, "rows"),
        P("dp", "tm", None, None, None, None, "rows"),
        P("dp", "tm", None, None, None),
        P(("rows", "dp"), None),
        P("dp", None),
    )
    return jax.shard_map(
        local,
        mesh=mesh,
        in_specs=placed,
        out_specs=P("dp", "tm", None, None, "rows", None),
        check_vma=False,
    )
```

profile of v0, /device:TPU:1, one launch (start us, length us, event | category | flops | bytes accessed | tf_op | source)
XLA Modules:
  0.0 197.3 jit_solution(13249731325557714642)
XLA Ops:
  6.5 0.0 all-gather.2.cloned.1.call-start
  6.5 5.1 %collective-permute-start = (bf16[1,1,1,1,384,2,768]{6,5,4,3,2,1,0:T(2,128)(2,1)}, bf16[1,1,1,1,384,2,768]{6,5,4,3,2,1,0:T(2,128)(2,1)S(1)}, u32[]{:S(2)}, u32[]{:S(2)}) collective-permute-start(bf16[1,1,1,1,384,2,768]{6,5,4,3,2,1,0:T(2,128)(2,1)} %param.6), channel_id=1, source_target_pairs={{0,2},{2,4},{4,6},{6,8},{8,10},{10,12},{12,14},{14,16},{16,18},{18... | collective-permute-start | bytes 3538952 | tf_op jit(solution)/shard_map/ppermute | solution.py:15
  11.7 1.3 collective-permute-start.1
  13.0 0.0 all-gather.2.cloned.1.call-update
  13.0 0.0 reduce-scatter.2.cloned.1.call-start
  13.0 2.1 %copy.9 = bf16[1,1,1,1,384,768]{4,5,3,2,1,0:T(8,128)(2,1)} copy(bf16[1,1,1,1,384,768]{5,4,3,2,1,0:T(8,128)(2,1)} %param.5) | data formatting | bytes 1179648 | tf_op args[0]
  15.2 0.7 compare_and_fusion
  15.8 0.1 broadcast_in_dim.52
  15.9 0.7 fusion.34
  16.6 0.7 compare_and_fusion.1
  17.3 45.2 %collective-permute-done = bf16[1,1,1,1,384,2,768]{6,5,4,3,2,1,0:T(2,128)(2,1)S(1)} collective-permute-done((bf16[1,1,1,1,384,2,768]{6,5,4,3,2,1,0:T(2,128)(2,1)}, bf16[1,1,1,1,384,2,768]{6,5,4,3,2,1,0:T(2,128)(2,1)S(1)}, u32[]{:S(2)}, u32[]{:S(2)}) %collective-permute-start) | collective-permute-done | bytes 1179680 | tf_op jit(solution)/shard_map/ppermute | solution.py:15
  62.5 7.6 %collective-permute-done.1 = bf16[1,1,1,1,384,2,768]{6,5,4,3,2,1,0:T(2,128)(2,1)S(1)} collective-permute-done((bf16[1,1,1,1,384,2,768]{6,5,4,3,2,1,0:T(2,128)(2,1)}, bf16[1,1,1,1,384,2,768]{6,5,4,3,2,1,0:T(2,128)(2,1)S(1)}, u32[]{:S(2)}, u32[]{:S(2)}) %collective-permute-start.1) | collective-permute-done | bytes 1179680 | tf_op jit(solution)/shard_map/ppermute | solution.py:18
  70.1 8.5 %maximum_bitcast_fusion = bf16[3,384,2,768]{3,2,1,0:T(2,128)(2,1)} fusion(bf16[1,1,1,1,384,2,768]{6,5,4,3,2,1,0:T(2,128)(2,1)S(1)} %collective-permute-done.1, bf16[1,1,1,1,384,2,768]{6,5,4,3,2,1,0:T(2,128)(2,1)} %param.6, bf16[1,1,1,1,384,2,768]{6,5,4,3,2,1,0:T(2,128)(2,1)S(1)} %collective-permute-done), kind=kLoop, calls=%fused_computation.16 | loop fusion | flops 3538944 | bytes 7077888 | tf_op jit(solution)/shard_map/reshape;squeeze | solution.py:33
  78.6 10.0 %gather_fusion = bf16[3,384,2,768]{3,2,1,0:T(2,128)(2,1)S(1)} fusion(bf16[3,384,2,768]{3,2,1,0:T(2,128)(2,1)} %maximum_bitcast_fusion, s32[1024]{0:T(1024)S(1)} %pad_clamp_fusion), kind=kCustom, calls=%fused_computation | custom fusion | bytes 7077900 | tf_op jit(solution)/shard_map/while/body/eval_jaxpr/jit(_take)/gather | solution.py:58
  88.6 3.1 %broadcast_select_fusion = bf16[3,384,2,768]{3,2,1,0:T(2,128)(2,1)S(1)} fusion(bf16[3,384,2,768]{3,2,1,0:T(2,128)(2,1)S(1)} %gather_fusion, pred[3]{0:T(512)(128)(4,1)S(1)} %compare_and_fusion.1), kind=kLoop, calls=%fused_computation.9 | loop fusion | flops 1769472 | bytes 7077891 | tf_op jit(solution)/shard_map/while/body/eval_jaxpr/jit(_take)/select_n | solution.py:58
  91.7 22.2 %slice_reduce_fusion.1 = (bf16[3,384,768]{2,1,0:T(8,128)(2,1)}, bf16[3,384,768]{2,1,0:T(8,128)(2,1)}) fusion(bf16[3,384,2,768]{3,2,1,0:T(2,128)(2,1)S(1)} %broadcast_select_fusion), kind=kLoop, calls=%fused_computation.15 | loop fusion | bytes 7077888 | tf_op jit(solution)/shard_map/while/body/eval_jaxpr/slice | solution.py:60
  113.9 3.6 %squeeze.21 = bf16[1152,6,128]{2,1,0:T(8,128)(2,1)S(1)} reshape(bf16[3,384,768]{2,1,0:T(8,128)(2,1)} %get-tuple-element.16) | data formatting | bytes 3538944 | tf_op jit(solution)/shard_map/while/body/eval_jaxpr/reshape;while/body/eval_jaxpr/squeeze | solution.py:59
  117.5 4.9 %squeeze.20 = bf16[1152,6,128]{2,1,0:T(8,128)(2,1)} reshape(bf16[3,384,768]{2,1,0:T(8,128)(2,1)} %get-tuple-element.15) | data formatting | bytes 3538944 | tf_op jit(solution)/shard_map/while/body/eval_jaxpr/reshape;while/body/eval_jaxpr/squeeze | solution.py:60
  122.4 2.6 %fusion.12 = f32[6,1152,384]{2,1,0:T(8,128)S(1)} fusion(bf16[384,6,128]{0,2,1:T(8,128)(2,1)} %bitcast.91, bf16[1152,6,128]{2,1,0:T(8,128)(2,1)S(1)} %squeeze.21), kind=kOutput, calls=%fused_computation.18 | convolution fusion | flops 679477248 | bytes 12976128 | tf_op jit(solution)/shard_map/while/body/eval_jaxpr/qnd,knd->nqk/dot_general | solution.py:62
  125.0 0.0 copy-start
  125.0 7.3 %bitcast_reduce_fusion = (f32[6,384]{1,0:T(8,128)S(1)}, f32[6,1152,384]{2,1,0:T(8,128)}) fusion(f32[6,1152,384]{2,1,0:T(8,128)S(1)} %fusion.12, pred[1152]{0:T(1024)(128)(4,1)S(1)} %broadcast_in_dim.53), kind=kOutput, calls=%fused_computation.3 | output fusion | flops 15926399 | bytes 21244032 | tf_op jit(solution)/shard_map/while/body/eval_jaxpr/sub | solution.py:66
  132.3 0.0 copy-done
  132.3 5.5 %fusion.14 = bf16[6,128,384]{2,1,0:T(8,128)(2,1)S(1)} fusion(f32[6,1152,384]{2,1,0:T(8,128)} %get-tuple-element.29, f32[6,384]{1,0:T(8,128)S(1)} %get-tuple-element.28, bf16[1152,6,128]{2,1,0:T(8,128)(2,1)S(1)} %copy-done), kind=kOutput, calls=%fused_computation.20 | convolution fusion | flops 685080576 | bytes 12985344 | tf_op jit(solution)/shard_map/while/body/eval_jaxpr/nqk,knd->qnd/dot_general | solution.py:69
  137.8 8.6 %all-gather.2.cloned.1.call-done = bf16[768,1536]{1,0:T(8,128)(2,1)} async-done(((bf16[32,1536]{1,0:T(8,128)(2,1)}), bf16[768,1536]{1,0:T(8,128)(2,1)}) %all-gather.2.cloned.1.call-update) | async-done | bytes 2359312 | tf_op jit(solution)/shard_map/all_gather | solution.py:80
  146.4 0.0 copy-start.1
  146.4 4.2 %fusion.39 = f32[384,1536]{1,0:T(8,128)} fusion(bf16[384,768]{0,1:T(8,128)(2,1)S(1)} %bitcast.92, bf16[768,1536]{1,0:T(8,128)(2,1)} %all-gather.2.cloned.1.call-done), kind=kOutput, calls=%fused_computation.57 | convolution fusion | flops 905969664 | bytes 5308416 | tf_op jit(solution)/shard_map/dot_general | solution.py:82
  150.6 0.0 reduce-scatter.2.cloned.1.call-update
  150.6 0.0 copy-done.1
  150.7 37.6 %reduce-scatter.2.cloned.1.call-done = f32[192,1536]{1,0:T(8,128)} async-done(((f32[384,1536]{1,0:T(8,128)}), f32[192,1536]{1,0:T(8,128)}) %reduce-scatter.2.cloned.1.call-update) | async-done | bytes 1179664 | tf_op jit(solution)/shard_map/reduce_scatter | solution.py:81
  188.3 2.2 %fusion.19 = bf16[1,1,1,1,192,1536]{5,4,3,2,1,0:T(8,128)(2,1)} fusion(f32[192,1536]{1,0:T(8,128)} %reduce-scatter.2.cloned.1.call-done, f32[1536]{0:T(1024)S(1)} %reduce.1), kind=kLoop, calls=%fused_computation.22 | loop fusion | flops 589824 | bytes 1775616 | tf_op jit(solution)/shard_map/reshape | solution.py:88
  (3 shorter events, 0.1 us)
Async XLA Ops:
  6.5 139.9 %all-gather.2.cloned.1.call-start = ((), (), s32[]{:S(2)}) async-start(), calls=%async_computation.1 | async-start | bytes 2457600 | tf_op jit(solution)/shard_map/all_gather | solution.py:80
  6.5 56.0 %collective-permute-start = (bf16[1,1,1,1,384,2,768]{6,5,4,3,2,1,0:T(2,128)(2,1)}, bf16[1,1,1,1,384,2,768]{6,5,4,3,2,1,0:T(2,128)(2,1)S(1)}, u32[]{:S(2)}, u32[]{:S(2)}) collective-permute-start(bf16[1,1,1,1,384,2,768]{6,5,4,3,2,1,0:T(2,128)(2,1)} %param.6), channel_id=1, source_target_pairs={{0,2},{2,4},{4,6},{6,8},{8,10},{10,12},{12,14},{14,16},{16,18},{18... | collective-permute-start | bytes 3538952 | tf_op jit(solution)/shard_map/ppermute | solution.py:15
  11.7 58.4 %collective-permute-start.1 = (bf16[1,1,1,1,384,2,768]{6,5,4,3,2,1,0:T(2,128)(2,1)}, bf16[1,1,1,1,384,2,768]{6,5,4,3,2,1,0:T(2,128)(2,1)S(1)}, u32[]{:S(2)}, u32[]{:S(2)}) collective-permute-start(bf16[1,1,1,1,384,2,768]{6,5,4,3,2,1,0:T(2,128)(2,1)} %param.6), channel_id=1, source_target_pairs={{2,0},{4,2},{6,4},{8,6},{10,8},{12,10},{14,12},{16,14},{18,16},{20... | collective-permute-start | bytes 3538952 | tf_op jit(solution)/shard_map/ppermute | solution.py:18
  13.0 175.3 %reduce-scatter.2.cloned.1.call-start = ((), (), s32[]{:S(2)}) async-start(), calls=%async_computation.2 | async-start | bytes 3538944 | tf_op jit(solution)/shard_map/reduce_scatter | solution.py:81
  125.0 7.3 %copy-start = (bf16[1152,6,128]{2,1,0:T(8,128)(2,1)S(1)}, bf16[1152,6,128]{2,1,0:T(8,128)(2,1)}, u32[]{:S(2)}) copy-start(bf16[1152,6,128]{2,1,0:T(8,128)(2,1)} %squeeze.20) | copy-start | bytes 5308420
  146.4 4.2 %copy-start.1 = (f32[1,1536]{1,0:T(1,128)S(1)}, f32[1,1536]{1,0:T(1,128)}, u32[]{:S(2)}) copy-start(f32[1,1536]{1,0:T(1,128)} %param.9) | copy-start | bytes 18436
Sparse Core Ops, SparseCore 0:
  13.1 133.2 all-gather.1
  150.7 37.4 reduce-scatter.1
where the time goes:
time: 198 us; the launch traced here: 197 us
  waiting for transfers between devices  99 us (50%)
  local copies, waits for them, and re-layouts  42.9 us (22%)
  other arithmetic  23.1 us (12%)
  between operations  13.5 us (7%)
  matrix products  12.3 us (6%)
  starting transfers between devices  6.44 us (3%)
    ppermute x1, waiting for transfers between devices, with_halo(): lax.ppermute(lax.slice_in_dim(block, block.shape[dim] - width, None, axis...  45.2 us
    reduce_scatter x1, waiting for transfers between devices, local(): lax.psum_scatter(jnp.dot(reordered, head_rows, preferred_element_type=jnp...  37.6 us
    slice x1, local copies, waits for them, and re-layouts, per_tile(): values = key_tiles[:, :, 1, :].reshape(keep * tl, local_heads, HD)  22.2 us
    gather x1, local copies, waits for them, and re-layouts, per_tile(): key_tiles = jnp.take(ext_flat, index_row, axis=0)  9.99 us
    all_gather x1, waiting for transfers between devices, local(): head_rows = lax.all_gather(out_weight, 'dp', axis=0, tiled=True)  8.58 us
    another operation x1, other arithmetic, local(): ext_flat = extended[0].reshape(3 * tiles, tl, 2, local_width)  8.47 us
    ppermute x1, waiting for transfers between devices, with_halo(): lax.ppermute(lax.slice_in_dim(block, 0, width, axis=dim), axis, backward)  7.56 us
    sub x1, other arithmetic, per_tile(): prob = jnp.where(mask, jnp.exp(scores - top), 0.0)  7.27 us
  transfers between devices with their start and end apart: 4, of which 4 were waited for; matrix products, arithmetic and copies ran while one was open for 36% of the time, Pallas kernels for 0%

commit v1 on v0

v1 whole, which is shorter than its diff:
```python
import functools

import jax
import jax.numpy as jnp
from jax import lax
from jax.experimental import pallas as pl
from jax.experimental.pallas import tpu as pltpu
from jax.sharding import Mesh
from jax.sharding import PartitionSpec as P

HD = 128
DOUT = 1536

DP = ("z", "ylo")
TM = ("x", "yhi")
ROWS = "core"


def attend_kernel(flags_ref, q_ref, kvp_ref, kvc_ref, kvn_ref, o_ref):
    scale = float(HD) ** (-0.5)
    q = q_ref[...]
    tiles = (kvp_ref, kvc_ref, kvn_ref)
    scores = []
    for j, kv_ref in enumerate(tiles):
        k = kv_ref[:, 0, :]
        s = lax.dot_general(
            q, k, (((1,), (1,)), ((), ())), preferred_element_type=jnp.float32
        ) * scale
        scores.append(jnp.where(flags_ref[j] > 0, s, -jnp.inf))
    top = jnp.max(scores[0], axis=1, keepdims=True)
    for s in scores[1:]:
        top = jnp.maximum(top, jnp.max(s, axis=1, keepdims=True))
    probs = [jnp.exp(s - top) for s in scores]
    total = probs[0].sum(axis=1, keepdims=True)
    for p in probs[1:]:
        total = total + p.sum(axis=1, keepdims=True)
    inv = 1.0 / total
    acc = None
    for p, kv_ref in zip(probs, tiles):
        w = (p * inv).astype(jnp.bfloat16)
        part = jnp.dot(w, kv_ref[:, 1, :], preferred_element_type=jnp.float32)
        acc = part if acc is None else acc + part
    o_ref[...] = acc.astype(o_ref.dtype)


def attend(flags, q, kv_prev, kv_own, kv_next):
    tl, width = q.shape
    heads = width // HD
    kv_spec = pl.BlockSpec((tl, 2, HD), lambda h, f: (0, 0, h))
    grid_spec = pltpu.PrefetchScalarGridSpec(
        num_scalar_prefetch=1,
        grid=(heads,),
        in_specs=[pl.BlockSpec((tl, HD), lambda h, f: (0, h)), kv_spec, kv_spec, kv_spec],
        out_specs=pl.BlockSpec((tl, HD), lambda h, f: (0, h)),
    )
    flops = heads * 2 * 2 * tl * 3 * tl * HD
    return pl.pallas_call(
        attend_kernel,
        grid_spec=grid_spec,
        out_shape=jax.ShapeDtypeStruct((tl, width), jnp.bfloat16),
        cost_estimate=pl.CostEstimate(
            flops=flops,
            transcendentals=heads * tl * 3 * tl,
            bytes_accessed=2 * (tl * width * 2 + 3 * tl * 2 * width),
        ),
    )(flags, q, kv_prev, kv_own, kv_next)


def local(queries, keys_values, window_offsets, out_weight, gate):
    tl = queries.shape[4]
    all_time = lax.axis_size(TM)
    time_now = lax.axis_index(TM)

    forward = [(i, i + 1) for i in range(all_time - 1)]
    backward = [(i + 1, i) for i in range(all_time - 1)]
    kv = keys_values[0, 0, 0, 0]
    kv_prev = lax.ppermute(kv, TM, forward)
    kv_next = lax.ppermute(kv, TM, backward)

    head_rows = lax.all_gather(out_weight, "ylo", axis=0, tiled=True)
    head_rows = lax.all_gather(head_rows, "z", axis=0, tiled=True)

    offsets = window_offsets[0, 0, 0, 0]
    near_t = time_now + offsets // 9 - 1
    same_hw = (offsets // 3 % 3 == 1) & (offsets % 3 == 1)
    inside = same_hw & (near_t >= 0) & (near_t < all_time)
    deltas = jnp.array([-1, 0, 1], jnp.int32)
    hit = inside[None, :] & (near_t[None, :] == time_now + deltas[:, None])
    flags = jnp.any(hit, axis=1).astype(jnp.int32)

    attended = attend(flags, queries[0, 0, 0, 0], kv_prev, kv, kv_next)

    bands = lax.axis_size(ROWS)
    band = tl // bands
    me = lax.axis_index(ROWS)
    other = 1 - me
    mine_rows = lax.dynamic_slice_in_dim(attended, me * band, band, axis=0)
    other_rows = lax.dynamic_slice_in_dim(attended, other * band, band, axis=0)
    sent = jnp.dot(other_rows, head_rows, preferred_element_type=jnp.float32)
    got = lax.ppermute(sent, ROWS, [(0, 1), (1, 0)])
    kept = jnp.dot(mine_rows, head_rows, preferred_element_type=jnp.float32)
    projection = kept + got
    mixed = (gate[0][None, :] * projection).astype(jnp.bfloat16)
    return mixed.reshape(1, 1, 1, 1, band, DOUT)


def solution(mesh):
    devices = mesh.devices.reshape(12, 2, 4, 4, 2)
    fine = Mesh(devices, ("z", "ylo", "x", "yhi", "core"))
    placed = (
        P(DP, TM, None, None, None, ROWS),
        P(DP, TM, None, None, None, None, ROWS),
        P(DP, TM, None, None, None),
        P((ROWS,) + DP, None),
        P(DP, None),
    )
    return jax.shard_map(
        local,
        mesh=fine,
        in_specs=placed,
        out_specs=P(DP, TM, None, None, ROWS, None),
        check_vma=False,
    )
```

time: 198 us -> 110 us (0.56)
  waiting for transfers between devices: 99 us -> 53.8 us
  local copies, waits for them, and re-layouts: 42.9 us -> 1.03 us
  other arithmetic: 23.1 us -> 2.07 us
  Pallas kernels: 0 us -> 17 us
  matrix products: 12.3 us -> 5.35 us
  blocking collectives: 0 us -> 6.62 us
  starting transfers between devices: 6.44 us -> 10.3 us
    reduce_scatter x1 -> x0, waiting for transfers between devices: 37.6 us -> none  [local(): lax.psum_scatter(jnp.dot(reordered, head_rows, preferred_element_type=jnp...]
    slice x1 -> x0, local copies, waits for them, and re-layouts: 22.2 us -> none  [per_tile(): values = key_tiles[:, :, 1, :].reshape(keep * tl, local_heads, HD)]
    pallas_call x0 -> x1, Pallas kernels: none -> 17 us  [attend(): pl.pallas_call(attend_kernel, grid_spec=grid_spec, out_shape=jax.ShapeDty...]
    gather x1 -> x0, local copies, waits for them, and re-layouts: 9.99 us -> none  [per_tile(): key_tiles = jnp.take(ext_flat, index_row, axis=0)]
    all_gather x1, waiting for transfers between devices: 8.58 us -> 0.01 us  [local(): head_rows = lax.all_gather(head_rows, 'z', axis=0, tiled=True)]
    squeeze x2 -> x0, local copies, waits for them, and re-layouts: 8.55 us -> none  [the longest x1 4.93 us: per_tile(): values = key_tiles[:, :, 1, :].reshape(keep * tl, local_heads, HD)]
    another operation x1 -> x0, other arithmetic: 8.47 us -> none  [local(): ext_flat = extended[0].reshape(3 * tiles, tl, 2, local_width)]
    sub x1 -> x0, other arithmetic: 7.27 us -> none  [per_tile(): prob = jnp.where(mask, jnp.exp(scores - top), 0.0)]
  transfers between devices with their start and end apart: 4 -> 4, of which waited for: 4 -> 3; matrix products, arithmetic and copies ran while one was open for 36% -> 2% of each run, Pallas kernels for 0% -> 15%
where the time goes in v1:
time: 110 us
  waiting for transfers between devices  53.8 us (49%)
  Pallas kernels  17 us (15%)
  between operations  13.5 us (12%)
  starting transfers between devices  10.3 us (9%)
  blocking collectives  6.62 us (6%)
  matrix products  5.35 us (5%)
  other arithmetic  2.07 us (2%)
    ppermute x1, waiting for transfers between devices, local(): kv_prev = lax.ppermute(kv, TM, forward)  39.5 us
    pallas_call x1, Pallas kernels, attend(): pl.pallas_call(attend_kernel, grid_spec=grid_spec, out_shape=jax.ShapeDty...  17 us
    ppermute x1, waiting for transfers between devices, local(): kv_next = lax.ppermute(kv, TM, backward)  11.8 us
    all_gather x1, blocking collectives, local(): head_rows = lax.all_gather(out_weight, 'ylo', axis=0, tiled=True)  6.62 us
    ppermute x1, starting transfers between devices, local(): kv_prev = lax.ppermute(kv, TM, forward)  4.8 us
    ppermute x1, starting transfers between devices, local(): got = lax.ppermute(sent, ROWS, [(0, 1), (1, 0)])  4.18 us
    dot_general x1, matrix products, local(): kept = jnp.dot(mine_rows, head_rows, preferred_element_type=jnp.float32)  2.82 us
    ppermute x1, waiting for transfers between devices, local(): got = lax.ppermute(sent, ROWS, [(0, 1), (1, 0)])  2.54 us
  transfers between devices with their start and end apart: 4, of which 3 were waited for; matrix products, arithmetic and copies ran while one was open for 2% of the time, Pallas kernels for 15%

profile of v1, /device:TPU:1, one launch (start us, length us, event | category | flops | bytes accessed | tf_op | source)
XLA Modules:
  0.0 109.6 jit_solution(6785980322841509706)
XLA Ops:
  6.5 0.0 all-gather.2.cloned.1.call-start
  6.5 6.6 %all_gather.6 = bf16[64,1536]{1,0:T(8,128)(2,1)} all-gather(bf16[32,1536]{1,0:T(8,128)(2,1)} %param.9), channel_id=1, replica_groups=mesh['z'=12,'ylo'=2,'x'=4,'yhi'=4,'core'=2] {'ylo'}, dimensions={0}, use_global_device_ids=true | all-gather | bytes 294912 | tf_op jit(solution)/shard_map/all_gather | solution.py:80
  13.2 0.0 all-gather.2.cloned.1.call-update
  13.2 4.8 %collective-permute-start = (bf16[384,2,768]{2,1,0:T(2,128)(2,1)}, bf16[384,2,768]{2,1,0:T(2,128)(2,1)S(1)}, u32[]{:S(2)}, u32[]{:S(2)}) collective-permute-start(bf16[384,2,768]{2,1,0:T(2,128)(2,1)} %bitcast.37), channel_id=1, source_target_pairs={{0,2},{2,4},{4,6},{6,8},{8,10},{10,12},{12,14},{14,16},{16,18},{18... | collective-permute-start | bytes 3538952 | tf_op jit(solution)/shard_map/ppermute | solution.py:77
  18.0 1.3 %collective-permute-start.1 = (bf16[384,2,768]{2,1,0:T(2,128)(2,1)}, bf16[384,2,768]{2,1,0:T(2,128)(2,1)S(1)}, u32[]{:S(2)}, u32[]{:S(2)}) collective-permute-start(bf16[384,2,768]{2,1,0:T(2,128)(2,1)} %bitcast.38), channel_id=1, source_target_pairs={{2,0},{4,2},{6,4},{8,6},{10,8},{12,10},{14,12},{16,14},{18,16},{20... | collective-permute-start | bytes 3538952 | tf_op jit(solution)/shard_map/ppermute | solution.py:78
  19.3 0.7 broadcast_add_fusion
  20.0 0.7 compare_and_fusion
  20.7 0.2 and_reduce_fusion
  20.8 0.5 convert_element_type.6.flags_ref
  21.4 39.5 %collective-permute-done.kvp_ref = bf16[384,2,768]{2,1,0:T(2,128)(2,1)S(1)} collective-permute-done((bf16[384,2,768]{2,1,0:T(2,128)(2,1)}, bf16[384,2,768]{2,1,0:T(2,128)(2,1)S(1)}, u32[]{:S(2)}, u32[]{:S(2)}) %collective-permute-start) | collective-permute-done | bytes 1179680 | tf_op jit(solution)/shard_map/ppermute | solution.py:77
  60.8 0.0 copy-start.2
  60.8 11.8 %collective-permute-done.1.kvn_ref = bf16[384,2,768]{2,1,0:T(2,128)(2,1)S(1)} collective-permute-done((bf16[384,2,768]{2,1,0:T(2,128)(2,1)}, bf16[384,2,768]{2,1,0:T(2,128)(2,1)S(1)}, u32[]{:S(2)}, u32[]{:S(2)}) %collective-permute-start.1) | collective-permute-done | bytes 1179680 | tf_op jit(solution)/shard_map/ppermute | solution.py:78
  72.6 0.0 copy-start.3
  72.6 0.0 copy-done.2
  72.6 1.0 copy-done.3
  73.6 17.0 %shard_map.64 = bf16[384,768]{1,0:T(8,128)(2,1)} custom-call(s32[3]{0:T(128)} %convert_element_type.6.flags_ref, bf16[384,768]{1,0:T(8,128)(2,1)} %bitcast.40, bf16[384,2,768]{2,1,0:T(2,128)(2,1)} %copy-done.2, bf16[384,2,768]{2,1,0:T(2,128)(2,1)} %bitcast.39, bf16[384,2,768]{2,1,0:T(2,128)(2,1)} %copy-done.3), custom_call_target="tpu_custom_call" | custom-call | flops 1358954496 | bytes 4718592 | tf_op jit(solution)/shard_map/pallas_call | solution.py:57
  90.6 0.0 copy-start.1
  90.6 0.0 all-gather.2.cloned.1.call-done
  90.6 0.0 copy-start
  90.6 2.5 %fusion.3 = f32[192,1536]{1,0:T(8,128)S(1)} fusion(bf16[768,1536]{1,0:T(8,128)(2,1)} %all-gather.2.cloned.1.call-done, bf16[384,768]{1,0:T(8,128)(2,1)} %shard_map.64, s32[]{:T(128)S(6)} %select_n.49), kind=kOutput, calls=%fused_computation.4 | convolution fusion | flops 452984832 | bytes 3833860 | tf_op jit(solution)/shard_map/dot_general | solution.py:99
  93.2 4.2 %collective-permute-start.2 = (f32[192,1536]{1,0:T(8,128)S(1)}, f32[192,1536]{1,0:T(8,128)}, u32[]{:S(2)}, u32[]{:S(2)}) collective-permute-start(f32[192,1536]{1,0:T(8,128)S(1)} %fusion.3), channel_id=1, source_target_pairs={{0,1},{1,0},{2,3},{3,2},{4,5},{5,4},{6,7},{7,6},{8,9},{9,8},{10,11... | collective-permute-start | bytes 3538952 | tf_op jit(solution)/shard_map/ppermute | solution.py:100
  97.4 0.0 copy-done.1
  97.4 2.5 %collective-permute-done.2 = f32[192,1536]{1,0:T(8,128)} collective-permute-done((f32[192,1536]{1,0:T(8,128)S(1)}, f32[192,1536]{1,0:T(8,128)}, u32[]{:S(2)}, u32[]{:S(2)}) %collective-permute-start.2) | collective-permute-done | bytes 1179680 | tf_op jit(solution)/shard_map/ppermute | solution.py:100
  100.0 0.0 copy-done
  100.0 2.8 %fusion.2 = bf16[1,1,1,1,192,1536]{5,4,3,2,1,0:T(8,128)(2,1)} fusion(f32[192,1536]{1,0:T(8,128)} %collective-permute-done.2, bf16[768,1536]{1,0:T(8,128)(2,1)S(1)} %copy-done, f32[1536]{0:T(1024)S(1)} %reduce, bf16[384,768]{1,0:T(8,128)(2,1)} %shard_map.64, s32[]{:T(128)S(6)} %select_n.48), kind=kOutput, calls=%fused_computation.3 | convolution fusion | flops 453869568 | bytes 4429828 | tf_op jit(solution)/shard_map/dot_general | solution.py:101
  (1 shorter events, 0.0 us)
Async XLA Ops:
  6.5 84.1 %all-gather.2.cloned.1.call-start = ((), (), s32[]{:S(2)}) async-start(), calls=%async_computation | async-start | bytes 2555904 | tf_op jit(solution)/shard_map/all_gather | solution.py:81
  13.2 47.6 %collective-permute-start = (bf16[384,2,768]{2,1,0:T(2,128)(2,1)}, bf16[384,2,768]{2,1,0:T(2,128)(2,1)S(1)}, u32[]{:S(2)}, u32[]{:S(2)}) collective-permute-start(bf16[384,2,768]{2,1,0:T(2,128)(2,1)} %bitcast.37), channel_id=1, source_target_pairs={{0,2},{2,4},{4,6},{6,8},{8,10},{10,12},{12,14},{14,16},{16,18},{18... | collective-permute-start | bytes 3538952 | tf_op jit(solution)/shard_map/ppermute | solution.py:77
  18.0 54.6 %collective-permute-start.1 = (bf16[384,2,768]{2,1,0:T(2,128)(2,1)}, bf16[384,2,768]{2,1,0:T(2,128)(2,1)S(1)}, u32[]{:S(2)}, u32[]{:S(2)}) collective-permute-start(bf16[384,2,768]{2,1,0:T(2,128)(2,1)} %bitcast.38), channel_id=1, source_target_pairs={{2,0},{4,2},{6,4},{8,6},{10,8},{12,10},{14,12},{16,14},{18,16},{20... | collective-permute-start | bytes 3538952 | tf_op jit(solution)/shard_map/ppermute | solution.py:78
  60.8 11.8 %copy-start.2 = (bf16[384,2,768]{2,1,0:T(2,128)(2,1)}, bf16[384,2,768]{2,1,0:T(2,128)(2,1)S(1)}, u32[]{:S(2)}) copy-start(bf16[384,2,768]{2,1,0:T(2,128)(2,1)S(1)} %collective-permute-done.kvp_ref) | copy-start | bytes 3538948
  72.6 1.0 copy-start.3
  90.6 6.7 %copy-start.1 = (f32[1,1536]{1,0:T(1,128)S(1)}, f32[1,1536]{1,0:T(1,128)}, u32[]{:S(2)}) copy-start(f32[1,1536]{1,0:T(1,128)} %param.10) | copy-start | bytes 18436
  90.6 9.3 %copy-start = (bf16[768,1536]{1,0:T(8,128)(2,1)S(1)}, bf16[768,1536]{1,0:T(8,128)(2,1)}, u32[]{:S(2)}) copy-start(bf16[768,1536]{1,0:T(8,128)(2,1)} %all-gather.2.cloned.1.call-done) | copy-start | bytes 7077892
  93.2 6.8 %collective-permute-start.2 = (f32[192,1536]{1,0:T(8,128)S(1)}, f32[192,1536]{1,0:T(8,128)}, u32[]{:S(2)}, u32[]{:S(2)}) collective-permute-start(f32[192,1536]{1,0:T(8,128)S(1)} %fusion.3), channel_id=1, source_target_pairs={{0,1},{1,0},{2,3},{3,2},{4,5},{5,4},{6,7},{7,6},{8,9},{9,8},{10,11... | collective-permute-start | bytes 3538952 | tf_op jit(solution)/shard_map/ppermute | solution.py:100
Sparse Core Ops, SparseCore 0:
  13.3 63.0 all-gather.1

commit v2 on v1

--- a/solution.py
+++ b/solution.py
@@ -66,6 +66,27 @@
     )(flags, q, kv_prev, kv_own, kv_next)
 
 
+def gather_ring(piece, axis):
+    count = lax.axis_size(axis)
+    here = lax.axis_index(axis)
+    rows = piece.shape[0]
+    whole = jnp.zeros((count * rows,) + piece.shape[1:], piece.dtype)
+    whole = lax.dynamic_update_slice_in_dim(whole, piece, here * rows, axis=0)
+    right = [(i, (i + 1) % count) for i in range(count)]
+    left = [(i, (i - 1) % count) for i in range(count)]
+    fwd = piece
+    bwd = piece
+    for step in range(1, count // 2 + 1):
+        fwd = lax.ppermute(fwd, axis, right)
+        at = (here - step + count) % count
+        whole = lax.dynamic_update_slice_in_dim(whole, fwd, at * rows, axis=0)
+        if step < count - step:
+            bwd = lax.ppermute(bwd, axis, left)
+            at = (here + step) % count
+            whole = lax.dynamic_update_slice_in_dim(whole, bwd, at * rows, axis=0)
+    return whole
+
+
 def local(queries, keys_values, window_offsets, out_weight, gate):
     tl = queries.shape[4]
     all_time = lax.axis_size(TM)
@@ -77,8 +98,12 @@
     kv_prev = lax.ppermute(kv, TM, forward)
     kv_next = lax.ppermute(kv, TM, backward)
 
-    head_rows = lax.all_gather(out_weight, "ylo", axis=0, tiled=True)
-    head_rows = lax.all_gather(head_rows, "z", axis=0, tiled=True)
+    pair = lax.ppermute(out_weight, "ylo", [(0, 1), (1, 0)])
+    low = lax.axis_index("ylo") == 0
+    head_rows = jnp.concatenate(
+        [jnp.where(low, out_weight, pair), jnp.where(low, pair, out_weight)], axis=0
+    )
+    head_rows = gather_ring(head_rows, "z")
 
     offsets = window_offsets[0, 0, 0, 0]
     near_t = time_now + offsets // 9 - 1
@@ -99,6 +124,7 @@
     sent = jnp.dot(other_rows, head_rows, preferred_element_type=jnp.float32)
     got = lax.ppermute(sent, ROWS, [(0, 1), (1, 0)])
     kept = jnp.dot(mine_rows, head_rows, preferred_element_type=jnp.float32)
+    kept = lax.optimization_barrier(kept)
     projection = kept + got
     mixed = (gate[0][None, :] * projection).astype(jnp.bfloat16)
     return mixed.reshape(1, 1, 1, 1, band, DOUT)

time: 110 us -> 150 us (1.36)
  the two profiles are of different devices: /device:TPU:1 before, /device:TPU:17 now
where the time goes in v2:
time: 150 us
  starting transfers between devices  67.5 us (45%)
  waiting for transfers between devices  56.2 us (37%)
  Pallas kernels  16.9 us (11%)
  other arithmetic  4.73 us (3%)
  matrix products  3.18 us (2%)
    ppermute x1, waiting for transfers between devices, local(): pair = lax.ppermute(out_weight, 'ylo', [(0, 1), (1, 0)])  46.8 us
    ppermute x5, starting transfers between devices, gather_ring(): bwd = lax.ppermute(bwd, axis, left)  31 us
    pallas_call x1, Pallas kernels, attend(): pl.pallas_call(attend_kernel, grid_spec=grid_spec, out_shape=jax.ShapeDty...  16.9 us
    ppermute x6, starting transfers between devices, gather_ring(): fwd = lax.ppermute(fwd, axis, right)  13.6 us
    ppermute x1, starting transfers between devices, local(): got = lax.ppermute(sent, ROWS, [(0, 1), (1, 0)])  12.3 us
    ppermute x6, waiting for transfers between devices, gather_ring(): fwd = lax.ppermute(fwd, axis, right)  8.47 us
    ppermute x1, starting transfers between devices, local(): kv_prev = lax.ppermute(kv, TM, forward)  5.55 us
    ppermute x1, starting transfers between devices, local(): pair = lax.ppermute(out_weight, 'ylo', [(0, 1), (1, 0)])  3.06 us
  transfers between devices with their start and end apart: 15, of which 7 were waited for; matrix products, arithmetic and copies ran while one was open for 3% of the time, Pallas kernels for 11%

profile of v2, /device:TPU:17, one launch (start us, length us, event | category | flops | bytes accessed | tf_op | source)
XLA Modules:
  0.0 149.6 jit_solution(15440083043480599587)
XLA Ops:
  0.0 0.0 copy-start.1
  0.0 5.6 %collective-permute-start = (bf16[384,2,768]{2,1,0:T(2,128)(2,1)}, bf16[384,2,768]{2,1,0:T(2,128)(2,1)}, u32[]{:S(2)}, u32[]{:S(2)}) collective-permute-start(bf16[384,2,768]{2,1,0:T(2,128)(2,1)} %bitcast.37), channel_id=1, source_target_pairs={{0,2},{2,4},{4,6},{6,8},{8,10},{10,12},{12,14},{14,16},{16,18},{18... | collective-permute-start | bytes 3538952 | tf_op jit(solution)/shard_map/ppermute | solution.py:98
  5.6 1.9 %collective-permute-start.1 = (bf16[384,2,768]{2,1,0:T(2,128)(2,1)}, bf16[384,2,768]{2,1,0:T(2,128)(2,1)}, u32[]{:S(2)}, u32[]{:S(2)}) collective-permute-start(bf16[384,2,768]{2,1,0:T(2,128)(2,1)} %bitcast.38), channel_id=1, source_target_pairs={{2,0},{4,2},{6,4},{8,6},{10,8},{12,10},{14,12},{16,14},{18,16},{20... | collective-permute-start | bytes 3538952 | tf_op jit(solution)/shard_map/ppermute | solution.py:99
  7.5 3.1 %collective-permute-start.2 = (bf16[32,1536]{1,0:T(8,128)(2,1)}, bf16[32,1536]{1,0:T(8,128)(2,1)S(1)}, u32[]{:S(2)}, u32[]{:S(2)}) collective-permute-start(bf16[32,1536]{1,0:T(8,128)(2,1)} %param.9), channel_id=1, source_target_pairs={{0,32},{32,0},{1,33},{33,1},{2,34},{34,2},{3,35},{35,3},{4,36},{36... | collective-permute-start | bytes 294920 | tf_op jit(solution)/shard_map/ppermute | solution.py:101
  10.6 0.7 compare_and_fusion
  11.3 46.8 %collective-permute-done.2 = bf16[32,1536]{1,0:T(8,128)(2,1)S(1)} collective-permute-done((bf16[32,1536]{1,0:T(8,128)(2,1)}, bf16[32,1536]{1,0:T(8,128)(2,1)S(1)}, u32[]{:S(2)}, u32[]{:S(2)}) %collective-permute-start.2) | collective-permute-done | bytes 98336 | tf_op jit(solution)/shard_map/ppermute | solution.py:101
  58.0 0.9 broadcast_select_fusion.1
  59.0 0.2 broadcast_in_dim.2
  59.2 4.1 %collective-permute-start.3 = (bf16[64,1536]{1,0:T(8,128)(2,1)S(1)}, bf16[64,1536]{1,0:T(8,128)(2,1)S(1)}, u32[]{:S(2)}, u32[]{:S(2)}) collective-permute-start(bf16[64,1536]{1,0:T(8,128)(2,1)S(1)} %get-tuple-element.7), channel_id=1, source_target_pairs={{0,64},{64,128},{128,192},{192,256},{256,320},{320,384},{384,448},... | collective-permute-start | bytes 589832 | tf_op jit(solution)/shard_map/ppermute | solution.py:80
  63.3 12.2 %collective-permute-start.4 = (bf16[64,1536]{1,0:T(8,128)(2,1)S(1)}, bf16[64,1536]{1,0:T(8,128)(2,1)S(1)}, u32[]{:S(2)}, u32[]{:S(2)}) collective-permute-start(bf16[64,1536]{1,0:T(8,128)(2,1)S(1)} %get-tuple-element.7), channel_id=1, source_target_pairs={{0,704},{64,0},{128,64},{192,128},{256,192},{320,256},{384,320},{4... | collective-permute-start | bytes 589832 | tf_op jit(solution)/shard_map/ppermute | solution.py:84
  75.5 0.0 copy-done.1
  75.7 0.2 and_reduce_fusion
  75.9 0.6 convert_element_type.6.flags_ref
  76.5 0.1 collective-permute-done.3
  76.6 1.9 %collective-permute-start.5 = (bf16[64,1536]{1,0:T(8,128)(2,1)S(1)}, bf16[64,1536]{1,0:T(8,128)(2,1)S(1)}, u32[]{:S(2)}, u32[]{:S(2)}) collective-permute-start(bf16[64,1536]{1,0:T(8,128)(2,1)S(1)} %collective-permute-done.3), channel_id=1, source_target_pairs={{0,64},{64,128},{128,192},{192,256},{256,320},{320,384},{384,448},... | collective-permute-start | bytes 589832 | tf_op jit(solution)/shard_map/ppermute | solution.py:80
  78.5 0.0 collective-permute-done.4
  78.5 4.6 %collective-permute-start.6 = (bf16[64,1536]{1,0:T(8,128)(2,1)S(1)}, bf16[64,1536]{1,0:T(8,128)(2,1)S(1)}, u32[]{:S(2)}, u32[]{:S(2)}) collective-permute-start(bf16[64,1536]{1,0:T(8,128)(2,1)S(1)} %collective-permute-done.4), channel_id=1, source_target_pairs={{0,704},{64,0},{128,64},{192,128},{256,192},{320,256},{384,320},{4... | collective-permute-start | bytes 589832 | tf_op jit(solution)/shard_map/ppermute | solution.py:84
  83.2 1.0 collective-permute-done.5
  84.2 1.9 %collective-permute-start.7 = (bf16[64,1536]{1,0:T(8,128)(2,1)S(1)}, bf16[64,1536]{1,0:T(8,128)(2,1)S(1)}, u32[]{:S(2)}, u32[]{:S(2)}) collective-permute-start(bf16[64,1536]{1,0:T(8,128)(2,1)S(1)} %collective-permute-done.5), channel_id=1, source_target_pairs={{0,64},{64,128},{128,192},{192,256},{256,320},{320,384},{384,448},... | collective-permute-start | bytes 589832 | tf_op jit(solution)/shard_map/ppermute | solution.py:80
  86.1 0.0 collective-permute-done.6
  86.1 4.6 %collective-permute-start.8 = (bf16[64,1536]{1,0:T(8,128)(2,1)S(1)}, bf16[64,1536]{1,0:T(8,128)(2,1)S(1)}, u32[]{:S(2)}, u32[]{:S(2)}) collective-permute-start(bf16[64,1536]{1,0:T(8,128)(2,1)S(1)} %collective-permute-done.6), channel_id=1, source_target_pairs={{0,704},{64,0},{128,64},{192,128},{256,192},{320,256},{384,320},{4... | collective-permute-start | bytes 589832 | tf_op jit(solution)/shard_map/ppermute | solution.py:84
  90.8 1.9 %collective-permute-done.7 = bf16[64,1536]{1,0:T(8,128)(2,1)S(1)} collective-permute-done((bf16[64,1536]{1,0:T(8,128)(2,1)S(1)}, bf16[64,1536]{1,0:T(8,128)(2,1)S(1)}, u32[]{:S(2)}, u32[]{:S(2)}) %collective-permute-start.7) | collective-permute-done | bytes 196640 | tf_op jit(solution)/shard_map/ppermute | solution.py:80
  92.7 1.9 %collective-permute-start.9 = (bf16[64,1536]{1,0:T(8,128)(2,1)S(1)}, bf16[64,1536]{1,0:T(8,128)(2,1)S(1)}, u32[]{:S(2)}, u32[]{:S(2)}) collective-permute-start(bf16[64,1536]{1,0:T(8,128)(2,1)S(1)} %collective-permute-done.7), channel_id=1, source_target_pairs={{0,64},{64,128},{128,192},{192,256},{256,320},{320,384},{384,448},... | collective-permute-start | bytes 589832 | tf_op jit(solution)/shard_map/ppermute | solution.py:80
  94.6 0.0 collective-permute-done.8
  94.7 4.9 %collective-permute-start.10 = (bf16[64,1536]{1,0:T(8,128)(2,1)S(1)}, bf16[64,1536]{1,0:T(8,128)(2,1)S(1)}, u32[]{:S(2)}, u32[]{:S(2)}) collective-permute-start(bf16[64,1536]{1,0:T(8,128)(2,1)S(1)} %collective-permute-done.8), channel_id=1, source_target_pairs={{0,704},{64,0},{128,64},{192,128},{256,192},{320,256},{384,320},{4... | collective-permute-start | bytes 589832 | tf_op jit(solution)/shard_map/ppermute | solution.py:84
  99.6 3.0 %collective-permute-done.9 = bf16[64,1536]{1,0:T(8,128)(2,1)S(1)} collective-permute-done((bf16[64,1536]{1,0:T(8,128)(2,1)S(1)}, bf16[64,1536]{1,0:T(8,128)(2,1)S(1)}, u32[]{:S(2)}, u32[]{:S(2)}) %collective-permute-start.9) | collective-permute-done | bytes 196640 | tf_op jit(solution)/shard_map/ppermute | solution.py:80
  102.6 1.9 %collective-permute-start.11 = (bf16[64,1536]{1,0:T(8,128)(2,1)S(1)}, bf16[64,1536]{1,0:T(8,128)(2,1)S(1)}, u32[]{:S(2)}, u32[]{:S(2)}) collective-permute-start(bf16[64,1536]{1,0:T(8,128)(2,1)S(1)} %collective-permute-done.9), channel_id=1, source_target_pairs={{0,64},{64,128},{128,192},{192,256},{256,320},{320,384},{384,448},... | collective-permute-start | bytes 589832 | tf_op jit(solution)/shard_map/ppermute | solution.py:80
  104.5 0.0 collective-permute-done.10
  104.5 4.8 %collective-permute-start.12 = (bf16[64,1536]{1,0:T(8,128)(2,1)S(1)}, bf16[64,1536]{1,0:T(8,128)(2,1)S(1)}, u32[]{:S(2)}, u32[]{:S(2)}) collective-permute-start(bf16[64,1536]{1,0:T(8,128)(2,1)S(1)} %collective-permute-done.10), channel_id=1, source_target_pairs={{0,704},{64,0},{128,64},{192,128},{256,192},{320,256},{384,320},{4... | collective-permute-start | bytes 589832 | tf_op jit(solution)/shard_map/ppermute | solution.py:84
  109.4 2.4 %collective-permute-done.11 = bf16[64,1536]{1,0:T(8,128)(2,1)S(1)} collective-permute-done((bf16[64,1536]{1,0:T(8,128)(2,1)S(1)}, bf16[64,1536]{1,0:T(8,128)(2,1)S(1)}, u32[]{:S(2)}, u32[]{:S(2)}) %collective-permute-start.11) | collective-permute-done | bytes 196640 | tf_op jit(solution)/shard_map/ppermute | solution.py:80
  111.7 1.9 %collective-permute-start.13 = (bf16[64,1536]{1,0:T(8,128)(2,1)S(1)}, bf16[64,1536]{1,0:T(8,128)(2,1)S(1)}, u32[]{:S(2)}, u32[]{:S(2)}) collective-permute-start(bf16[64,1536]{1,0:T(8,128)(2,1)S(1)} %collective-permute-done.11), channel_id=1, source_target_pairs={{0,64},{64,128},{128,192},{192,256},{256,320},{320,384},{384,448},... | collective-permute-start | bytes 589832 | tf_op jit(solution)/shard_map/ppermute | solution.py:80
  113.7 0.0 collective-permute-done.12
  113.7 0.0 collective-permute-done.kvp_ref
  113.7 0.0 collective-permute-done.1.kvn_ref
  113.7 16.9 %shard_map.64 = bf16[384,768]{1,0:T(8,128)(2,1)} custom-call(s32[3]{0:T(128)} %convert_element_type.6.flags_ref, bf16[384,768]{1,0:T(8,128)(2,1)} %bitcast.40, bf16[384,2,768]{2,1,0:T(2,128)(2,1)} %collective-permute-done.kvp_ref, bf16[384,2,768]{2,1,0:T(2,128)(2,1)} %bitcast.39, bf16[384,2,768]{2,1,0:T(2,128)(2,1)} %collective-permute-done.1.kvn_ref), custom_call_target="tpu_custom_call" | custom-call | flops 1358954496 | bytes 4718592 | tf_op jit(solution)/shard_map/pallas_call | solution.py:57
  130.7 0.0 copy-start
  130.7 0.0 collective-permute-done.13
  130.7 1.6 %fusion.1 = f32[192,1536]{1,0:T(8,128)S(1)} fusion(bf16[768,1536]{1,0:T(8,128)(2,1)S(1)} %constant_dynamic-update-slice_fusion, bf16[384,768]{1,0:T(8,128)(2,1)} %shard_map.64, s32[]{:T(128)S(6)} %select_n.169), kind=kOutput, calls=%fused_computation.2 | convolution fusion | flops 452984832 | bytes 3833860 | tf_op jit(solution)/shard_map/dot_general | solution.py:124
  132.3 12.3 %collective-permute-start.14 = (f32[192,1536]{1,0:T(8,128)S(1)}, f32[192,1536]{1,0:T(8,128)}, u32[]{:S(2)}, u32[]{:S(2)}) collective-permute-start(f32[192,1536]{1,0:T(8,128)S(1)} %fusion.1), channel_id=1, source_target_pairs={{0,1},{1,0},{2,3},{3,2},{4,5},{5,4},{6,7},{7,6},{8,9},{9,8},{10,11... | collective-permute-start | bytes 3538952 | tf_op jit(solution)/shard_map/ppermute | solution.py:125
  144.7 0.0 copy-done
  144.7 1.6 %fusion.3 = f32[192,1536]{1,0:T(8,128)S(1)} fusion(bf16[768,1536]{1,0:T(8,128)(2,1)S(1)} %constant_dynamic-update-slice_fusion, bf16[384,768]{1,0:T(8,128)(2,1)} %shard_map.64, s32[]{:T(128)S(6)} %select_n.142), kind=kOutput, calls=%fused_computation.4 | convolution fusion | flops 452984832 | bytes 3833860 | tf_op jit(solution)/shard_map/dot_general | solution.py:126
  146.3 0.9 collective-permute-done.14
  147.3 2.3 %fusion = bf16[1,1,1,1,192,1536]{5,4,3,2,1,0:T(8,128)(2,1)} fusion(f32[192,1536]{1,0:T(8,128)S(1)} %fusion.3, f32[192,1536]{1,0:T(8,128)} %collective-permute-done.14, f32[1536]{0:T(1024)S(1)} %reduce), kind=kLoop, calls=%fused_computation.1 | loop fusion | flops 884736 | bytes 2955264 | tf_op jit(solution)/shard_map/reshape | solution.py:130
  (14 shorter events, 0.3 us)
Async XLA Ops:
  0.0 75.5 %copy-start.1 = (s32[3]{0:T(128)S(1)}, s32[3]{0:T(128)}, u32[]{:S(2)}) copy-start(s32[3]{0:T(128)} %constant.123.clone) | copy-start | bytes 40
  0.0 113.7 %collective-permute-start = (bf16[384,2,768]{2,1,0:T(2,128)(2,1)}, bf16[384,2,768]{2,1,0:T(2,128)(2,1)}, u32[]{:S(2)}, u32[]{:S(2)}) collective-permute-start(bf16[384,2,768]{2,1,0:T(2,128)(2,1)} %bitcast.37), channel_id=1, source_target_pairs={{0,2},{2,4},{4,6},{6,8},{8,10},{10,12},{12,14},{14,16},{16,18},{18... | collective-permute-start | bytes 3538952 | tf_op jit(solution)/shard_map/ppermute | solution.py:98
  5.6 108.2 %collective-permute-start.1 = (bf16[384,2,768]{2,1,0:T(2,128)(2,1)}, bf16[384,2,768]{2,1,0:T(2,128)(2,1)}, u32[]{:S(2)}, u32[]{:S(2)}) collective-permute-start(bf16[384,2,768]{2,1,0:T(2,128)(2,1)} %bitcast.38), channel_id=1, source_target_pairs={{2,0},{4,2},{6,4},{8,6},{10,8},{12,10},{14,12},{16,14},{18,16},{20... | collective-permute-start | bytes 3538952 | tf_op jit(solution)/shard_map/ppermute | solution.py:99
  7.5 50.6 %collective-permute-start.2 = (bf16[32,1536]{1,0:T(8,128)(2,1)}, bf16[32,1536]{1,0:T(8,128)(2,1)S(1)}, u32[]{:S(2)}, u32[]{:S(2)}) collective-permute-start(bf16[32,1536]{1,0:T(8,128)(2,1)} %param.9), channel_id=1, source_target_pairs={{0,32},{32,0},{1,33},{33,1},{2,34},{34,2},{3,35},{35,3},{4,36},{36... | collective-permute-start | bytes 294920 | tf_op jit(solution)/shard_map/ppermute | solution.py:101
  59.2 17.4 %collective-permute-start.3 = (bf16[64,1536]{1,0:T(8,128)(2,1)S(1)}, bf16[64,1536]{1,0:T(8,128)(2,1)S(1)}, u32[]{:S(2)}, u32[]{:S(2)}) collective-permute-start(bf16[64,1536]{1,0:T(8,128)(2,1)S(1)} %get-tuple-element.7), channel_id=1, source_target_pairs={{0,64},{64,128},{128,192},{192,256},{256,320},{320,384},{384,448},... | collective-permute-start | bytes 589832 | tf_op jit(solution)/shard_map/ppermute | solution.py:80
  63.3 15.3 %collective-permute-start.4 = (bf16[64,1536]{1,0:T(8,128)(2,1)S(1)}, bf16[64,1536]{1,0:T(8,128)(2,1)S(1)}, u32[]{:S(2)}, u32[]{:S(2)}) collective-permute-start(bf16[64,1536]{1,0:T(8,128)(2,1)S(1)} %get-tuple-element.7), channel_id=1, source_target_pairs={{0,704},{64,0},{128,64},{192,128},{256,192},{320,256},{384,320},{4... | collective-permute-start | bytes 589832 | tf_op jit(solution)/shard_map/ppermute | solution.py:84
  76.6 7.6 %collective-permute-start.5 = (bf16[64,1536]{1,0:T(8,128)(2,1)S(1)}, bf16[64,1536]{1,0:T(8,128)(2,1)S(1)}, u32[]{:S(2)}, u32[]{:S(2)}) collective-permute-start(bf16[64,1536]{1,0:T(8,128)(2,1)S(1)} %collective-permute-done.3), channel_id=1, source_target_pairs={{0,64},{64,128},{128,192},{192,256},{256,320},{320,384},{384,448},... | collective-permute-start | bytes 589832 | tf_op jit(solution)/shard_map/ppermute | solution.py:80
  78.5 7.6 %collective-permute-start.6 = (bf16[64,1536]{1,0:T(8,128)(2,1)S(1)}, bf16[64,1536]{1,0:T(8,128)(2,1)S(1)}, u32[]{:S(2)}, u32[]{:S(2)}) collective-permute-start(bf16[64,1536]{1,0:T(8,128)(2,1)S(1)} %collective-permute-done.4), channel_id=1, source_target_pairs={{0,704},{64,0},{128,64},{192,128},{256,192},{320,256},{384,320},{4... | collective-permute-start | bytes 589832 | tf_op jit(solution)/shard_map/ppermute | solution.py:84
  84.2 8.5 %collective-permute-start.7 = (bf16[64,1536]{1,0:T(8,128)(2,1)S(1)}, bf16[64,1536]{1,0:T(8,128)(2,1)S(1)}, u32[]{:S(2)}, u32[]{:S(2)}) collective-permute-start(bf16[64,1536]{1,0:T(8,128)(2,1)S(1)} %collective-permute-done.5), channel_id=1, source_target_pairs={{0,64},{64,128},{128,192},{192,256},{256,320},{320,384},{384,448},... | collective-permute-start | bytes 589832 | tf_op jit(solution)/shard_map/ppermute | solution.py:80
  86.1 8.5 %collective-permute-start.8 = (bf16[64,1536]{1,0:T(8,128)(2,1)S(1)}, bf16[64,1536]{1,0:T(8,128)(2,1)S(1)}, u32[]{:S(2)}, u32[]{:S(2)}) collective-permute-start(bf16[64,1536]{1,0:T(8,128)(2,1)S(1)} %collective-permute-done.6), channel_id=1, source_target_pairs={{0,704},{64,0},{128,64},{192,128},{256,192},{320,256},{384,320},{4... | collective-permute-start | bytes 589832 | tf_op jit(solution)/shard_map/ppermute | solution.py:84
  92.7 9.8 %collective-permute-start.9 = (bf16[64,1536]{1,0:T(8,128)(2,1)S(1)}, bf16[64,1536]{1,0:T(8,128)(2,1)S(1)}, u32[]{:S(2)}, u32[]{:S(2)}) collective-permute-start(bf16[64,1536]{1,0:T(8,128)(2,1)S(1)} %collective-permute-done.7), channel_id=1, source_target_pairs={{0,64},{64,128},{128,192},{192,256},{256,320},{320,384},{384,448},... | collective-permute-start | bytes 589832 | tf_op jit(solution)/shard_map/ppermute | solution.py:80
  94.7 9.8 %collective-permute-start.10 = (bf16[64,1536]{1,0:T(8,128)(2,1)S(1)}, bf16[64,1536]{1,0:T(8,128)(2,1)S(1)}, u32[]{:S(2)}, u32[]{:S(2)}) collective-permute-start(bf16[64,1536]{1,0:T(8,128)(2,1)S(1)} %collective-permute-done.8), channel_id=1, source_target_pairs={{0,704},{64,0},{128,64},{192,128},{256,192},{320,256},{384,320},{4... | collective-permute-start | bytes 589832 | tf_op jit(solution)/shard_map/ppermute | solution.py:84
  102.6 9.2 %collective-permute-start.11 = (bf16[64,1536]{1,0:T(8,128)(2,1)S(1)}, bf16[64,1536]{1,0:T(8,128)(2,1)S(1)}, u32[]{:S(2)}, u32[]{:S(2)}) collective-permute-start(bf16[64,1536]{1,0:T(8,128)(2,1)S(1)} %collective-permute-done.9), channel_id=1, source_target_pairs={{0,64},{64,128},{128,192},{192,256},{256,320},{320,384},{384,448},... | collective-permute-start | bytes 589832 | tf_op jit(solution)/shard_map/ppermute | solution.py:80
  104.5 9.2 %collective-permute-start.12 = (bf16[64,1536]{1,0:T(8,128)(2,1)S(1)}, bf16[64,1536]{1,0:T(8,128)(2,1)S(1)}, u32[]{:S(2)}, u32[]{:S(2)}) collective-permute-start(bf16[64,1536]{1,0:T(8,128)(2,1)S(1)} %collective-permute-done.10), channel_id=1, source_target_pairs={{0,704},{64,0},{128,64},{192,128},{256,192},{320,256},{384,320},{4... | collective-permute-start | bytes 589832 | tf_op jit(solution)/shard_map/ppermute | solution.py:84
  111.7 19.0 %collective-permute-start.13 = (bf16[64,1536]{1,0:T(8,128)(2,1)S(1)}, bf16[64,1536]{1,0:T(8,128)(2,1)S(1)}, u32[]{:S(2)}, u32[]{:S(2)}) collective-permute-start(bf16[64,1536]{1,0:T(8,128)(2,1)S(1)} %collective-permute-done.11), channel_id=1, source_target_pairs={{0,64},{64,128},{128,192},{192,256},{256,320},{320,384},{384,448},... | collective-permute-start | bytes 589832 | tf_op jit(solution)/shard_map/ppermute | solution.py:80
  130.7 14.0 %copy-start = (f32[1,1536]{1,0:T(1,128)S(1)}, f32[1,1536]{1,0:T(1,128)}, u32[]{:S(2)}) copy-start(f32[1,1536]{1,0:T(1,128)} %param.10) | copy-start | bytes 18436
  132.3 14.9 %collective-permute-start.14 = (f32[192,1536]{1,0:T(8,128)S(1)}, f32[192,1536]{1,0:T(8,128)}, u32[]{:S(2)}, u32[]{:S(2)}) collective-permute-start(f32[192,1536]{1,0:T(8,128)S(1)} %fusion.1), channel_id=1, source_target_pairs={{0,1},{1,0},{2,3},{3,2},{4,5},{5,4},{6,7},{7,6},{8,9},{9,8},{10,11... | collective-permute-start | bytes 3538952 | tf_op jit(solution)/shard_map/ppermute | solution.py:125

commit v3 on v1

--- a/solution.py
+++ b/solution.py
@@ -14,6 +14,7 @@
 DP = ("z", "ylo")
 TM = ("x", "yhi")
 ROWS = "core"
+Y = ("ylo", "yhi")
 
 
 def attend_kernel(flags_ref, q_ref, kvp_ref, kvc_ref, kvn_ref, o_ref):
@@ -77,8 +78,7 @@
     kv_prev = lax.ppermute(kv, TM, forward)
     kv_next = lax.ppermute(kv, TM, backward)
 
-    head_rows = lax.all_gather(out_weight, "ylo", axis=0, tiled=True)
-    head_rows = lax.all_gather(head_rows, "z", axis=0, tiled=True)
+    own_rows = lax.all_gather(out_weight, "z", axis=0, tiled=True)
 
     offsets = window_offsets[0, 0, 0, 0]
     near_t = time_now + offsets // 9 - 1
@@ -88,17 +88,39 @@
     hit = inside[None, :] & (near_t[None, :] == time_now + deltas[:, None])
     flags = jnp.any(hit, axis=1).astype(jnp.int32)
 
+    ys = lax.axis_size(Y)
+    his = lax.axis_size("yhi")
+    slot = [(y % 2) * his + y // 2 for y in range(ys)]
+    up = [(slot[y], slot[(y + 1) % ys]) for y in range(ys)]
+    down = [(slot[y], slot[(y - 1) % ys]) for y in range(ys)]
+    half = own_rows.shape[0] // 2
+    own_rows, kv_prev, kv_next = lax.optimization_barrier((own_rows, kv_prev, kv_next))
+    from_below = lax.ppermute(own_rows[:half], Y, up)
+    from_above = lax.ppermute(own_rows[half:], Y, down)
+    other_rows = jnp.concatenate([from_below, from_above], axis=0)
+
     attended = attend(flags, queries[0, 0, 0, 0], kv_prev, kv, kv_next)
+
+    parity = lax.axis_index("ylo")
+    zs = lax.axis_size("z")
+    split = attended.reshape(tl, zs, 2, -1)
+    a_own = lax.dynamic_index_in_dim(split, parity, axis=2, keepdims=False).reshape(tl, -1)
+    a_other = lax.dynamic_index_in_dim(split, 1 - parity, axis=2, keepdims=False).reshape(tl, -1)
 
     bands = lax.axis_size(ROWS)
     band = tl // bands
     me = lax.axis_index(ROWS)
-    other = 1 - me
-    mine_rows = lax.dynamic_slice_in_dim(attended, me * band, band, axis=0)
-    other_rows = lax.dynamic_slice_in_dim(attended, other * band, band, axis=0)
-    sent = jnp.dot(other_rows, head_rows, preferred_element_type=jnp.float32)
+
+    def project(start):
+        own = lax.dynamic_slice_in_dim(a_own, start, band, axis=0)
+        far = lax.dynamic_slice_in_dim(a_other, start, band, axis=0)
+        return jnp.dot(own, own_rows, preferred_element_type=jnp.float32) + jnp.dot(
+            far, other_rows, preferred_element_type=jnp.float32
+        )
+
+    sent = project((1 - me) * band)
     got = lax.ppermute(sent, ROWS, [(0, 1), (1, 0)])
-    kept = jnp.dot(mine_rows, head_rows, preferred_element_type=jnp.float32)
+    kept = lax.optimization_barrier(project(me * band))
     projection = kept + got
     mixed = (gate[0][None, :] * projection).astype(jnp.bfloat16)
     return mixed.reshape(1, 1, 1, 1, band, DOUT)

time: 110 us -> 123 us (1.12)
  starting transfers between devices: 10.3 us -> 22.9 us
  blocking collectives: 6.62 us -> 0 us
  local copies, waits for them, and re-layouts: 1.03 us -> 4.57 us
  waiting for transfers between devices: 53.8 us -> 57.3 us
  matrix products: 5.35 us -> 3.35 us
  other arithmetic: 2.07 us -> 3.72 us
    ppermute x1, waiting for transfers between devices: 11.8 us -> 22.9 us  [local(): kv_next = lax.ppermute(kv, TM, backward)]
    ppermute x1, waiting for transfers between devices: 39.5 us -> 32.1 us  [local(): kv_prev = lax.ppermute(kv, TM, forward)]
    all_gather x1 -> x0, blocking collectives: 6.62 us -> none  [local(): head_rows = lax.all_gather(out_weight, 'ylo', axis=0, tiled=True)]
    ppermute x0 -> x2, starting transfers between devices: none -> 6.49 us  [the longest x1 3.55 us: local(): from_above = lax.ppermute(own_rows[half:], Y, down)]
    ppermute x1, starting transfers between devices: 4.18 us -> 10 us  [local(): got = lax.ppermute(sent, ROWS, [(0, 1), (1, 0)])]
    reshape x0 -> x1, other arithmetic: none -> 2.3 us  [local(): return mixed.reshape(1, 1, 1, 1, band, DOUT)]
    dot_general x2 -> x4, matrix products: 5.35 us -> 3.35 us  [the longest x2 2.18 us: project(): jnp.dot(own, own_rows, preferred_element_type=jnp.float32)]
    pallas_call x0 -> x1, local copies, waits for them, and re-layouts: none -> 1.37 us  [attend(): pl.pallas_call(attend_kernel, grid_spec=grid_spec, out_shape=jax.ShapeDty...]
  transfers between devices with their start and end apart: 4 -> 6, of which waited for: 3 -> 3; matrix products, arithmetic and copies ran while one was open for 2% -> 3% of each run, Pallas kernels for 15% -> 14%
where the time goes in v3:
time: 123 us; the launch traced here: 122 us
  waiting for transfers between devices  57.3 us (47%)
  starting transfers between devices  22.9 us (19%)
  Pallas kernels  16.9 us (14%)
  between operations  13.6 us (11%)
  local copies, waits for them, and re-layouts  4.57 us (4%)
  other arithmetic  3.72 us (3%)
  matrix products  3.35 us (3%)
    ppermute x1, waiting for transfers between devices, local(): kv_prev = lax.ppermute(kv, TM, forward)  32.1 us
    ppermute x1, waiting for transfers between devices, local(): kv_next = lax.ppermute(kv, TM, backward)  22.9 us
    pallas_call x1, Pallas kernels, attend(): pl.pallas_call(attend_kernel, grid_spec=grid_spec, out_shape=jax.ShapeDty...  16.9 us
    ppermute x1, starting transfers between devices, local(): got = lax.ppermute(sent, ROWS, [(0, 1), (1, 0)])  10 us
    ppermute x1, starting transfers between devices, local(): kv_prev = lax.ppermute(kv, TM, forward)  5.12 us
    ppermute x1, starting transfers between devices, local(): from_above = lax.ppermute(own_rows[half:], Y, down)  3.55 us
    ppermute x1, starting transfers between devices, local(): from_below = lax.ppermute(own_rows[:half], Y, up)  2.94 us
  transfers between devices with their start and end apart: 6, of which 3 were waited for; matrix products, arithmetic and copies ran while one was open for 3% of the time, Pallas kernels for 14%

profile of v3, /device:TPU:1, one launch (start us, length us, event | category | flops | bytes accessed | tf_op | source)
XLA Modules:
  0.0 122.4 jit_solution(17977093094575574487)
XLA Ops:
  6.5 0.0 all-gather.2.cloned.1.call-start
  6.5 0.7 all-gather.2.cloned.1.call-update
  7.3 5.1 %collective-permute-start = (bf16[384,2,768]{2,1,0:T(2,128)(2,1)}, bf16[384,2,768]{2,1,0:T(2,128)(2,1)S(1)}, u32[]{:S(2)}, u32[]{:S(2)}) collective-permute-start(bf16[384,2,768]{2,1,0:T(2,128)(2,1)} %bitcast.47), channel_id=1, source_target_pairs={{0,2},{2,4},{4,6},{6,8},{8,10},{10,12},{12,14},{14,16},{16,18},{18... | collective-permute-start | bytes 3538952 | tf_op jit(solution)/shard_map/ppermute | solution.py:78
  12.4 1.3 %collective-permute-start.1 = (bf16[384,2,768]{2,1,0:T(2,128)(2,1)}, bf16[384,2,768]{2,1,0:T(2,128)(2,1)S(1)}, u32[]{:S(2)}, u32[]{:S(2)}) collective-permute-start(bf16[384,2,768]{2,1,0:T(2,128)(2,1)} %bitcast.48), channel_id=1, source_target_pairs={{2,0},{4,2},{6,4},{8,6},{10,8},{12,10},{14,12},{16,14},{18,16},{20... | collective-permute-start | bytes 3538952 | tf_op jit(solution)/shard_map/ppermute | solution.py:79
  13.7 0.7 compare_and_fusion
  14.4 0.0 copy-start.4
  14.4 32.1 %collective-permute-done.kvp_ref = bf16[384,2,768]{2,1,0:T(2,128)(2,1)S(1)} collective-permute-done((bf16[384,2,768]{2,1,0:T(2,128)(2,1)}, bf16[384,2,768]{2,1,0:T(2,128)(2,1)S(1)}, u32[]{:S(2)}, u32[]{:S(2)}) %collective-permute-start) | collective-permute-done | bytes 1179680 | tf_op jit(solution)/shard_map/ppermute | solution.py:78
  46.5 0.0 copy-start.2
  46.5 22.9 %collective-permute-done.1.kvn_ref = bf16[384,2,768]{2,1,0:T(2,128)(2,1)S(1)} collective-permute-done((bf16[384,2,768]{2,1,0:T(2,128)(2,1)}, bf16[384,2,768]{2,1,0:T(2,128)(2,1)S(1)}, u32[]{:S(2)}, u32[]{:S(2)}) %collective-permute-start.1) | collective-permute-done | bytes 1179680 | tf_op jit(solution)/shard_map/ppermute | solution.py:79
  69.4 0.0 copy-start.3
  69.4 1.0 copy-done.3
  70.5 0.0 all-gather.2.cloned.1.call-done
  70.5 1.3 %fusion.13 = (bf16[192,1536]{1,0:T(8,128)(2,1)S(1)}, bf16[192,1536]{1,0:T(8,128)(2,1)S(1)}) fusion(bf16[384,1536]{1,0:T(8,128)(2,1)} %all-gather.2.cloned.1.call-done), kind=kLoop, calls=%fused_computation.28 | loop fusion | bytes 2359296 | tf_op jit(solution)/shard_map/slice | solution.py:99
  71.8 0.0 copy-done.2
  71.8 2.9 %collective-permute-start.2 = (bf16[192,1536]{1,0:T(8,128)(2,1)S(1)}, bf16[192,1536]{1,0:T(8,128)(2,1)S(1)}, u32[]{:S(2)}, u32[]{:S(2)}) collective-permute-start(bf16[192,1536]{1,0:T(8,128)(2,1)S(1)} %get-tuple-element.14), channel_id=1, source_target_pairs={{0,32},{32,2},{2,34},{34,4},{4,36},{36,6},{6,38},{38,0},{1,33},{33... | collective-permute-start | bytes 1769480 | tf_op jit(solution)/shard_map/ppermute | solution.py:98
  74.7 0.0 copy-done.4
  74.8 3.6 %collective-permute-start.3 = (bf16[192,1536]{1,0:T(8,128)(2,1)S(1)}, bf16[192,1536]{1,0:T(8,128)(2,1)S(1)}, u32[]{:S(2)}, u32[]{:S(2)}) collective-permute-start(bf16[192,1536]{1,0:T(8,128)(2,1)S(1)} %get-tuple-element.13), channel_id=1, source_target_pairs={{0,38},{32,0},{2,32},{34,2},{4,34},{36,4},{6,36},{38,6},{1,39},{33... | collective-permute-start | bytes 1769480 | tf_op jit(solution)/shard_map/ppermute | solution.py:99
  78.3 0.2 and_reduce_fusion
  78.5 0.5 convert_element_type.6.flags_ref
  79.0 16.9 %shard_map.64 = bf16[384,768]{1,0:T(8,128)(2,1)} custom-call(s32[3]{0:T(128)} %convert_element_type.6.flags_ref, bf16[384,768]{1,0:T(8,128)(2,1)} %bitcast.50, bf16[384,2,768]{2,1,0:T(2,128)(2,1)} %copy-done.2, bf16[384,2,768]{2,1,0:T(2,128)(2,1)} %bitcast.49, bf16[384,2,768]{2,1,0:T(2,128)(2,1)} %copy-done.3), custom_call_target="tpu_custom_call" | custom-call | flops 1358954496 | bytes 4718592 | tf_op jit(solution)/shard_map/pallas_call | solution.py:58
  96.0 1.4 %copy.8 = bf16[384,768]{0,1:T(8,128)(2,1)S(1)} copy(bf16[384,768]{1,0:T(8,128)(2,1)} %shard_map.64) | data formatting | bytes 1179648 | tf_op jit(solution)/shard_map/pallas_call | solution.py:58
  97.3 0.1 constant_dynamic-slice_fusion.1
  97.4 0.0 collective-permute-done.2
  97.5 0.0 collective-permute-done.3
  97.6 0.0 copy-start
  97.6 0.6 fusion.1
  98.2 0.7 copy-done
  98.8 0.0 copy-start.1
  98.8 1.6 %convolution_add_fusion = f32[192,1536]{1,0:T(8,128)} fusion(f32[192,1536]{1,0:T(8,128)S(1)} %fusion.1, bf16[384,1536]{1,0:T(8,128)(2,1)S(1)} %copy-done, bf16[384,384]{0,1:T(8,128)(2,1)S(1)} %bitcast.43, s32[]{:T(128)S(6)} %select_n.60), kind=kOutput, calls=%fused_computation | convolution fusion | flops 226787328 | bytes 3735556 | tf_op jit(solution)/shard_map/dot_general | solution.py:117
  100.4 10.0 %collective-permute-start.4 = (f32[192,1536]{1,0:T(8,128)}, f32[192,1536]{1,0:T(8,128)}, u32[]{:S(2)}, u32[]{:S(2)}) collective-permute-start(f32[192,1536]{1,0:T(8,128)} %convolution_add_fusion), channel_id=1, source_target_pairs={{0,1},{1,0},{2,3},{3,2},{4,5},{5,4},{6,7},{7,6},{8,9},{9,8},{10,11... | collective-permute-start | bytes 3538952 | tf_op jit(solution)/shard_map/ppermute | solution.py:122
  110.5 0.0 copy-done.1
  110.5 0.6 fusion.4
  111.1 0.6 convolution_add_fusion.1
  111.7 1.6 %collective-permute-done.4 = f32[192,1536]{1,0:T(8,128)} collective-permute-done((f32[192,1536]{1,0:T(8,128)}, f32[192,1536]{1,0:T(8,128)}, u32[]{:S(2)}, u32[]{:S(2)}) %collective-permute-start.4) | collective-permute-done | bytes 1179680 | tf_op jit(solution)/shard_map/ppermute | solution.py:122
  113.3 2.3 %fusion = bf16[1,1,1,1,192,1536]{5,4,3,2,1,0:T(8,128)(2,1)} fusion(f32[192,1536]{1,0:T(8,128)S(1)} %convolution_add_fusion.1, f32[192,1536]{1,0:T(8,128)} %collective-permute-done.4, f32[1536]{0:T(1024)S(1)} %reduce), kind=kLoop, calls=%fused_computation.3 | loop fusion | flops 884736 | bytes 2955264 | tf_op jit(solution)/shard_map/reshape | solution.py:126
  (4 shorter events, 0.1 us)
Async XLA Ops:
  6.5 63.9 %all-gather.2.cloned.1.call-start = ((), (), s32[]{:S(2)}) async-start(), calls=%async_computation | async-start | bytes 1277952 | tf_op jit(solution)/shard_map/all_gather | solution.py:81
  7.3 39.2 %collective-permute-start = (bf16[384,2,768]{2,1,0:T(2,128)(2,1)}, bf16[384,2,768]{2,1,0:T(2,128)(2,1)S(1)}, u32[]{:S(2)}, u32[]{:S(2)}) collective-permute-start(bf16[384,2,768]{2,1,0:T(2,128)(2,1)} %bitcast.47), channel_id=1, source_target_pairs={{0,2},{2,4},{4,6},{6,8},{8,10},{10,12},{12,14},{14,16},{16,18},{18... | collective-permute-start | bytes 3538952 | tf_op jit(solution)/shard_map/ppermute | solution.py:78
  12.4 57.0 %collective-permute-start.1 = (bf16[384,2,768]{2,1,0:T(2,128)(2,1)}, bf16[384,2,768]{2,1,0:T(2,128)(2,1)S(1)}, u32[]{:S(2)}, u32[]{:S(2)}) collective-permute-start(bf16[384,2,768]{2,1,0:T(2,128)(2,1)} %bitcast.48), channel_id=1, source_target_pairs={{2,0},{4,2},{6,4},{8,6},{10,8},{12,10},{14,12},{16,14},{18,16},{20... | collective-permute-start | bytes 3538952 | tf_op jit(solution)/shard_map/ppermute | solution.py:79
  14.4 60.4 %copy-start.4 = (s32[3]{0:T(128)S(1)}, s32[3]{0:T(128)}, u32[]{:S(2)}) copy-start(s32[3]{0:T(128)} %constant.69.clone) | copy-start | bytes 40
  46.5 25.3 %copy-start.2 = (bf16[384,2,768]{2,1,0:T(2,128)(2,1)}, bf16[384,2,768]{2,1,0:T(2,128)(2,1)S(1)}, u32[]{:S(2)}) copy-start(bf16[384,2,768]{2,1,0:T(2,128)(2,1)S(1)} %collective-permute-done.kvp_ref) | copy-start | bytes 3538948
  69.4 1.0 copy-start.3
  71.8 25.7 %collective-permute-start.2 = (bf16[192,1536]{1,0:T(8,128)(2,1)S(1)}, bf16[192,1536]{1,0:T(8,128)(2,1)S(1)}, u32[]{:S(2)}, u32[]{:S(2)}) collective-permute-start(bf16[192,1536]{1,0:T(8,128)(2,1)S(1)} %get-tuple-element.14), channel_id=1, source_target_pairs={{0,32},{32,2},{2,34},{34,4},{4,36},{36,6},{6,38},{38,0},{1,33},{33... | collective-permute-start | bytes 1769480 | tf_op jit(solution)/shard_map/ppermute | solution.py:98
  74.8 22.7 %collective-permute-start.3 = (bf16[192,1536]{1,0:T(8,128)(2,1)S(1)}, bf16[192,1536]{1,0:T(8,128)(2,1)S(1)}, u32[]{:S(2)}, u32[]{:S(2)}) collective-permute-start(bf16[192,1536]{1,0:T(8,128)(2,1)S(1)} %get-tuple-element.13), channel_id=1, source_target_pairs={{0,38},{32,0},{2,32},{34,2},{4,34},{36,4},{6,36},{38,6},{1,39},{33... | collective-permute-start | bytes 1769480 | tf_op jit(solution)/shard_map/ppermute | solution.py:99
  97.6 1.3 %copy-start = (bf16[384,1536]{1,0:T(8,128)(2,1)S(1)}, bf16[384,1536]{1,0:T(8,128)(2,1)}, u32[]{:S(2)}) copy-start(bf16[384,1536]{1,0:T(8,128)(2,1)} %all-gather.2.cloned.1.call-done) | copy-start | bytes 3538948
  98.8 11.7 %copy-start.1 = (f32[1,1536]{1,0:T(1,128)S(1)}, f32[1,1536]{1,0:T(1,128)}, u32[]{:S(2)}) copy-start(f32[1,1536]{1,0:T(1,128)} %param.10) | copy-start | bytes 18436
  100.4 12.8 %collective-permute-start.4 = (f32[192,1536]{1,0:T(8,128)}, f32[192,1536]{1,0:T(8,128)}, u32[]{:S(2)}, u32[]{:S(2)}) collective-permute-start(f32[192,1536]{1,0:T(8,128)} %convolution_add_fusion), channel_id=1, source_target_pairs={{0,1},{1,0},{2,3},{3,2},{4,5},{5,4},{6,7},{7,6},{8,9},{9,8},{10,11... | collective-permute-start | bytes 3538952 | tf_op jit(solution)/shard_map/ppermute | solution.py:122
Sparse Core Ops, SparseCore 0:
  9.7 60.4 all-gather.1

commit v4 on v3

--- a/solution.py
+++ b/solution.py
@@ -67,6 +67,19 @@
     )(flags, q, kv_prev, kv_own, kv_next)
 
 
+def gather_direct(piece, axis):
+    count = lax.axis_size(axis)
+    here = lax.axis_index(axis)
+    rows = piece.shape[0]
+    whole = jnp.zeros((count * rows,) + piece.shape[1:], piece.dtype)
+    whole = lax.dynamic_update_slice_in_dim(whole, piece, here * rows, axis=0)
+    for shift in range(1, count):
+        moved = lax.ppermute(piece, axis, [(i, (i + shift) % count) for i in range(count)])
+        at = (here - shift + count) % count
+        whole = lax.dynamic_update_slice_in_dim(whole, moved, at * rows, axis=0)
+    return whole
+
+
 def local(queries, keys_values, window_offsets, out_weight, gate):
     tl = queries.shape[4]
     all_time = lax.axis_size(TM)
@@ -78,7 +91,9 @@
     kv_prev = lax.ppermute(kv, TM, forward)
     kv_next = lax.ppermute(kv, TM, backward)
 
-    own_rows = lax.all_gather(out_weight, "z", axis=0, tiled=True)
+    zs = lax.axis_size("z")
+    spread = jnp.broadcast_to(out_weight[None], (zs,) + out_weight.shape)
+    own_rows = lax.all_to_all(spread, "z", 0, 0, tiled=True).reshape(-1, out_weight.shape[1])
 
     offsets = window_offsets[0, 0, 0, 0]
     near_t = time_now + offsets // 9 - 1
@@ -102,7 +117,6 @@
     attended = attend(flags, queries[0, 0, 0, 0], kv_prev, kv, kv_next)
 
     parity = lax.axis_index("ylo")
-    zs = lax.axis_size("z")
     split = attended.reshape(tl, zs, 2, -1)
     a_own = lax.dynamic_index_in_dim(split, parity, axis=2, keepdims=False).reshape(tl, -1)
     a_other = lax.dynamic_index_in_dim(split, 1 - parity, axis=2, keepdims=False).reshape(tl, -1)

time: 123 us -> 118 us (0.959)
  between operations: 13.6 us -> 0.17 us
  starting transfers between devices: 22.9 us -> 32.7 us
  waiting for transfers between devices: 57.3 us -> 55.5 us
    all_to_all x0 -> x1, starting transfers between devices: none -> 15.8 us  [local(): lax.all_to_all(spread, 'z', 0, 0, tiled=True)]
    ppermute x1, waiting for transfers between devices: 22.9 us -> 15 us  [local(): kv_next = lax.ppermute(kv, TM, backward)]
    ppermute x1, waiting for transfers between devices: 32.1 us -> 38.9 us  [local(): kv_prev = lax.ppermute(kv, TM, forward)]
    ppermute x1, starting transfers between devices: 10 us -> 3.88 us  [local(): got = lax.ppermute(sent, ROWS, [(0, 1), (1, 0)])]
    broadcast_in_dim x0 -> x1, local copies, waits for them, and re-layouts: none -> 2.02 us  [local(): spread = jnp.broadcast_to(out_weight[None], (zs,) + out_weight.shape)]
    unnamed x11 -> x9, local copies, waits for them, and re-layouts: 1.76 us -> 0.06 us
where the time goes in v4:
time: 118 us; the launch traced here: 117 us
  waiting for transfers between devices  55.5 us (47%)
  starting transfers between devices  32.7 us (28%)
  Pallas kernels  17 us (14%)
  local copies, waits for them, and re-layouts  5.53 us (5%)
  matrix products  3.38 us (3%)
  other arithmetic  3.14 us (3%)
    ppermute x1, waiting for transfers between devices, local(): kv_prev = lax.ppermute(kv, TM, forward)  38.9 us
    pallas_call x1, Pallas kernels, attend(): pl.pallas_call(attend_kernel, grid_spec=grid_spec, out_shape=jax.ShapeDty...  17 us
    all_to_all x1, starting transfers between devices, local(): lax.all_to_all(spread, 'z', 0, 0, tiled=True)  15.8 us
    ppermute x1, waiting for transfers between devices, local(): kv_next = lax.ppermute(kv, TM, backward)  15 us
    ppermute x1, starting transfers between devices, local(): kv_prev = lax.ppermute(kv, TM, forward)  5.26 us
    ppermute x1, starting transfers between devices, local(): from_above = lax.ppermute(own_rows[half:], Y, down)  4.57 us
    ppermute x1, starting transfers between devices, local(): got = lax.ppermute(sent, ROWS, [(0, 1), (1, 0)])  3.88 us
  transfers between devices with their start and end apart: 6, of which 3 were waited for; matrix products, arithmetic and copies ran while one was open for 3% of the time, Pallas kernels for 14%

profile of v4, /device:TPU:1, one launch (start us, length us, event | category | flops | bytes accessed | tf_op | source)
XLA Modules:
  0.0 117.4 jit_solution(18351829693408313736)
XLA Ops:
  0.0 2.0 %broadcast_in_dim.2 = bf16[12,32,1536]{2,1,0:T(8,128)(2,1)} broadcast(bf16[32,1536]{1,0:T(8,128)(2,1)} %param.9), dimensions={1,2} | broadcast | bytes 1277952 | tf_op jit(solution)/shard_map/broadcast_in_dim | solution.py:95
  2.0 0.0 copy-start.2
  2.0 0.0 copy-start.1
  2.0 15.8 %all-to-all-start = ((bf16[12,32,1536]{2,1,0:T(8,128)(2,1)}), bf16[12,32,1536]{2,1,0:T(8,128)(2,1)S(1)}, u32[]{:S(2)}, u32[]{:S(2)}) async-start(bf16[12,32,1536]{2,1,0:T(8,128)(2,1)} %broadcast_in_dim.2), calls=%async_computation | async-start | bytes 2359296 | tf_op jit(solution)/shard_map/all_to_all | solution.py:96
  17.9 0.0 copy-done.2
  17.9 5.3 %collective-permute-start = (bf16[384,2,768]{2,1,0:T(2,128)(2,1)S(1)}, bf16[384,2,768]{2,1,0:T(2,128)(2,1)}, u32[]{:S(2)}, u32[]{:S(2)}) collective-permute-start(bf16[384,2,768]{2,1,0:T(2,128)(2,1)S(1)} %bitcast.52), channel_id=1, source_target_pairs={{0,2},{2,4},{4,6},{6,8},{8,10},{10,12},{12,14},{14,16},{16,18},{18... | collective-permute-start | bytes 3538952 | tf_op jit(solution)/shard_map/ppermute | solution.py:91
  23.1 1.3 %collective-permute-start.1 = (bf16[384,2,768]{2,1,0:T(2,128)(2,1)S(1)}, bf16[384,2,768]{2,1,0:T(2,128)(2,1)}, u32[]{:S(2)}, u32[]{:S(2)}) collective-permute-start(bf16[384,2,768]{2,1,0:T(2,128)(2,1)S(1)} %bitcast.53), channel_id=1, source_target_pairs={{2,0},{4,2},{6,4},{8,6},{10,8},{12,10},{14,12},{16,14},{18,16},{20... | collective-permute-start | bytes 3538952 | tf_op jit(solution)/shard_map/ppermute | solution.py:92
  24.4 0.0 copy-done.1
  24.5 38.9 %collective-permute-done.kvp_ref = bf16[384,2,768]{2,1,0:T(2,128)(2,1)} collective-permute-done((bf16[384,2,768]{2,1,0:T(2,128)(2,1)S(1)}, bf16[384,2,768]{2,1,0:T(2,128)(2,1)}, u32[]{:S(2)}, u32[]{:S(2)}) %collective-permute-start) | collective-permute-done | bytes 1179680 | tf_op jit(solution)/shard_map/ppermute | solution.py:91
  63.4 15.0 %collective-permute-done.1.kvn_ref = bf16[384,2,768]{2,1,0:T(2,128)(2,1)} collective-permute-done((bf16[384,2,768]{2,1,0:T(2,128)(2,1)S(1)}, bf16[384,2,768]{2,1,0:T(2,128)(2,1)}, u32[]{:S(2)}, u32[]{:S(2)}) %collective-permute-start.1) | collective-permute-done | bytes 1179680 | tf_op jit(solution)/shard_map/ppermute | solution.py:92
  78.4 0.0 all-to-all-done
  78.4 0.0 copy-start.3
  78.4 0.9 fusion.13
  79.3 1.9 %collective-permute-start.2 = (bf16[192,1536]{1,0:T(8,128)(2,1)S(1)}, bf16[192,1536]{1,0:T(8,128)(2,1)S(1)}, u32[]{:S(2)}, u32[]{:S(2)}) collective-permute-start(bf16[192,1536]{1,0:T(8,128)(2,1)S(1)} %get-tuple-element.14), channel_id=1, source_target_pairs={{0,32},{32,2},{2,34},{34,4},{4,36},{36,6},{6,38},{38,0},{1,33},{33... | collective-permute-start | bytes 1769480 | tf_op jit(solution)/shard_map/ppermute | solution.py:113
  81.2 0.0 copy-done.3
  81.2 4.6 %collective-permute-start.3 = (bf16[192,1536]{1,0:T(8,128)(2,1)}, bf16[192,1536]{1,0:T(8,128)(2,1)}, u32[]{:S(2)}, u32[]{:S(2)}) collective-permute-start(bf16[192,1536]{1,0:T(8,128)(2,1)} %get-tuple-element.13), channel_id=1, source_target_pairs={{0,38},{32,0},{2,32},{34,2},{4,34},{36,4},{6,36},{38,6},{1,39},{33... | collective-permute-start | bytes 1769480 | tf_op jit(solution)/shard_map/ppermute | solution.py:114
  85.8 0.2 and_reduce_fusion
  86.0 0.6 convert_element_type.6.flags_ref
  86.6 17.0 %shard_map.64 = bf16[384,768]{1,0:T(8,128)(2,1)} custom-call(s32[3]{0:T(128)} %convert_element_type.6.flags_ref, bf16[384,768]{1,0:T(8,128)(2,1)} %bitcast.54, bf16[384,2,768]{2,1,0:T(2,128)(2,1)} %collective-permute-done.kvp_ref, bf16[384,2,768]{2,1,0:T(2,128)(2,1)} %bitcast.51, bf16[384,2,768]{2,1,0:T(2,128)(2,1)} %collective-permute-done.1.kvn_ref), custom_call_target="tpu_custom_call" | custom-call | flops 1358954496 | bytes 4718592 | tf_op jit(solution)/shard_map/pallas_call | solution.py:58
  103.6 1.4 %copy.8 = bf16[384,768]{0,1:T(8,128)(2,1)S(1)} copy(bf16[384,768]{1,0:T(8,128)(2,1)} %shard_map.64) | data formatting | bytes 1179648 | tf_op jit(solution)/shard_map/pallas_call | solution.py:58
  104.9 0.1 constant_dynamic-slice_fusion.1
  105.0 0.0 collective-permute-done.2
  105.1 0.0 collective-permute-done.3
  105.1 1.1 constant_dynamic-update-slice_fusion
  106.2 0.6 fusion.1
  106.8 0.0 copy-start
  106.8 1.6 %convolution_add_fusion = f32[192,1536]{1,0:T(8,128)} fusion(f32[192,1536]{1,0:T(8,128)S(1)} %fusion.1, bf16[384,1536]{1,0:T(8,128)(2,1)S(1)} %bitcast.44, bf16[384,384]{0,1:T(8,128)(2,1)S(1)} %bitcast.47, s32[]{:T(128)S(6)} %select_n.60), kind=kOutput, calls=%fused_computation | convolution fusion | flops 226787328 | bytes 3735556 | tf_op jit(solution)/shard_map/dot_general | solution.py:131
  108.4 3.9 %collective-permute-start.4 = (f32[192,1536]{1,0:T(8,128)}, f32[192,1536]{1,0:T(8,128)}, u32[]{:S(2)}, u32[]{:S(2)}) collective-permute-start(f32[192,1536]{1,0:T(8,128)} %convolution_add_fusion), channel_id=1, source_target_pairs={{0,1},{1,0},{2,3},{3,2},{4,5},{5,4},{6,7},{7,6},{8,9},{9,8},{10,11... | collective-permute-start | bytes 3538952 | tf_op jit(solution)/shard_map/ppermute | solution.py:136
  112.3 0.0 copy-done
  112.4 0.6 fusion.4
  113.0 0.6 convolution_add_fusion.1
  113.5 1.6 %collective-permute-done.4 = f32[192,1536]{1,0:T(8,128)} collective-permute-done((f32[192,1536]{1,0:T(8,128)}, f32[192,1536]{1,0:T(8,128)}, u32[]{:S(2)}, u32[]{:S(2)}) %collective-permute-start.4) | collective-permute-done | bytes 1179680 | tf_op jit(solution)/shard_map/ppermute | solution.py:136
  115.1 2.3 %fusion = bf16[1,1,1,1,192,1536]{5,4,3,2,1,0:T(8,128)(2,1)} fusion(f32[192,1536]{1,0:T(8,128)S(1)} %convolution_add_fusion.1, f32[192,1536]{1,0:T(8,128)} %collective-permute-done.4, f32[1536]{0:T(1024)S(1)} %reduce), kind=kLoop, calls=%fused_computation.3 | loop fusion | flops 884736 | bytes 2955264 | tf_op jit(solution)/shard_map/reshape | solution.py:140
  (4 shorter events, 0.1 us)
Async XLA Ops:
  2.0 15.9 %copy-start.2 = (bf16[1,1,1,1,384,2,768]{6,5,4,3,2,1,0:T(2,128)(2,1)S(1)}, bf16[1,1,1,1,384,2,768]{6,5,4,3,2,1,0:T(2,128)(2,1)}, u32[]{:S(2)}) copy-start(bf16[1,1,1,1,384,2,768]{6,5,4,3,2,1,0:T(2,128)(2,1)} %param.7) | copy-start | bytes 3538948
  2.0 22.4 %copy-start.1 = (s32[1,1,1,1,3]{4,3,2,1,0:T(1,128)S(1)}, s32[1,1,1,1,3]{4,3,2,1,0:T(1,128)}, u32[]{:S(2)}) copy-start(s32[1,1,1,1,3]{4,3,2,1,0:T(1,128)} %param.8) | copy-start | bytes 40
  2.0 76.4 %all-to-all-start = ((bf16[12,32,1536]{2,1,0:T(8,128)(2,1)}), bf16[12,32,1536]{2,1,0:T(8,128)(2,1)S(1)}, u32[]{:S(2)}, u32[]{:S(2)}) async-start(bf16[12,32,1536]{2,1,0:T(8,128)(2,1)} %broadcast_in_dim.2), calls=%async_computation | async-start | bytes 2359296 | tf_op jit(solution)/shard_map/all_to_all | solution.py:96
  17.9 45.5 %collective-permute-start = (bf16[384,2,768]{2,1,0:T(2,128)(2,1)S(1)}, bf16[384,2,768]{2,1,0:T(2,128)(2,1)}, u32[]{:S(2)}, u32[]{:S(2)}) collective-permute-start(bf16[384,2,768]{2,1,0:T(2,128)(2,1)S(1)} %bitcast.52), channel_id=1, source_target_pairs={{0,2},{2,4},{4,6},{6,8},{8,10},{10,12},{12,14},{14,16},{16,18},{18... | collective-permute-start | bytes 3538952 | tf_op jit(solution)/shard_map/ppermute | solution.py:91
  23.1 55.3 %collective-permute-start.1 = (bf16[384,2,768]{2,1,0:T(2,128)(2,1)S(1)}, bf16[384,2,768]{2,1,0:T(2,128)(2,1)}, u32[]{:S(2)}, u32[]{:S(2)}) collective-permute-start(bf16[384,2,768]{2,1,0:T(2,128)(2,1)S(1)} %bitcast.53), channel_id=1, source_target_pairs={{2,0},{4,2},{6,4},{8,6},{10,8},{12,10},{14,12},{16,14},{18,16},{20... | collective-permute-start | bytes 3538952 | tf_op jit(solution)/shard_map/ppermute | solution.py:92
  78.4 2.8 %copy-start.3 = (s32[3]{0:T(128)S(1)}, s32[3]{0:T(128)}, u32[]{:S(2)}) copy-start(s32[3]{0:T(128)} %constant.69.clone) | copy-start | bytes 40
  79.3 25.7 %collective-permute-start.2 = (bf16[192,1536]{1,0:T(8,128)(2,1)S(1)}, bf16[192,1536]{1,0:T(8,128)(2,1)S(1)}, u32[]{:S(2)}, u32[]{:S(2)}) collective-permute-start(bf16[192,1536]{1,0:T(8,128)(2,1)S(1)} %get-tuple-element.14), channel_id=1, source_target_pairs={{0,32},{32,2},{2,34},{34,4},{4,36},{36,6},{6,38},{38,0},{1,33},{33... | collective-permute-start | bytes 1769480 | tf_op jit(solution)/shard_map/ppermute | solution.py:113
  81.2 23.8 %collective-permute-start.3 = (bf16[192,1536]{1,0:T(8,128)(2,1)}, bf16[192,1536]{1,0:T(8,128)(2,1)}, u32[]{:S(2)}, u32[]{:S(2)}) collective-permute-start(bf16[192,1536]{1,0:T(8,128)(2,1)} %get-tuple-element.13), channel_id=1, source_target_pairs={{0,38},{32,0},{2,32},{34,2},{4,34},{36,4},{6,36},{38,6},{1,39},{33... | collective-permute-start | bytes 1769480 | tf_op jit(solution)/shard_map/ppermute | solution.py:114
  106.8 5.5 %copy-start = (f32[1,1536]{1,0:T(1,128)S(1)}, f32[1,1536]{1,0:T(1,128)}, u32[]{:S(2)}) copy-start(f32[1,1536]{1,0:T(1,128)} %param.10) | copy-start | bytes 18436
  108.4 6.7 %collective-permute-start.4 = (f32[192,1536]{1,0:T(8,128)}, f32[192,1536]{1,0:T(8,128)}, u32[]{:S(2)}, u32[]{:S(2)}) collective-permute-start(f32[192,1536]{1,0:T(8,128)} %convolution_add_fusion), channel_id=1, source_target_pairs={{0,1},{1,0},{2,3},{3,2},{4,5},{5,4},{6,7},{7,6},{8,9},{9,8},{10,11... | collective-permute-start | bytes 3538952 | tf_op jit(solution)/shard_map/ppermute | solution.py:136

commit v5 on v4

--- a/solution.py
+++ b/solution.py
@@ -17,54 +17,92 @@
 Y = ("ylo", "yhi")
 
 
-def attend_kernel(flags_ref, q_ref, kvp_ref, kvc_ref, kvn_ref, o_ref):
+def scores_of(q, kv_ref, live):
     scale = float(HD) ** (-0.5)
+    s = lax.dot_general(
+        q, kv_ref[:, 0, :], (((1,), (1,)), ((), ())), preferred_element_type=jnp.float32
+    ) * scale
+    return jnp.where(live, s, -jnp.inf)
+
+
+def centre_kernel(flags_ref, q_ref, kv_ref, m_ref, l_ref, acc_ref):
+    live = flags_ref[1] > 0
+    s = scores_of(q_ref[...], kv_ref, live)
+    top = jnp.max(s, axis=1, keepdims=True)
+    p = jnp.where(live, jnp.exp(s - top), 0.0)
+    m_ref[0] = jnp.where(live, top, -jnp.inf)
+    l_ref[0] = p.sum(axis=1, keepdims=True)
+    acc_ref[...] = jnp.dot(
+        p.astype(jnp.bfloat16), kv_ref[:, 1, :], preferred_element_type=jnp.float32
+    )
+
+
+def side_kernel(flags_ref, q_ref, kvp_ref, kvn_ref, m_ref, l_ref, acc_ref, o_ref):
     q = q_ref[...]
-    tiles = (kvp_ref, kvc_ref, kvn_ref)
-    scores = []
-    for j, kv_ref in enumerate(tiles):
-        k = kv_ref[:, 0, :]
-        s = lax.dot_general(
-            q, k, (((1,), (1,)), ((), ())), preferred_element_type=jnp.float32
-        ) * scale
-        scores.append(jnp.where(flags_ref[j] > 0, s, -jnp.inf))
-    top = jnp.max(scores[0], axis=1, keepdims=True)
-    for s in scores[1:]:
-        top = jnp.maximum(top, jnp.max(s, axis=1, keepdims=True))
-    probs = [jnp.exp(s - top) for s in scores]
-    total = probs[0].sum(axis=1, keepdims=True)
-    for p in probs[1:]:
-        total = total + p.sum(axis=1, keepdims=True)
-    inv = 1.0 / total
-    acc = None
-    for p, kv_ref in zip(probs, tiles):
-        w = (p * inv).astype(jnp.bfloat16)
-        part = jnp.dot(w, kv_ref[:, 1, :], preferred_element_type=jnp.float32)
-        acc = part if acc is None else acc + part
-    o_ref[...] = acc.astype(o_ref.dtype)
-
-
-def attend(flags, q, kv_prev, kv_own, kv_next):
+    s_p = scores_of(q, kvp_ref, flags_ref[0] > 0)
+    s_n = scores_of(q, kvn_ref, flags_ref[2] > 0)
+    m_c = m_ref[0]
+    top = jnp.maximum(
+        m_c, jnp.maximum(jnp.max(s_p, axis=1, keepdims=True), jnp.max(s_n, axis=1, keepdims=True))
+    )
+    alpha = jnp.exp(m_c - top)
+    p_p = jnp.exp(s_p - top)
+    p_n = jnp.exp(s_n - top)
+    total = alpha * l_ref[0] + p_p.sum(axis=1, keepdims=True) + p_n.sum(axis=1, keepdims=True)
+    acc = alpha * acc_ref[...]
+    acc = acc + jnp.dot(p_p.astype(jnp.bfloat16), kvp_ref[:, 1, :], preferred_element_type=jnp.float32)
+    acc = acc + jnp.dot(p_n.astype(jnp.bfloat16), kvn_ref[:, 1, :], preferred_element_type=jnp.float32)
+    o_ref[...] = (acc / total).astype(o_ref.dtype)
+
+
+def attend_centre(flags, q, kv_own):
     tl, width = q.shape
     heads = width // HD
     kv_spec = pl.BlockSpec((tl, 2, HD), lambda h, f: (0, 0, h))
-    grid_spec = pltpu.PrefetchScalarGridSpec(
-        num_scalar_prefetch=1,
-        grid=(heads,),
-        in_specs=[pl.BlockSpec((tl, HD), lambda h, f: (0, h)), kv_spec, kv_spec, kv_spec],
-        out_specs=pl.BlockSpec((tl, HD), lambda h, f: (0, h)),
-    )
-    flops = heads * 2 * 2 * tl * 3 * tl * HD
+    q_spec = pl.BlockSpec((tl, HD), lambda h, f: (0, h))
+    stat_spec = pl.BlockSpec((1, tl, 1), lambda h, f: (h, 0, 0))
+    stat_shape = jax.ShapeDtypeStruct((heads, tl, 1), jnp.float32)
+    tile_flops = heads * 2 * 2 * tl * tl * HD
+    m_c, l_c, acc_c = pl.pallas_call(
+        centre_kernel,
+        grid_spec=pltpu.PrefetchScalarGridSpec(
+            num_scalar_prefetch=1,
+            grid=(heads,),
+            in_specs=[q_spec, kv_spec],
+            out_specs=[stat_spec, stat_spec, q_spec],
+        ),
+        out_shape=[stat_shape, stat_shape, jax.ShapeDtypeStruct((tl, width), jnp.float32)],
+        cost_estimate=pl.CostEstimate(
+            flops=tile_flops,
+            transcendentals=heads * tl * tl,
+            bytes_accessed=tl * width * 2 * 3 + tl * width * 4,
+        ),
+    )(flags, q, kv_own)
+    return m_c, l_c, acc_c
+
+
+def attend_sides(flags, q, kv_prev, kv_next, m_c, l_c, acc_c):
+    tl, width = q.shape
+    heads = width // HD
+    kv_spec = pl.BlockSpec((tl, 2, HD), lambda h, f: (0, 0, h))
+    q_spec = pl.BlockSpec((tl, HD), lambda h, f: (0, h))
+    stat_spec = pl.BlockSpec((1, tl, 1), lambda h, f: (h, 0, 0))
+    tile_flops = heads * 2 * 2 * tl * tl * HD
     return pl.pallas_call(
-        attend_kernel,
-        grid_spec=grid_spec,
+        side_kernel,
+        grid_spec=pltpu.PrefetchScalarGridSpec(
+            num_scalar_prefetch=1,
+            grid=(heads,),
+            in_specs=[q_spec, kv_spec, kv_spec, stat_spec, stat_spec, q_spec],
+            out_specs=q_spec,
+        ),
         out_shape=jax.ShapeDtypeStruct((tl, width), jnp.bfloat16),
         cost_estimate=pl.CostEstimate(
-            flops=flops,
-            transcendentals=heads * tl * 3 * tl,
-            bytes_accessed=2 * (tl * width * 2 + 3 * tl * 2 * width),
-        ),
-    )(flags, q, kv_prev, kv_own, kv_next)
+            flops=2 * tile_flops,
+            transcendentals=2 * heads * tl * tl,
+            bytes_accessed=tl * width * 2 * 6 + tl * width * 4,
+        ),
+    )(flags, q, kv_prev, kv_next, m_c, l_c, acc_c)
 
 
 def gather_direct(piece, axis):
@@ -109,12 +147,15 @@
     up = [(slot[y], slot[(y + 1) % ys]) for y in range(ys)]
     down = [(slot[y], slot[(y - 1) % ys]) for y in range(ys)]
     half = own_rows.shape[0] // 2
-    own_rows, kv_prev, kv_next = lax.optimization_barrier((own_rows, kv_prev, kv_next))
+    q = queries[0, 0, 0, 0]
+    centre = attend_centre(flags, q, kv)
+    own_rows, kv_prev, kv_next, centre = lax.optimization_barrier(
+        (own_rows, kv_prev, kv_next, centre)
+    )
     from_below = lax.ppermute(own_rows[:half], Y, up)
     from_above = lax.ppermute(own_rows[half:], Y, down)
-    other_rows = jnp.concatenate([from_below, from_above], axis=0)
-
-    attended = attend(flags, queries[0, 0, 0, 0], kv_prev, kv, kv_next)
+
+    attended = attend_sides(flags, q, kv_prev, kv_next, *centre)
 
     parity = lax.axis_index("ylo")
     split = attended.reshape(tl, zs, 2, -1)
@@ -128,9 +169,9 @@
     def project(start):
         own = lax.dynamic_slice_in_dim(a_own, start, band, axis=0)
         far = lax.dynamic_slice_in_dim(a_other, start, band, axis=0)
-        return jnp.dot(own, own_rows, preferred_element_type=jnp.float32) + jnp.dot(
-            far, other_rows, preferred_element_type=jnp.float32
-        )
+        part = jnp.dot(own, own_rows, preferred_element_type=jnp.float32)
+        part = part + jnp.dot(far[:, :half], from_below, preferred_element_type=jnp.float32)
+        return part + jnp.dot(far[:, half:], from_above, preferred_element_type=jnp.float32)
 
     sent = project((1 - me) * band)
     got = lax.ppermute(sent, ROWS, [(0, 1), (1, 0)])

time: 118 us -> 114 us (0.966)
  the two profiles are of different devices: /device:TPU:1 before, /device:TPU:7 now
where the time goes in v5:
time: 114 us
  waiting for transfers between devices  41.1 us (36%)
  starting transfers between devices  38.7 us (34%)
  Pallas kernels  21.4 us (19%)
  local copies, waits for them, and re-layouts  5.27 us (5%)
  matrix products  3.91 us (3%)
  other arithmetic  3.07 us (3%)
    ppermute x1, waiting for transfers between devices, local(): kv_next = lax.ppermute(kv, TM, backward)  39.8 us
    all_to_all x1, starting transfers between devices, local(): lax.all_to_all(spread, 'z', 0, 0, tiled=True)  15 us
    pallas_call x1, Pallas kernels, attend_sides(): pl.pallas_call(side_kernel, grid_spec=pltpu.PrefetchScalarGridSpec(num_sc...  13 us
    pallas_call x1, Pallas kernels, attend_centre(): pl.pallas_call(centre_kernel, grid_spec=pltpu.PrefetchScalarGridSpec(num_...  8.43 us
    ppermute x1, starting transfers between devices, local(): from_below = lax.ppermute(own_rows[:half], Y, up)  8.11 us
    ppermute x1, starting transfers between devices, local(): kv_next = lax.ppermute(kv, TM, backward)  6.15 us
    ppermute x1, starting transfers between devices, local(): got = lax.ppermute(sent, ROWS, [(0, 1), (1, 0)])  5.55 us
    reshape x1, other arithmetic, local(): return mixed.reshape(1, 1, 1, 1, band, DOUT)  2.3 us
  transfers between devices with their start and end apart: 6, of which 2 were waited for; matrix products, arithmetic and copies ran while one was open for 4% of the time, Pallas kernels for 19%

profile of v5, /device:TPU:7, one launch (start us, length us, event | category | flops | bytes accessed | tf_op | source)
XLA Modules:
  0.0 113.7 jit_solution(2493742634165130604)
XLA Ops:
  0.0 2.0 %broadcast_in_dim.2 = bf16[12,32,1536]{2,1,0:T(8,128)(2,1)} broadcast(bf16[32,1536]{1,0:T(8,128)(2,1)} %param.9), dimensions={1,2} | broadcast | bytes 1277952 | tf_op jit(solution)/shard_map/broadcast_in_dim | solution.py:133
  2.0 0.0 copy-start.4
  2.0 0.0 copy-start.3
  2.0 15.0 %all-to-all-start = ((bf16[12,32,1536]{2,1,0:T(8,128)(2,1)}), bf16[12,32,1536]{2,1,0:T(8,128)(2,1)S(1)}, u32[]{:S(2)}, u32[]{:S(2)}) async-start(bf16[12,32,1536]{2,1,0:T(8,128)(2,1)} %broadcast_in_dim.2), calls=%async_computation | async-start | bytes 2359296 | tf_op jit(solution)/shard_map/all_to_all | solution.py:134
  17.1 6.2 %collective-permute-start.1 = (bf16[384,2,768]{2,1,0:T(2,128)(2,1)}, bf16[384,2,768]{2,1,0:T(2,128)(2,1)S(1)}, u32[]{:S(2)}, u32[]{:S(2)}) collective-permute-start(bf16[384,2,768]{2,1,0:T(2,128)(2,1)} %bitcast.7.kv_ref), channel_id=1, source_target_pairs={{2,0},{4,2},{6,4},{8,6},{10,8},{12,10},{14,12},{16,14},{18,16},{20... | collective-permute-start | bytes 3538952 | tf_op jit(solution)/shard_map/ppermute | solution.py:130
  23.2 1.9 %collective-permute-start = (bf16[384,2,768]{2,1,0:T(2,128)(2,1)}, bf16[384,2,768]{2,1,0:T(2,128)(2,1)S(1)}, u32[]{:S(2)}, u32[]{:S(2)}) collective-permute-start(bf16[384,2,768]{2,1,0:T(2,128)(2,1)} %bitcast.7.kv_ref), channel_id=1, source_target_pairs={{0,2},{2,4},{4,6},{6,8},{8,10},{10,12},{12,14},{14,16},{16,18},{18... | collective-permute-start | bytes 3538952 | tf_op jit(solution)/shard_map/ppermute | solution.py:129
  25.2 0.0 copy-done.4
  25.2 0.0 copy-done.3
  25.2 0.2 and_reduce_fusion
  25.4 0.5 convert_element_type.6.flags_ref
  25.9 8.4 %shard_map.64 = (f32[6,384,1]{2,1,0:T(8,128)}, f32[6,384,1]{2,1,0:T(8,128)}, f32[384,768]{1,0:T(8,128)}) custom-call(s32[3]{0:T(128)} %convert_element_type.6.flags_ref, bf16[384,768]{1,0:T(8,128)(2,1)} %bitcast.48, bf16[384,2,768]{2,1,0:T(2,128)(2,1)} %bitcast.7.kv_ref), custom_call_target="tpu_custom_call" | custom-call | flops 452984832 | bytes 2949120 | tf_op jit(solution)/shard_map/pallas_call | solution.py:66
  34.4 39.8 %collective-permute-done.1.kvn_ref = bf16[384,2,768]{2,1,0:T(2,128)(2,1)S(1)} collective-permute-done((bf16[384,2,768]{2,1,0:T(2,128)(2,1)}, bf16[384,2,768]{2,1,0:T(2,128)(2,1)S(1)}, u32[]{:S(2)}, u32[]{:S(2)}) %collective-permute-start.1) | collective-permute-done | bytes 1179680 | tf_op jit(solution)/shard_map/ppermute | solution.py:130
  74.2 0.0 copy-start
  74.2 0.0 collective-permute-done.kvp_ref
  74.2 0.0 copy-start.1
  74.2 0.0 all-to-all-done
  74.2 1.2 %fusion.19 = (bf16[192,1536]{1,0:T(8,128)(2,1)}, bf16[192,1536]{1,0:T(8,128)(2,1)}) fusion(bf16[384,1536]{1,0:T(8,128)(2,1)S(1)} %bitcast.45), kind=kLoop, calls=%fused_computation.32 | loop fusion | bytes 2359296 | tf_op jit(solution)/shard_map/slice | solution.py:155
  75.4 0.2 copy-done
  75.6 0.4 copy-done.1
  76.0 8.1 %collective-permute-start.2 = (bf16[192,1536]{1,0:T(8,128)(2,1)}, bf16[192,1536]{1,0:T(8,128)(2,1)S(1)}, u32[]{:S(2)}, u32[]{:S(2)}) collective-permute-start(bf16[192,1536]{1,0:T(8,128)(2,1)} %get-tuple-element.25), channel_id=1, source_target_pairs={{0,32},{32,2},{2,34},{34,4},{4,36},{36,6},{6,38},{38,0},{1,33},{33... | collective-permute-start | bytes 1769480 | tf_op jit(solution)/shard_map/ppermute | solution.py:155
  84.1 1.9 %collective-permute-start.3 = (bf16[192,1536]{1,0:T(8,128)(2,1)}, bf16[192,1536]{1,0:T(8,128)(2,1)S(1)}, u32[]{:S(2)}, u32[]{:S(2)}) collective-permute-start(bf16[192,1536]{1,0:T(8,128)(2,1)} %get-tuple-element.26), channel_id=1, source_target_pairs={{0,38},{32,0},{2,32},{34,2},{4,34},{36,4},{6,36},{38,6},{1,39},{33... | collective-permute-start | bytes 1769480 | tf_op jit(solution)/shard_map/ppermute | solution.py:156
  86.0 13.0 %shard_map.65 = bf16[384,768]{1,0:T(8,128)(2,1)} custom-call(s32[3]{0:T(128)} %convert_element_type.6.flags_ref, bf16[384,768]{1,0:T(8,128)(2,1)} %bitcast.49, bf16[384,2,768]{2,1,0:T(2,128)(2,1)} %copy-done.1, bf16[384,2,768]{2,1,0:T(2,128)(2,1)} %copy-done, f32[6,384,1]{2,1,0:T(8,128)} %get-tuple-element.19.m_ref, f32[6,384,1]{2,1,0:T(8,128)} %get-tuple-element.20.l_ref, ...), custom_call_target="tpu_custom_call" | custom-call | flops 905969664 | bytes 4718592 | tf_op jit(solution)/shard_map/pallas_call | solution.py:91
  99.0 1.4 %copy.8 = bf16[384,768]{0,1:T(8,128)(2,1)S(1)} copy(bf16[384,768]{1,0:T(8,128)(2,1)} %shard_map.65) | data formatting | bytes 1179648 | tf_op jit(solution)/shard_map/pallas_call | solution.py:91
  100.4 0.1 constant_dynamic-slice_fusion.1
  100.5 0.0 collective-permute-done.2
  100.5 0.4 fusion.7
  100.9 0.0 collective-permute-done.3
  100.9 0.4 fusion.5
  101.4 0.0 copy-start.2
  101.4 1.6 %fusion.1 = f32[192,1536]{1,0:T(8,128)} fusion(f32[192,1536]{1,0:T(8,128)S(1)} %fusion.5, f32[192,1536]{1,0:T(8,128)S(1)} %fusion.7, bf16[384,1536]{1,0:T(8,128)(2,1)S(1)} %bitcast.46, bf16[384,384]{0,1:T(8,128)(2,1)S(1)} %bitcast.51, s32[]{:T(128)S(6)} %select_n.60), kind=kOutput, calls=%fused_computation.3 | convolution fusion | flops 227082240 | bytes 4915204 | tf_op jit(solution)/shard_map/dot_general | solution.py:172
  103.0 5.6 %collective-permute-start.4 = (f32[192,1536]{1,0:T(8,128)}, f32[192,1536]{1,0:T(8,128)}, u32[]{:S(2)}, u32[]{:S(2)}) collective-permute-start(f32[192,1536]{1,0:T(8,128)} %fusion.1), channel_id=1, source_target_pairs={{0,1},{1,0},{2,3},{3,2},{4,5},{5,4},{6,7},{7,6},{8,9},{9,8},{10,11... | collective-permute-start | bytes 3538952 | tf_op jit(solution)/shard_map/ppermute | solution.py:177
  108.6 0.0 copy-done.2
  108.6 0.4 fusion.9
  109.0 0.4 fusion.11
  109.5 0.6 fusion
  110.1 1.3 %collective-permute-done.4 = f32[192,1536]{1,0:T(8,128)} collective-permute-done((f32[192,1536]{1,0:T(8,128)}, f32[192,1536]{1,0:T(8,128)}, u32[]{:S(2)}, u32[]{:S(2)}) %collective-permute-start.4) | collective-permute-done | bytes 1179680 | tf_op jit(solution)/shard_map/ppermute | solution.py:177
  111.4 2.3 %fusion.2 = bf16[1,1,1,1,192,1536]{5,4,3,2,1,0:T(8,128)(2,1)} fusion(f32[192,1536]{1,0:T(8,128)S(1)} %fusion, f32[192,1536]{1,0:T(8,128)} %collective-permute-done.4, f32[1536]{0:T(1024)S(1)} %reduce), kind=kLoop, calls=%fused_computation.5 | loop fusion | flops 884736 | bytes 2955264 | tf_op jit(solution)/shard_map/reshape | solution.py:181
  (3 shorter events, 0.1 us)
Async XLA Ops:
  2.0 23.1 %copy-start.4 = (s32[3]{0:T(128)S(1)}, s32[3]{0:T(128)}, u32[]{:S(2)}) copy-start(s32[3]{0:T(128)} %constant.69.clone) | copy-start | bytes 40
  2.0 23.1 %copy-start.3 = (s32[1,1,1,1,3]{4,3,2,1,0:T(1,128)S(1)}, s32[1,1,1,1,3]{4,3,2,1,0:T(1,128)}, u32[]{:S(2)}) copy-start(s32[1,1,1,1,3]{4,3,2,1,0:T(1,128)} %param.8) | copy-start | bytes 40
  2.0 72.2 %all-to-all-start = ((bf16[12,32,1536]{2,1,0:T(8,128)(2,1)}), bf16[12,32,1536]{2,1,0:T(8,128)(2,1)S(1)}, u32[]{:S(2)}, u32[]{:S(2)}) async-start(bf16[12,32,1536]{2,1,0:T(8,128)(2,1)} %broadcast_in_dim.2), calls=%async_computation | async-start | bytes 2359296 | tf_op jit(solution)/shard_map/all_to_all | solution.py:134
  17.1 57.1 %collective-permute-start.1 = (bf16[384,2,768]{2,1,0:T(2,128)(2,1)}, bf16[384,2,768]{2,1,0:T(2,128)(2,1)S(1)}, u32[]{:S(2)}, u32[]{:S(2)}) collective-permute-start(bf16[384,2,768]{2,1,0:T(2,128)(2,1)} %bitcast.7.kv_ref), channel_id=1, source_target_pairs={{2,0},{4,2},{6,4},{8,6},{10,8},{12,10},{14,12},{16,14},{18,16},{20... | collective-permute-start | bytes 3538952 | tf_op jit(solution)/shard_map/ppermute | solution.py:130
  23.2 51.0 %collective-permute-start = (bf16[384,2,768]{2,1,0:T(2,128)(2,1)}, bf16[384,2,768]{2,1,0:T(2,128)(2,1)S(1)}, u32[]{:S(2)}, u32[]{:S(2)}) collective-permute-start(bf16[384,2,768]{2,1,0:T(2,128)(2,1)} %bitcast.7.kv_ref), channel_id=1, source_target_pairs={{0,2},{2,4},{4,6},{6,8},{8,10},{10,12},{12,14},{14,16},{16,18},{18... | collective-permute-start | bytes 3538952 | tf_op jit(solution)/shard_map/ppermute | solution.py:129
  74.2 1.4 %copy-start = (bf16[384,2,768]{2,1,0:T(2,128)(2,1)}, bf16[384,2,768]{2,1,0:T(2,128)(2,1)S(1)}, u32[]{:S(2)}) copy-start(bf16[384,2,768]{2,1,0:T(2,128)(2,1)S(1)} %collective-permute-done.1.kvn_ref) | copy-start | bytes 3538948
  74.2 1.8 %copy-start.1 = (bf16[384,2,768]{2,1,0:T(2,128)(2,1)}, bf16[384,2,768]{2,1,0:T(2,128)(2,1)S(1)}, u32[]{:S(2)}) copy-start(bf16[384,2,768]{2,1,0:T(2,128)(2,1)S(1)} %collective-permute-done.kvp_ref) | copy-start | bytes 3538948
  76.0 24.5 %collective-permute-start.2 = (bf16[192,1536]{1,0:T(8,128)(2,1)}, bf16[192,1536]{1,0:T(8,128)(2,1)S(1)}, u32[]{:S(2)}, u32[]{:S(2)}) collective-permute-start(bf16[192,1536]{1,0:T(8,128)(2,1)} %get-tuple-element.25), channel_id=1, source_target_pairs={{0,32},{32,2},{2,34},{34,4},{4,36},{36,6},{6,38},{38,0},{1,33},{33... | collective-permute-start | bytes 1769480 | tf_op jit(solution)/shard_map/ppermute | solution.py:155
  84.1 16.8 %collective-permute-start.3 = (bf16[192,1536]{1,0:T(8,128)(2,1)}, bf16[192,1536]{1,0:T(8,128)(2,1)S(1)}, u32[]{:S(2)}, u32[]{:S(2)}) collective-permute-start(bf16[192,1536]{1,0:T(8,128)(2,1)} %get-tuple-element.26), channel_id=1, source_target_pairs={{0,38},{32,0},{2,32},{34,2},{4,34},{36,4},{6,36},{38,6},{1,39},{33... | collective-permute-start | bytes 1769480 | tf_op jit(solution)/shard_map/ppermute | solution.py:156
  101.4 7.2 %copy-start.2 = (f32[1,1536]{1,0:T(1,128)S(1)}, f32[1,1536]{1,0:T(1,128)}, u32[]{:S(2)}) copy-start(f32[1,1536]{1,0:T(1,128)} %param.10) | copy-start | bytes 18436
  103.0 8.4 %collective-permute-start.4 = (f32[192,1536]{1,0:T(8,128)}, f32[192,1536]{1,0:T(8,128)}, u32[]{:S(2)}, u32[]{:S(2)}) collective-permute-start(f32[192,1536]{1,0:T(8,128)} %fusion.1), channel_id=1, source_target_pairs={{0,1},{1,0},{2,3},{3,2},{4,5},{5,4},{6,7},{7,6},{8,9},{9,8},{10,11... | collective-permute-start | bytes 3538952 | tf_op jit(solution)/shard_map/ppermute | solution.py:177

commit v6 on v5

--- a/solution.py
+++ b/solution.py
@@ -14,7 +14,6 @@
 DP = ("z", "ylo")
 TM = ("x", "yhi")
 ROWS = "core"
-Y = ("ylo", "yhi")
 
 
 def scores_of(q, kv_ref, live):
@@ -105,33 +104,27 @@
     )(flags, q, kv_prev, kv_next, m_c, l_c, acc_c)
 
 
-def gather_direct(piece, axis):
-    count = lax.axis_size(axis)
-    here = lax.axis_index(axis)
-    rows = piece.shape[0]
-    whole = jnp.zeros((count * rows,) + piece.shape[1:], piece.dtype)
-    whole = lax.dynamic_update_slice_in_dim(whole, piece, here * rows, axis=0)
-    for shift in range(1, count):
-        moved = lax.ppermute(piece, axis, [(i, (i + shift) % count) for i in range(count)])
-        at = (here - shift + count) % count
-        whole = lax.dynamic_update_slice_in_dim(whole, moved, at * rows, axis=0)
-    return whole
-
-
 def local(queries, keys_values, window_offsets, out_weight, gate):
     tl = queries.shape[4]
     all_time = lax.axis_size(TM)
     time_now = lax.axis_index(TM)
 
+    pair = lax.ppermute(out_weight, "ylo", [(0, 1), (1, 0)])
+    low = lax.axis_index("ylo") == 0
+    both = jnp.concatenate(
+        [jnp.where(low, out_weight, pair), jnp.where(low, pair, out_weight)], axis=0
+    )
+    kv = keys_values[0, 0, 0, 0]
+    kv, both = lax.optimization_barrier((kv, both))
+
     forward = [(i, i + 1) for i in range(all_time - 1)]
     backward = [(i + 1, i) for i in range(all_time - 1)]
-    kv = keys_values[0, 0, 0, 0]
     kv_prev = lax.ppermute(kv, TM, forward)
     kv_next = lax.ppermute(kv, TM, backward)
 
     zs = lax.axis_size("z")
-    spread = jnp.broadcast_to(out_weight[None], (zs,) + out_weight.shape)
-    own_rows = lax.all_to_all(spread, "z", 0, 0, tiled=True).reshape(-1, out_weight.shape[1])
+    spread = jnp.broadcast_to(both[None], (zs,) + both.shape)
+    head_rows = lax.all_to_all(spread, "z", 0, 0, tiled=True).reshape(-1, both.shape[1])
 
     offsets = window_offsets[0, 0, 0, 0]
     near_t = time_now + offsets // 9 - 1
@@ -141,41 +134,20 @@
     hit = inside[None, :] & (near_t[None, :] == time_now + deltas[:, None])
     flags = jnp.any(hit, axis=1).astype(jnp.int32)
 
-    ys = lax.axis_size(Y)
-    his = lax.axis_size("yhi")
-    slot = [(y % 2) * his + y // 2 for y in range(ys)]
-    up = [(slot[y], slot[(y + 1) % ys]) for y in range(ys)]
-    down = [(slot[y], slot[(y - 1) % ys]) for y in range(ys)]
-    half = own_rows.shape[0] // 2
     q = queries[0, 0, 0, 0]
     centre = attend_centre(flags, q, kv)
-    own_rows, kv_prev, kv_next, centre = lax.optimization_barrier(
-        (own_rows, kv_prev, kv_next, centre)
-    )
-    from_below = lax.ppermute(own_rows[:half], Y, up)
-    from_above = lax.ppermute(own_rows[half:], Y, down)
-
+    kv_prev, kv_next, centre = lax.optimization_barrier((kv_prev, kv_next, centre))
     attended = attend_sides(flags, q, kv_prev, kv_next, *centre)
-
-    parity = lax.axis_index("ylo")
-    split = attended.reshape(tl, zs, 2, -1)
-    a_own = lax.dynamic_index_in_dim(split, parity, axis=2, keepdims=False).reshape(tl, -1)
-    a_other = lax.dynamic_index_in_dim(split, 1 - parity, axis=2, keepdims=False).reshape(tl, -1)
 
     bands = lax.axis_size(ROWS)
     band = tl // bands
     me = lax.axis_index(ROWS)
-
-    def project(start):
-        own = lax.dynamic_slice_in_dim(a_own, start, band, axis=0)
-        far = lax.dynamic_slice_in_dim(a_other, start, band, axis=0)
-        part = jnp.dot(own, own_rows, preferred_element_type=jnp.float32)
-        part = part + jnp.dot(far[:, :half], from_below, preferred_element_type=jnp.float32)
-        return part + jnp.dot(far[:, half:], from_above, preferred_element_type=jnp.float32)
-
-    sent = project((1 - me) * band)
+    mine_rows = lax.dynamic_slice_in_dim(attended, me * band, band, axis=0)
+    other_rows = lax.dynamic_slice_in_dim(attended, (1 - me) * band, band, axis=0)
+    sent = jnp.dot(other_rows, head_rows, preferred_element_type=jnp.float32)
     got = lax.ppermute(sent, ROWS, [(0, 1), (1, 0)])
-    kept = lax.optimization_barrier(project(me * band))
+    kept = jnp.dot(mine_rows, head_rows, preferred_element_type=jnp.float32)
+    kept = lax.optimization_barrier(kept)
     projection = kept + got
     mixed = (gate[0][None, :] * projection).astype(jnp.bfloat16)
     return mixed.reshape(1, 1, 1, 1, band, DOUT)

time: 114 us -> 118 us (1.035)
  the two profiles are of different devices: /device:TPU:7 before, /device:TPU:1 now
where the time goes in v6:
time: 118 us; the launch traced here: 117 us
  waiting for transfers between devices  52.4 us (44%)
  starting transfers between devices  34.2 us (29%)
  Pallas kernels  21.4 us (18%)
  other arithmetic  4 us (3%)
  matrix products  3.32 us (3%)
  local copies, waits for them, and re-layouts  1.64 us (1%)
    ppermute x1, waiting for transfers between devices, local(): kv_prev = lax.ppermute(kv, TM, forward)  28.7 us
    ppermute x1, waiting for transfers between devices, local(): kv_next = lax.ppermute(kv, TM, backward)  18.1 us
    all_to_all x1, starting transfers between devices, local(): lax.all_to_all(spread, 'z', 0, 0, tiled=True).reshape(-1, both.shape[1])  15.2 us
    pallas_call x1, Pallas kernels, attend_sides(): pl.pallas_call(side_kernel, grid_spec=pltpu.PrefetchScalarGridSpec(num_sc...  13 us
    ppermute x1, starting transfers between devices, local(): got = lax.ppermute(sent, ROWS, [(0, 1), (1, 0)])  9.42 us
    pallas_call x1, Pallas kernels, attend_centre(): pl.pallas_call(centre_kernel, grid_spec=pltpu.PrefetchScalarGridSpec(num_...  8.37 us
    ppermute x1, starting transfers between devices, local(): kv_prev = lax.ppermute(kv, TM, forward)  4.29 us
    ppermute x1, starting transfers between devices, local(): pair = lax.ppermute(out_weight, 'ylo', [(0, 1), (1, 0)])  4.02 us
  transfers between devices with their start and end apart: 5, of which 5 were waited for; matrix products, arithmetic and copies ran while one was open for 1% of the time, Pallas kernels for 18%

profile of v6, /device:TPU:1, one launch (start us, length us, event | category | flops | bytes accessed | tf_op | source)
XLA Modules:
  0.0 117.0 jit_solution(16090419191849732171)
XLA Ops:
  0.0 4.0 %collective-permute-start = (bf16[32,1536]{1,0:T(8,128)(2,1)}, bf16[32,1536]{1,0:T(8,128)(2,1)S(1)}, u32[]{:S(2)}, u32[]{:S(2)}) collective-permute-start(bf16[32,1536]{1,0:T(8,128)(2,1)} %param.9), channel_id=1, source_target_pairs={{0,32},{32,0},{1,33},{33,1},{2,34},{34,2},{3,35},{35,3},{4,36},{36... | collective-permute-start | bytes 294920 | tf_op jit(solution)/shard_map/ppermute | solution.py:112
  4.0 2.2 %collective-permute-done = bf16[32,1536]{1,0:T(8,128)(2,1)S(1)} collective-permute-done((bf16[32,1536]{1,0:T(8,128)(2,1)}, bf16[32,1536]{1,0:T(8,128)(2,1)S(1)}, u32[]{:S(2)}, u32[]{:S(2)}) %collective-permute-start) | collective-permute-done | bytes 98336 | tf_op jit(solution)/shard_map/ppermute | solution.py:112
  6.2 0.9 broadcast_select_fusion.1
  7.2 1.6 %broadcast_in_dim.2 = bf16[12,64,1536]{2,1,0:T(8,128)(2,1)} broadcast(bf16[64,1536]{1,0:T(8,128)(2,1)S(1)} %pad_maximum_fusion), dimensions={1,2} | broadcast | bytes 2555904 | tf_op jit(solution)/shard_map/broadcast_in_dim | solution.py:126
  8.8 0.0 copy-start.4
  8.8 0.0 copy-start.3
  8.8 15.2 %all-to-all-start = ((bf16[12,64,1536]{2,1,0:T(8,128)(2,1)}), bf16[12,64,1536]{2,1,0:T(8,128)(2,1)S(1)}, u32[]{:S(2)}, u32[]{:S(2)}) async-start(bf16[12,64,1536]{2,1,0:T(8,128)(2,1)} %broadcast_in_dim.2), calls=%async_computation | async-start | bytes 4718592 | tf_op jit(solution)/shard_map/all_to_all | solution.py:127
  24.0 4.3 %collective-permute-start.1 = (bf16[384,2,768]{2,1,0:T(2,128)(2,1)}, bf16[384,2,768]{2,1,0:T(2,128)(2,1)S(1)}, u32[]{:S(2)}, u32[]{:S(2)}) collective-permute-start(bf16[384,2,768]{2,1,0:T(2,128)(2,1)} %bitcast.42), channel_id=1, source_target_pairs={{0,2},{2,4},{4,6},{6,8},{8,10},{10,12},{12,14},{14,16},{16,18},{18... | collective-permute-start | bytes 3538952 | tf_op jit(solution)/shard_map/ppermute | solution.py:122
  28.3 1.3 %collective-permute-start.2 = (bf16[384,2,768]{2,1,0:T(2,128)(2,1)}, bf16[384,2,768]{2,1,0:T(2,128)(2,1)}, u32[]{:S(2)}, u32[]{:S(2)}) collective-permute-start(bf16[384,2,768]{2,1,0:T(2,128)(2,1)} %bitcast.43), channel_id=1, source_target_pairs={{2,0},{4,2},{6,4},{8,6},{10,8},{12,10},{14,12},{16,14},{18,16},{20... | collective-permute-start | bytes 3538952 | tf_op jit(solution)/shard_map/ppermute | solution.py:123
  29.6 0.0 copy-done.4
  29.6 0.0 copy-done.3
  29.6 0.2 and_reduce_fusion
  29.8 0.5 convert_element_type.6.flags_ref
  30.4 8.4 %shard_map.64 = (f32[6,384,1]{2,1,0:T(8,128)}, f32[6,384,1]{2,1,0:T(8,128)}, f32[384,768]{1,0:T(8,128)}) custom-call(s32[3]{0:T(128)} %convert_element_type.6.flags_ref, bf16[384,768]{1,0:T(8,128)(2,1)} %bitcast.40, bf16[384,2,768]{2,1,0:T(2,128)(2,1)} %bitcast.44), custom_call_target="tpu_custom_call" | custom-call | flops 452984832 | bytes 2949120 | tf_op jit(solution)/shard_map/pallas_call | solution.py:65
  38.7 28.7 %collective-permute-done.1.kvp_ref = bf16[384,2,768]{2,1,0:T(2,128)(2,1)S(1)} collective-permute-done((bf16[384,2,768]{2,1,0:T(2,128)(2,1)}, bf16[384,2,768]{2,1,0:T(2,128)(2,1)S(1)}, u32[]{:S(2)}, u32[]{:S(2)}) %collective-permute-start.1) | collective-permute-done | bytes 1179680 | tf_op jit(solution)/shard_map/ppermute | solution.py:122
  67.5 0.0 copy-start.1
  67.5 18.1 %collective-permute-done.2.kvn_ref = bf16[384,2,768]{2,1,0:T(2,128)(2,1)} collective-permute-done((bf16[384,2,768]{2,1,0:T(2,128)(2,1)}, bf16[384,2,768]{2,1,0:T(2,128)(2,1)}, u32[]{:S(2)}, u32[]{:S(2)}) %collective-permute-start.2) | collective-permute-done | bytes 1179680 | tf_op jit(solution)/shard_map/ppermute | solution.py:123
  85.5 0.0 copy-done.1
  85.5 13.0 %shard_map.65 = bf16[384,768]{1,0:T(8,128)(2,1)} custom-call(s32[3]{0:T(128)} %convert_element_type.6.flags_ref, bf16[384,768]{1,0:T(8,128)(2,1)} %bitcast.41, bf16[384,2,768]{2,1,0:T(2,128)(2,1)} %copy-done.1, bf16[384,2,768]{2,1,0:T(2,128)(2,1)} %collective-permute-done.2.kvn_ref, f32[6,384,1]{2,1,0:T(8,128)} %get-tuple-element.21.m_ref, ...), custom_call_target="tpu_custom_call" | custom-call | flops 905969664 | bytes 4718592 | tf_op jit(solution)/shard_map/pallas_call | solution.py:90
  98.5 1.3 %all-to-all-done = bf16[12,64,1536]{2,1,0:T(8,128)(2,1)S(1)} async-done(((bf16[12,64,1536]{2,1,0:T(8,128)(2,1)}), bf16[12,64,1536]{2,1,0:T(8,128)(2,1)S(1)}, u32[]{:S(2)}, u32[]{:S(2)}) %all-to-all-start) | async-done | bytes 2359328 | tf_op jit(solution)/shard_map/all_to_all | solution.py:127
  99.8 0.0 copy-start.2
  99.8 0.0 copy-start
  99.8 2.7 %fusion.1 = f32[192,1536]{1,0:T(8,128)} fusion(bf16[768,1536]{1,0:T(8,128)(2,1)S(1)} %bitcast.38, bf16[384,768]{1,0:T(8,128)(2,1)} %shard_map.65, s32[]{:T(128)S(6)} %select_n.64), kind=kOutput, calls=%fused_computation.2 | convolution fusion | flops 452984832 | bytes 3833860 | tf_op jit(solution)/shard_map/dot_general | solution.py:147
  102.5 9.4 %collective-permute-start.3 = (f32[192,1536]{1,0:T(8,128)}, f32[192,1536]{1,0:T(8,128)}, u32[]{:S(2)}, u32[]{:S(2)}) collective-permute-start(f32[192,1536]{1,0:T(8,128)} %fusion.1), channel_id=1, source_target_pairs={{0,1},{1,0},{2,3},{3,2},{4,5},{5,4},{6,7},{7,6},{8,9},{9,8},{10,11... | collective-permute-start | bytes 3538952 | tf_op jit(solution)/shard_map/ppermute | solution.py:148
  111.9 0.0 copy-done.2
  112.0 0.0 copy-done
  112.0 0.6 fusion.3
  112.6 2.1 %collective-permute-done.3 = f32[192,1536]{1,0:T(8,128)} collective-permute-done((f32[192,1536]{1,0:T(8,128)}, f32[192,1536]{1,0:T(8,128)}, u32[]{:S(2)}, u32[]{:S(2)}) %collective-permute-start.3) | collective-permute-done | bytes 1179680 | tf_op jit(solution)/shard_map/ppermute | solution.py:148
  114.7 2.3 %fusion = bf16[1,1,1,1,192,1536]{5,4,3,2,1,0:T(8,128)(2,1)} fusion(f32[192,1536]{1,0:T(8,128)S(1)} %fusion.3, f32[192,1536]{1,0:T(8,128)} %collective-permute-done.3, f32[1536]{0:T(1024)S(1)} %reduce), kind=kLoop, calls=%fused_computation.1 | loop fusion | flops 884736 | bytes 2955264 | tf_op jit(solution)/shard_map/reshape | solution.py:153
  (4 shorter events, 0.1 us)
Async XLA Ops:
  0.0 6.2 %collective-permute-start = (bf16[32,1536]{1,0:T(8,128)(2,1)}, bf16[32,1536]{1,0:T(8,128)(2,1)S(1)}, u32[]{:S(2)}, u32[]{:S(2)}) collective-permute-start(bf16[32,1536]{1,0:T(8,128)(2,1)} %param.9), channel_id=1, source_target_pairs={{0,32},{32,0},{1,33},{33,1},{2,34},{34,2},{3,35},{35,3},{4,36},{36... | collective-permute-start | bytes 294920 | tf_op jit(solution)/shard_map/ppermute | solution.py:112
  8.8 20.8 %copy-start.4 = (s32[3]{0:T(128)S(1)}, s32[3]{0:T(128)}, u32[]{:S(2)}) copy-start(s32[3]{0:T(128)} %constant.61.clone) | copy-start | bytes 40
  8.8 20.8 %copy-start.3 = (s32[1,1,1,1,3]{4,3,2,1,0:T(1,128)S(1)}, s32[1,1,1,1,3]{4,3,2,1,0:T(1,128)}, u32[]{:S(2)}) copy-start(s32[1,1,1,1,3]{4,3,2,1,0:T(1,128)} %param.8) | copy-start | bytes 40
  8.8 91.0 %all-to-all-start = ((bf16[12,64,1536]{2,1,0:T(8,128)(2,1)}), bf16[12,64,1536]{2,1,0:T(8,128)(2,1)S(1)}, u32[]{:S(2)}, u32[]{:S(2)}) async-start(bf16[12,64,1536]{2,1,0:T(8,128)(2,1)} %broadcast_in_dim.2), calls=%async_computation | async-start | bytes 4718592 | tf_op jit(solution)/shard_map/all_to_all | solution.py:127
  24.0 43.5 %collective-permute-start.1 = (bf16[384,2,768]{2,1,0:T(2,128)(2,1)}, bf16[384,2,768]{2,1,0:T(2,128)(2,1)S(1)}, u32[]{:S(2)}, u32[]{:S(2)}) collective-permute-start(bf16[384,2,768]{2,1,0:T(2,128)(2,1)} %bitcast.42), channel_id=1, source_target_pairs={{0,2},{2,4},{4,6},{6,8},{8,10},{10,12},{12,14},{14,16},{16,18},{18... | collective-permute-start | bytes 3538952 | tf_op jit(solution)/shard_map/ppermute | solution.py:122
  28.3 57.3 %collective-permute-start.2 = (bf16[384,2,768]{2,1,0:T(2,128)(2,1)}, bf16[384,2,768]{2,1,0:T(2,128)(2,1)}, u32[]{:S(2)}, u32[]{:S(2)}) collective-permute-start(bf16[384,2,768]{2,1,0:T(2,128)(2,1)} %bitcast.43), channel_id=1, source_target_pairs={{2,0},{4,2},{6,4},{8,6},{10,8},{12,10},{14,12},{16,14},{18,16},{20... | collective-permute-start | bytes 3538952 | tf_op jit(solution)/shard_map/ppermute | solution.py:123
  67.5 18.1 %copy-start.1 = (bf16[384,2,768]{2,1,0:T(2,128)(2,1)}, bf16[384,2,768]{2,1,0:T(2,128)(2,1)S(1)}, u32[]{:S(2)}) copy-start(bf16[384,2,768]{2,1,0:T(2,128)(2,1)S(1)} %collective-permute-done.1.kvp_ref) | copy-start | bytes 3538948
  99.8 12.1 %copy-start.2 = (f32[1,1536]{1,0:T(1,128)S(1)}, f32[1,1536]{1,0:T(1,128)}, u32[]{:S(2)}) copy-start(f32[1,1536]{1,0:T(1,128)} %param.10) | copy-start | bytes 18436
  99.8 12.2 %copy-start = (bf16[384,768]{1,0:T(8,128)(2,1)S(1)}, bf16[384,768]{1,0:T(8,128)(2,1)}, u32[]{:S(2)}) copy-start(bf16[384,768]{1,0:T(8,128)(2,1)} %shard_map.65) | copy-start | bytes 1769476
  102.5 12.2 %collective-permute-start.3 = (f32[192,1536]{1,0:T(8,128)}, f32[192,1536]{1,0:T(8,128)}, u32[]{:S(2)}, u32[]{:S(2)}) collective-permute-start(f32[192,1536]{1,0:T(8,128)} %fusion.1), channel_id=1, source_target_pairs={{0,1},{1,0},{2,3},{3,2},{4,5},{5,4},{6,7},{7,6},{8,9},{9,8},{10,11... | collective-permute-start | bytes 3538952 | tf_op jit(solution)/shard_map/ppermute | solution.py:148

commit v7 on v5

--- a/solution.py
+++ b/solution.py
@@ -17,30 +17,30 @@
 Y = ("ylo", "yhi")
 
 
-def scores_of(q, kv_ref, live):
+def scores_of(q, k_ref, live):
     scale = float(HD) ** (-0.5)
     s = lax.dot_general(
-        q, kv_ref[:, 0, :], (((1,), (1,)), ((), ())), preferred_element_type=jnp.float32
+        q, k_ref[...], (((1,), (1,)), ((), ())), preferred_element_type=jnp.float32
     ) * scale
     return jnp.where(live, s, -jnp.inf)
 
 
-def centre_kernel(flags_ref, q_ref, kv_ref, m_ref, l_ref, acc_ref):
+def centre_kernel(flags_ref, q_ref, k_ref, v_ref, m_ref, l_ref, acc_ref):
     live = flags_ref[1] > 0
-    s = scores_of(q_ref[...], kv_ref, live)
+    s = scores_of(q_ref[...], k_ref, live)
     top = jnp.max(s, axis=1, keepdims=True)
     p = jnp.where(live, jnp.exp(s - top), 0.0)
     m_ref[0] = jnp.where(live, top, -jnp.inf)
     l_ref[0] = p.sum(axis=1, keepdims=True)
     acc_ref[...] = jnp.dot(
-        p.astype(jnp.bfloat16), kv_ref[:, 1, :], preferred_element_type=jnp.float32
-    )
-
-
-def side_kernel(flags_ref, q_ref, kvp_ref, kvn_ref, m_ref, l_ref, acc_ref, o_ref):
+        p.astype(jnp.bfloat16), v_ref[...], preferred_element_type=jnp.float32
+    )
+
+
+def side_kernel(flags_ref, q_ref, kp_ref, vp_ref, kn_ref, vn_ref, m_ref, l_ref, acc_ref, o_ref):
     q = q_ref[...]
-    s_p = scores_of(q, kvp_ref, flags_ref[0] > 0)
-    s_n = scores_of(q, kvn_ref, flags_ref[2] > 0)
+    s_p = scores_of(q, kp_ref, flags_ref[0] > 0)
+    s_n = scores_of(q, kn_ref, flags_ref[2] > 0)
     m_c = m_ref[0]
     top = jnp.maximum(
         m_c, jnp.maximum(jnp.max(s_p, axis=1, keepdims=True), jnp.max(s_n, axis=1, keepdims=True))
@@ -50,15 +50,33 @@
     p_n = jnp.exp(s_n - top)
     total = alpha * l_ref[0] + p_p.sum(axis=1, keepdims=True) + p_n.sum(axis=1, keepdims=True)
     acc = alpha * acc_ref[...]
-    acc = acc + jnp.dot(p_p.astype(jnp.bfloat16), kvp_ref[:, 1, :], preferred_element_type=jnp.float32)
-    acc = acc + jnp.dot(p_n.astype(jnp.bfloat16), kvn_ref[:, 1, :], preferred_element_type=jnp.float32)
+    acc = acc + jnp.dot(p_p.astype(jnp.bfloat16), vp_ref[...], preferred_element_type=jnp.float32)
+    acc = acc + jnp.dot(p_n.astype(jnp.bfloat16), vn_ref[...], preferred_element_type=jnp.float32)
     o_ref[...] = (acc / total).astype(o_ref.dtype)
+
+
+def split_kernel(kv_ref, o_ref):
+    o_ref[0] = kv_ref[:, 0, :]
+    o_ref[1] = kv_ref[:, 1, :]
+
+
+def split_keys_values(kv):
+    tl, _, width = kv.shape
+    return pl.pallas_call(
+        split_kernel,
+        grid=(width // HD,),
+        in_specs=[pl.BlockSpec((tl, 2, HD), lambda h: (0, 0, h))],
+        out_specs=pl.BlockSpec((2, tl, HD), lambda h: (0, 0, h)),
+        out_shape=jax.ShapeDtypeStruct((2, tl, width), kv.dtype),
+        cost_estimate=pl.CostEstimate(flops=0, transcendentals=0, bytes_accessed=4 * tl * width * 2),
+    )(kv)
 
 
 def attend_centre(flags, q, kv_own):
     tl, width = q.shape
     heads = width // HD
-    kv_spec = pl.BlockSpec((tl, 2, HD), lambda h, f: (0, 0, h))
+    k_spec = pl.BlockSpec((None, tl, HD), lambda h, f: (0, 0, h))
+    v_spec = pl.BlockSpec((None, tl, HD), lambda h, f: (1, 0, h))
     q_spec = pl.BlockSpec((tl, HD), lambda h, f: (0, h))
     stat_spec = pl.BlockSpec((1, tl, 1), lambda h, f: (h, 0, 0))
     stat_shape = jax.ShapeDtypeStruct((heads, tl, 1), jnp.float32)
@@ -68,7 +86,7 @@
         grid_spec=pltpu.PrefetchScalarGridSpec(
             num_scalar_prefetch=1,
             grid=(heads,),
-            in_specs=[q_spec, kv_spec],
+            in_specs=[q_spec, k_spec, v_spec],
             out_specs=[stat_spec, stat_spec, q_spec],
         ),
         out_shape=[stat_shape, stat_shape, jax.ShapeDtypeStruct((tl, width), jnp.float32)],
@@ -77,14 +95,15 @@
             transcendentals=heads * tl * tl,
             bytes_accessed=tl * width * 2 * 3 + tl * width * 4,
         ),
-    )(flags, q, kv_own)
+    )(flags, q, kv_own, kv_own)
     return m_c, l_c, acc_c
 
 
 def attend_sides(flags, q, kv_prev, kv_next, m_c, l_c, acc_c):
     tl, width = q.shape
     heads = width // HD
-    kv_spec = pl.BlockSpec((tl, 2, HD), lambda h, f: (0, 0, h))
+    k_spec = pl.BlockSpec((None, tl, HD), lambda h, f: (0, 0, h))
+    v_spec = pl.BlockSpec((None, tl, HD), lambda h, f: (1, 0, h))
     q_spec = pl.BlockSpec((tl, HD), lambda h, f: (0, h))
     stat_spec = pl.BlockSpec((1, tl, 1), lambda h, f: (h, 0, 0))
     tile_flops = heads * 2 * 2 * tl * tl * HD
@@ -93,7 +112,7 @@
         grid_spec=pltpu.PrefetchScalarGridSpec(
             num_scalar_prefetch=1,
             grid=(heads,),
-            in_specs=[q_spec, kv_spec, kv_spec, stat_spec, stat_spec, q_spec],
+            in_specs=[q_spec, k_spec, v_spec, k_spec, v_spec, stat_spec, stat_spec, q_spec],
             out_specs=q_spec,
         ),
         out_shape=jax.ShapeDtypeStruct((tl, width), jnp.bfloat16),
@@ -102,20 +121,7 @@
             transcendentals=2 * heads * tl * tl,
             bytes_accessed=tl * width * 2 * 6 + tl * width * 4,
         ),
-    )(flags, q, kv_prev, kv_next, m_c, l_c, acc_c)
-
-
-def gather_direct(piece, axis):
-    count = lax.axis_size(axis)
-    here = lax.axis_index(axis)
-    rows = piece.shape[0]
-    whole = jnp.zeros((count * rows,) + piece.shape[1:], piece.dtype)
-    whole = lax.dynamic_update_slice_in_dim(whole, piece, here * rows, axis=0)
-    for shift in range(1, count):
-        moved = lax.ppermute(piece, axis, [(i, (i + shift) % count) for i in range(count)])
-        at = (here - shift + count) % count
-        whole = lax.dynamic_update_slice_in_dim(whole, moved, at * rows, axis=0)
-    return whole
+    )(flags, q, kv_prev, kv_prev, kv_next, kv_next, m_c, l_c, acc_c)
 
 
 def local(queries, keys_values, window_offsets, out_weight, gate):
@@ -125,7 +131,7 @@
 
     forward = [(i, i + 1) for i in range(all_time - 1)]
     backward = [(i + 1, i) for i in range(all_time - 1)]
-    kv = keys_values[0, 0, 0, 0]
+    kv = split_keys_values(keys_values[0, 0, 0, 0])
     kv_prev = lax.ppermute(kv, TM, forward)
     kv_next = lax.ppermute(kv, TM, backward)
 

time: 114 us -> 118 us (1.035)
  the two profiles are of different devices: /device:TPU:7 before, /device:TPU:1 now
where the time goes in v7:
time: 118 us; the launch traced here: 117 us
  waiting for transfers between devices  52.4 us (44%)
  starting transfers between devices  31.1 us (26%)
  Pallas kernels  21.4 us (18%)
  local copies, waits for them, and re-layouts  4.97 us (4%)
  matrix products  3.88 us (3%)
  other arithmetic  3.07 us (3%)
    ppermute x1, waiting for transfers between devices, local(): kv_prev = lax.ppermute(kv, TM, forward)  32.6 us
    all_to_all x1, starting transfers between devices, local(): lax.all_to_all(spread, 'z', 0, 0, tiled=True)  15.7 us
    ppermute x1, waiting for transfers between devices, local(): kv_next = lax.ppermute(kv, TM, backward)  15.6 us
    pallas_call x1, Pallas kernels, attend_sides(): pl.pallas_call(side_kernel, grid_spec=pltpu.PrefetchScalarGridSpec(num_sc...  8.67 us
    pallas_call x1, Pallas kernels, attend_centre(): pl.pallas_call(centre_kernel, grid_spec=pltpu.PrefetchScalarGridSpec(num_...  6.78 us
    pallas_call x1, Pallas kernels, split_keys_values(): pl.pallas_call(split_kernel, grid=(width // HD,), in_specs=[pl.BlockSpec(...  5.96 us
    ppermute x1, starting transfers between devices, local(): from_above = lax.ppermute(own_rows[half:], Y, down)  4.57 us
    ppermute x1, starting transfers between devices, local(): kv_prev = lax.ppermute(kv, TM, forward)  4.28 us
  transfers between devices with their start and end apart: 6, of which 5 were waited for; matrix products, arithmetic and copies ran while one was open for 3% of the time, Pallas kernels for 18%

profile of v7, /device:TPU:1, one launch (start us, length us, event | category | flops | bytes accessed | tf_op | source)
XLA Modules:
  0.0 117.0 jit_solution(10318637451925899319)
XLA Ops:
  0.0 2.1 %broadcast_in_dim.2 = bf16[12,32,1536]{2,1,0:T(8,128)(2,1)} broadcast(bf16[32,1536]{1,0:T(8,128)(2,1)} %param.9), dimensions={1,2} | broadcast | bytes 1277952 | tf_op jit(solution)/shard_map/broadcast_in_dim | solution.py:139
  2.1 15.7 %all-to-all-start = ((bf16[12,32,1536]{2,1,0:T(8,128)(2,1)}), bf16[12,32,1536]{2,1,0:T(8,128)(2,1)S(1)}, u32[]{:S(2)}, u32[]{:S(2)}) async-start(bf16[12,32,1536]{2,1,0:T(8,128)(2,1)} %broadcast_in_dim.2), calls=%async_computation | async-start | bytes 2359296 | tf_op jit(solution)/shard_map/all_to_all | solution.py:140
  17.8 0.0 copy-start.4
  17.8 0.0 copy-start.3
  17.8 6.0 %shard_map.64.k_ref.v_ref = bf16[2,384,768]{2,1,0:T(8,128)(2,1)} custom-call(bf16[384,2,768]{2,1,0:T(2,128)(2,1)} %bitcast.57), custom_call_target="tpu_custom_call" | custom-call | bytes 2359296 | tf_op jit(solution)/shard_map/pallas_call | solution.py:65
  23.8 4.3 %collective-permute-start = (bf16[2,384,768]{2,1,0:T(8,128)(2,1)}, bf16[2,384,768]{2,1,0:T(8,128)(2,1)S(1)}, u32[]{:S(2)}, u32[]{:S(2)}) collective-permute-start(bf16[2,384,768]{2,1,0:T(8,128)(2,1)} %shard_map.64.k_ref.v_ref), channel_id=1, source_target_pairs={{0,2},{2,4},{4,6},{6,8},{8,10},{10,12},{12,14},{14,16},{16,18},{18... | collective-permute-start | bytes 3538952 | tf_op jit(solution)/shard_map/ppermute | solution.py:135
  28.0 1.3 %collective-permute-start.1 = (bf16[2,384,768]{2,1,0:T(8,128)(2,1)}, bf16[2,384,768]{2,1,0:T(8,128)(2,1)S(1)}, u32[]{:S(2)}, u32[]{:S(2)}) collective-permute-start(bf16[2,384,768]{2,1,0:T(8,128)(2,1)} %shard_map.64.k_ref.v_ref), channel_id=1, source_target_pairs={{2,0},{4,2},{6,4},{8,6},{10,8},{12,10},{14,12},{16,14},{18,16},{20... | collective-permute-start | bytes 3538952 | tf_op jit(solution)/shard_map/ppermute | solution.py:136
  29.4 0.0 copy-done.4
  29.4 0.0 copy-done.3
  29.4 0.2 and_reduce_fusion
  29.6 0.5 convert_element_type.6.flags_ref
  30.1 6.8 %shard_map.65 = (f32[6,384,1]{2,1,0:T(8,128)}, f32[6,384,1]{2,1,0:T(8,128)}, f32[384,768]{1,0:T(8,128)}) custom-call(s32[3]{0:T(128)} %convert_element_type.6.flags_ref, bf16[384,768]{1,0:T(8,128)(2,1)} %bitcast.48, bf16[2,384,768]{2,1,0:T(8,128)(2,1)} %shard_map.64.k_ref.v_ref, bf16[2,384,768]{2,1,0:T(8,128)(2,1)} %shard_map.64.k_ref.v_ref), custom_call_target="tpu_custom_call" | custom-call | flops 452984832 | bytes 2949120 | tf_op jit(solution)/shard_map/pallas_call | solution.py:84
  36.9 32.6 %collective-permute-done.kp_ref.vp_ref = bf16[2,384,768]{2,1,0:T(8,128)(2,1)S(1)} collective-permute-done((bf16[2,384,768]{2,1,0:T(8,128)(2,1)}, bf16[2,384,768]{2,1,0:T(8,128)(2,1)S(1)}, u32[]{:S(2)}, u32[]{:S(2)}) %collective-permute-start) | collective-permute-done | bytes 1179680 | tf_op jit(solution)/shard_map/ppermute | solution.py:135
  69.6 0.0 copy-start
  69.6 15.6 %collective-permute-done.1.kn_ref.vn_ref = bf16[2,384,768]{2,1,0:T(8,128)(2,1)S(1)} collective-permute-done((bf16[2,384,768]{2,1,0:T(8,128)(2,1)}, bf16[2,384,768]{2,1,0:T(8,128)(2,1)S(1)}, u32[]{:S(2)}, u32[]{:S(2)}) %collective-permute-start.1) | collective-permute-done | bytes 1179680 | tf_op jit(solution)/shard_map/ppermute | solution.py:136
  85.2 0.0 copy-start.1
  85.2 0.0 all-to-all-done
  85.2 1.2 %fusion.19 = (bf16[192,1536]{1,0:T(8,128)(2,1)}, bf16[192,1536]{1,0:T(8,128)(2,1)}) fusion(bf16[384,1536]{1,0:T(8,128)(2,1)S(1)} %bitcast.45), kind=kLoop, calls=%fused_computation.32 | loop fusion | bytes 2359296 | tf_op jit(solution)/shard_map/slice | solution.py:161
  86.4 0.0 copy-done
  86.4 0.2 copy-done.1
  86.6 1.9 %collective-permute-start.2 = (bf16[192,1536]{1,0:T(8,128)(2,1)}, bf16[192,1536]{1,0:T(8,128)(2,1)S(1)}, u32[]{:S(2)}, u32[]{:S(2)}) collective-permute-start(bf16[192,1536]{1,0:T(8,128)(2,1)} %get-tuple-element.25), channel_id=1, source_target_pairs={{0,32},{32,2},{2,34},{34,4},{4,36},{36,6},{6,38},{38,0},{1,33},{33... | collective-permute-start | bytes 1769480 | tf_op jit(solution)/shard_map/ppermute | solution.py:161
  88.6 4.6 %collective-permute-start.3 = (bf16[192,1536]{1,0:T(8,128)(2,1)}, bf16[192,1536]{1,0:T(8,128)(2,1)S(1)}, u32[]{:S(2)}, u32[]{:S(2)}) collective-permute-start(bf16[192,1536]{1,0:T(8,128)(2,1)} %get-tuple-element.26), channel_id=1, source_target_pairs={{0,38},{32,0},{2,32},{34,2},{4,34},{36,4},{6,36},{38,6},{1,39},{33... | collective-permute-start | bytes 1769480 | tf_op jit(solution)/shard_map/ppermute | solution.py:162
  93.1 8.7 %shard_map.66 = bf16[384,768]{1,0:T(8,128)(2,1)} custom-call(s32[3]{0:T(128)} %convert_element_type.6.flags_ref, bf16[384,768]{1,0:T(8,128)(2,1)} %bitcast.49, bf16[2,384,768]{2,1,0:T(8,128)(2,1)} %copy-done, bf16[2,384,768]{2,1,0:T(8,128)(2,1)} %copy-done, bf16[2,384,768]{2,1,0:T(8,128)(2,1)} %copy-done.1, bf16[2,384,768]{2,1,0:T(8,128)(2,1)} %copy-done.1, ...), custom_call_target="tpu_custom_call" | custom-call | flops 905969664 | bytes 4718592 | tf_op jit(solution)/shard_map/pallas_call | solution.py:110
  101.8 1.4 %copy.8 = bf16[384,768]{0,1:T(8,128)(2,1)S(1)} copy(bf16[384,768]{1,0:T(8,128)(2,1)} %shard_map.66) | data formatting | bytes 1179648 | tf_op jit(solution)/shard_map/pallas_call | solution.py:110
  103.2 0.1 constant_dynamic-slice_fusion.1
  103.3 0.9 collective-permute-done.2
  104.2 0.4 fusion.7
  104.6 1.8 %collective-permute-done.3 = bf16[192,1536]{1,0:T(8,128)(2,1)S(1)} collective-permute-done((bf16[192,1536]{1,0:T(8,128)(2,1)}, bf16[192,1536]{1,0:T(8,128)(2,1)S(1)}, u32[]{:S(2)}, u32[]{:S(2)}) %collective-permute-start.3) | collective-permute-done | bytes 589856 | tf_op jit(solution)/shard_map/ppermute | solution.py:162
  106.5 0.4 fusion.5
  106.9 0.0 copy-start.2
  106.9 1.6 %fusion.1 = f32[192,1536]{1,0:T(8,128)} fusion(f32[192,1536]{1,0:T(8,128)S(1)} %fusion.5, f32[192,1536]{1,0:T(8,128)S(1)} %fusion.7, bf16[384,1536]{1,0:T(8,128)(2,1)S(1)} %bitcast.46, bf16[384,384]{0,1:T(8,128)(2,1)S(1)} %bitcast.51, s32[]{:T(128)S(6)} %select_n.60), kind=kOutput, calls=%fused_computation.3 | convolution fusion | flops 227082240 | bytes 4915204 | tf_op jit(solution)/shard_map/dot_general | solution.py:178
  108.5 3.4 %collective-permute-start.4 = (f32[192,1536]{1,0:T(8,128)}, f32[192,1536]{1,0:T(8,128)}, u32[]{:S(2)}, u32[]{:S(2)}) collective-permute-start(f32[192,1536]{1,0:T(8,128)} %fusion.1), channel_id=1, source_target_pairs={{0,1},{1,0},{2,3},{3,2},{4,5},{5,4},{6,7},{7,6},{8,9},{9,8},{10,11... | collective-permute-start | bytes 3538952 | tf_op jit(solution)/shard_map/ppermute | solution.py:183
  111.9 0.0 copy-done.2
  112.0 0.4 fusion.11
  112.4 0.4 fusion.9
  112.8 0.6 fusion
  113.4 1.3 %collective-permute-done.4 = f32[192,1536]{1,0:T(8,128)} collective-permute-done((f32[192,1536]{1,0:T(8,128)}, f32[192,1536]{1,0:T(8,128)}, u32[]{:S(2)}, u32[]{:S(2)}) %collective-permute-start.4) | collective-permute-done | bytes 1179680 | tf_op jit(solution)/shard_map/ppermute | solution.py:183
  114.7 2.3 %fusion.2 = bf16[1,1,1,1,192,1536]{5,4,3,2,1,0:T(8,128)(2,1)} fusion(f32[192,1536]{1,0:T(8,128)S(1)} %fusion, f32[192,1536]{1,0:T(8,128)} %collective-permute-done.4, f32[1536]{0:T(1024)S(1)} %reduce), kind=kLoop, calls=%fused_computation.5 | loop fusion | flops 884736 | bytes 2955264 | tf_op jit(solution)/shard_map/reshape | solution.py:187
  (3 shorter events, 0.1 us)
Async XLA Ops:
  2.1 83.1 %all-to-all-start = ((bf16[12,32,1536]{2,1,0:T(8,128)(2,1)}), bf16[12,32,1536]{2,1,0:T(8,128)(2,1)S(1)}, u32[]{:S(2)}, u32[]{:S(2)}) async-start(bf16[12,32,1536]{2,1,0:T(8,128)(2,1)} %broadcast_in_dim.2), calls=%async_computation | async-start | bytes 2359296 | tf_op jit(solution)/shard_map/all_to_all | solution.py:140
  17.8 11.6 %copy-start.4 = (s32[3]{0:T(128)S(1)}, s32[3]{0:T(128)}, u32[]{:S(2)}) copy-start(s32[3]{0:T(128)} %constant.69.clone) | copy-start | bytes 40
  17.8 11.6 %copy-start.3 = (s32[1,1,1,1,3]{4,3,2,1,0:T(1,128)S(1)}, s32[1,1,1,1,3]{4,3,2,1,0:T(1,128)}, u32[]{:S(2)}) copy-start(s32[1,1,1,1,3]{4,3,2,1,0:T(1,128)} %param.8) | copy-start | bytes 40
  23.8 45.8 %collective-permute-start = (bf16[2,384,768]{2,1,0:T(8,128)(2,1)}, bf16[2,384,768]{2,1,0:T(8,128)(2,1)S(1)}, u32[]{:S(2)}, u32[]{:S(2)}) collective-permute-start(bf16[2,384,768]{2,1,0:T(8,128)(2,1)} %shard_map.64.k_ref.v_ref), channel_id=1, source_target_pairs={{0,2},{2,4},{4,6},{6,8},{8,10},{10,12},{12,14},{14,16},{16,18},{18... | collective-permute-start | bytes 3538952 | tf_op jit(solution)/shard_map/ppermute | solution.py:135
  28.0 57.2 %collective-permute-start.1 = (bf16[2,384,768]{2,1,0:T(8,128)(2,1)}, bf16[2,384,768]{2,1,0:T(8,128)(2,1)S(1)}, u32[]{:S(2)}, u32[]{:S(2)}) collective-permute-start(bf16[2,384,768]{2,1,0:T(8,128)(2,1)} %shard_map.64.k_ref.v_ref), channel_id=1, source_target_pairs={{2,0},{4,2},{6,4},{8,6},{10,8},{12,10},{14,12},{16,14},{18,16},{20... | collective-permute-start | bytes 3538952 | tf_op jit(solution)/shard_map/ppermute | solution.py:136
  69.6 16.9 %copy-start = (bf16[2,384,768]{2,1,0:T(8,128)(2,1)}, bf16[2,384,768]{2,1,0:T(8,128)(2,1)S(1)}, u32[]{:S(2)}) copy-start(bf16[2,384,768]{2,1,0:T(8,128)(2,1)S(1)} %collective-permute-done.kp_ref.vp_ref) | copy-start | bytes 3538948
  85.2 1.4 %copy-start.1 = (bf16[2,384,768]{2,1,0:T(8,128)(2,1)}, bf16[2,384,768]{2,1,0:T(8,128)(2,1)S(1)}, u32[]{:S(2)}) copy-start(bf16[2,384,768]{2,1,0:T(8,128)(2,1)S(1)} %collective-permute-done.1.kn_ref.vn_ref) | copy-start | bytes 3538948
  86.6 17.6 %collective-permute-start.2 = (bf16[192,1536]{1,0:T(8,128)(2,1)}, bf16[192,1536]{1,0:T(8,128)(2,1)S(1)}, u32[]{:S(2)}, u32[]{:S(2)}) collective-permute-start(bf16[192,1536]{1,0:T(8,128)(2,1)} %get-tuple-element.25), channel_id=1, source_target_pairs={{0,32},{32,2},{2,34},{34,4},{4,36},{36,6},{6,38},{38,0},{1,33},{33... | collective-permute-start | bytes 1769480 | tf_op jit(solution)/shard_map/ppermute | solution.py:161
  88.6 17.9 %collective-permute-start.3 = (bf16[192,1536]{1,0:T(8,128)(2,1)}, bf16[192,1536]{1,0:T(8,128)(2,1)S(1)}, u32[]{:S(2)}, u32[]{:S(2)}) collective-permute-start(bf16[192,1536]{1,0:T(8,128)(2,1)} %get-tuple-element.26), channel_id=1, source_target_pairs={{0,38},{32,0},{2,32},{34,2},{4,34},{36,4},{6,36},{38,6},{1,39},{33... | collective-permute-start | bytes 1769480 | tf_op jit(solution)/shard_map/ppermute | solution.py:162
  106.9 5.0 %copy-start.2 = (f32[1,1536]{1,0:T(1,128)S(1)}, f32[1,1536]{1,0:T(1,128)}, u32[]{:S(2)}) copy-start(f32[1,1536]{1,0:T(1,128)} %param.10) | copy-start | bytes 18436
  108.5 6.2 %collective-permute-start.4 = (f32[192,1536]{1,0:T(8,128)}, f32[192,1536]{1,0:T(8,128)}, u32[]{:S(2)}, u32[]{:S(2)}) collective-permute-start(f32[192,1536]{1,0:T(8,128)} %fusion.1), channel_id=1, source_target_pairs={{0,1},{1,0},{2,3},{3,2},{4,5},{5,4},{6,7},{7,6},{8,9},{9,8},{10,11... | collective-permute-start | bytes 3538952 | tf_op jit(solution)/shard_map/ppermute | solution.py:183

commit v8 on v7

--- a/solution.py
+++ b/solution.py
@@ -56,8 +56,7 @@
 
 
 def split_kernel(kv_ref, o_ref):
-    o_ref[0] = kv_ref[:, 0, :]
-    o_ref[1] = kv_ref[:, 1, :]
+    o_ref[...] = jnp.swapaxes(kv_ref[...], 0, 1)
 
 
 def split_keys_values(kv):

time: 118 us -> 116 us (0.983)
  Pallas kernels: 21.4 us -> 19.9 us
    pallas_call x1, Pallas kernels: 5.96 us -> 4.49 us  [split_keys_values(): pl.pallas_call(split_kernel, grid=(width // HD,), in_specs=[pl.BlockSpec(...]
  transfers between devices with their start and end apart: 6 -> 6, of which waited for: 5 -> 5; matrix products, arithmetic and copies ran while one was open for 3% -> 4% of each run, Pallas kernels for 18% -> 17%
where the time goes in v8:
time: 116 us
  waiting for transfers between devices  52.4 us (45%)
  starting transfers between devices  31.1 us (27%)
  Pallas kernels  19.9 us (17%)
  local copies, waits for them, and re-layouts  4.97 us (4%)
  matrix products  3.89 us (3%)
  other arithmetic  3.07 us (3%)
    ppermute x1, waiting for transfers between devices, local(): kv_prev = lax.ppermute(kv, TM, forward)  32.6 us
    all_to_all x1, starting transfers between devices, local(): lax.all_to_all(spread, 'z', 0, 0, tiled=True)  15.7 us
    ppermute x1, waiting for transfers between devices, local(): kv_next = lax.ppermute(kv, TM, backward)  15.6 us
    pallas_call x1, Pallas kernels, attend_sides(): pl.pallas_call(side_kernel, grid_spec=pltpu.PrefetchScalarGridSpec(num_sc...  8.67 us
    pallas_call x1, Pallas kernels, attend_centre(): pl.pallas_call(centre_kernel, grid_spec=pltpu.PrefetchScalarGridSpec(num_...  6.79 us
    ppermute x1, starting transfers between devices, local(): from_above = lax.ppermute(own_rows[half:], Y, down)  4.57 us
    pallas_call x1, Pallas kernels, split_keys_values(): pl.pallas_call(split_kernel, grid=(width // HD,), in_specs=[pl.BlockSpec(...  4.49 us
    ppermute x1, starting transfers between devices, local(): kv_prev = lax.ppermute(kv, TM, forward)  4.28 us
  transfers between devices with their start and end apart: 6, of which 5 were waited for; matrix products, arithmetic and copies ran while one was open for 4% of the time, Pallas kernels for 17%

profile of v8, /device:TPU:1, one launch (start us, length us, event | category | flops | bytes accessed | tf_op | source)
XLA Modules:
  0.0 115.5 jit_solution(215854080937556381)
XLA Ops:
  0.0 2.1 %broadcast_in_dim.2 = bf16[12,32,1536]{2,1,0:T(8,128)(2,1)} broadcast(bf16[32,1536]{1,0:T(8,128)(2,1)} %param.9), dimensions={1,2} | broadcast | bytes 1277952 | tf_op jit(solution)/shard_map/broadcast_in_dim | solution.py:138
  2.1 15.7 %all-to-all-start = ((bf16[12,32,1536]{2,1,0:T(8,128)(2,1)}), bf16[12,32,1536]{2,1,0:T(8,128)(2,1)S(1)}, u32[]{:S(2)}, u32[]{:S(2)}) async-start(bf16[12,32,1536]{2,1,0:T(8,128)(2,1)} %broadcast_in_dim.2), calls=%async_computation | async-start | bytes 2359296 | tf_op jit(solution)/shard_map/all_to_all | solution.py:139
  17.8 0.0 copy-start.4
  17.8 0.0 copy-start.3
  17.8 4.5 %shard_map.64.k_ref.v_ref = bf16[2,384,768]{2,1,0:T(8,128)(2,1)} custom-call(bf16[384,2,768]{2,1,0:T(2,128)(2,1)} %bitcast.57), custom_call_target="tpu_custom_call" | custom-call | bytes 2359296 | tf_op jit(solution)/shard_map/pallas_call | solution.py:64
  22.3 4.3 %collective-permute-start = (bf16[2,384,768]{2,1,0:T(8,128)(2,1)}, bf16[2,384,768]{2,1,0:T(8,128)(2,1)S(1)}, u32[]{:S(2)}, u32[]{:S(2)}) collective-permute-start(bf16[2,384,768]{2,1,0:T(8,128)(2,1)} %shard_map.64.k_ref.v_ref), channel_id=1, source_target_pairs={{0,2},{2,4},{4,6},{6,8},{8,10},{10,12},{12,14},{14,16},{16,18},{18... | collective-permute-start | bytes 3538952 | tf_op jit(solution)/shard_map/ppermute | solution.py:134
  26.6 1.3 %collective-permute-start.1 = (bf16[2,384,768]{2,1,0:T(8,128)(2,1)}, bf16[2,384,768]{2,1,0:T(8,128)(2,1)S(1)}, u32[]{:S(2)}, u32[]{:S(2)}) collective-permute-start(bf16[2,384,768]{2,1,0:T(8,128)(2,1)} %shard_map.64.k_ref.v_ref), channel_id=1, source_target_pairs={{2,0},{4,2},{6,4},{8,6},{10,8},{12,10},{14,12},{16,14},{18,16},{20... | collective-permute-start | bytes 3538952 | tf_op jit(solution)/shard_map/ppermute | solution.py:135
  27.9 0.0 copy-done.4
  27.9 0.0 copy-done.3
  27.9 0.2 and_reduce_fusion
  28.1 0.5 convert_element_type.6.flags_ref
  28.7 6.8 %shard_map.65 = (f32[6,384,1]{2,1,0:T(8,128)}, f32[6,384,1]{2,1,0:T(8,128)}, f32[384,768]{1,0:T(8,128)}) custom-call(s32[3]{0:T(128)} %convert_element_type.6.flags_ref, bf16[384,768]{1,0:T(8,128)(2,1)} %bitcast.48, bf16[2,384,768]{2,1,0:T(8,128)(2,1)} %shard_map.64.k_ref.v_ref, bf16[2,384,768]{2,1,0:T(8,128)(2,1)} %shard_map.64.k_ref.v_ref), custom_call_target="tpu_custom_call" | custom-call | flops 452984832 | bytes 2949120 | tf_op jit(solution)/shard_map/pallas_call | solution.py:83
  35.4 32.6 %collective-permute-done.kp_ref.vp_ref = bf16[2,384,768]{2,1,0:T(8,128)(2,1)S(1)} collective-permute-done((bf16[2,384,768]{2,1,0:T(8,128)(2,1)}, bf16[2,384,768]{2,1,0:T(8,128)(2,1)S(1)}, u32[]{:S(2)}, u32[]{:S(2)}) %collective-permute-start) | collective-permute-done | bytes 1179680 | tf_op jit(solution)/shard_map/ppermute | solution.py:134
  68.1 0.0 copy-start
  68.1 15.6 %collective-permute-done.1.kn_ref.vn_ref = bf16[2,384,768]{2,1,0:T(8,128)(2,1)S(1)} collective-permute-done((bf16[2,384,768]{2,1,0:T(8,128)(2,1)}, bf16[2,384,768]{2,1,0:T(8,128)(2,1)S(1)}, u32[]{:S(2)}, u32[]{:S(2)}) %collective-permute-start.1) | collective-permute-done | bytes 1179680 | tf_op jit(solution)/shard_map/ppermute | solution.py:135
  83.7 0.0 copy-start.1
  83.7 0.0 all-to-all-done
  83.7 1.2 %fusion.19 = (bf16[192,1536]{1,0:T(8,128)(2,1)}, bf16[192,1536]{1,0:T(8,128)(2,1)}) fusion(bf16[384,1536]{1,0:T(8,128)(2,1)S(1)} %bitcast.45), kind=kLoop, calls=%fused_computation.32 | loop fusion | bytes 2359296 | tf_op jit(solution)/shard_map/slice | solution.py:160
  84.9 0.0 copy-done
  84.9 0.2 copy-done.1
  85.2 1.9 %collective-permute-start.2 = (bf16[192,1536]{1,0:T(8,128)(2,1)}, bf16[192,1536]{1,0:T(8,128)(2,1)S(1)}, u32[]{:S(2)}, u32[]{:S(2)}) collective-permute-start(bf16[192,1536]{1,0:T(8,128)(2,1)} %get-tuple-element.25), channel_id=1, source_target_pairs={{0,32},{32,2},{2,34},{34,4},{4,36},{36,6},{6,38},{38,0},{1,33},{33... | collective-permute-start | bytes 1769480 | tf_op jit(solution)/shard_map/ppermute | solution.py:160
  87.1 4.6 %collective-permute-start.3 = (bf16[192,1536]{1,0:T(8,128)(2,1)}, bf16[192,1536]{1,0:T(8,128)(2,1)S(1)}, u32[]{:S(2)}, u32[]{:S(2)}) collective-permute-start(bf16[192,1536]{1,0:T(8,128)(2,1)} %get-tuple-element.26), channel_id=1, source_target_pairs={{0,38},{32,0},{2,32},{34,2},{4,34},{36,4},{6,36},{38,6},{1,39},{33... | collective-permute-start | bytes 1769480 | tf_op jit(solution)/shard_map/ppermute | solution.py:161
  91.7 8.7 %shard_map.66 = bf16[384,768]{1,0:T(8,128)(2,1)} custom-call(s32[3]{0:T(128)} %convert_element_type.6.flags_ref, bf16[384,768]{1,0:T(8,128)(2,1)} %bitcast.49, bf16[2,384,768]{2,1,0:T(8,128)(2,1)} %copy-done, bf16[2,384,768]{2,1,0:T(8,128)(2,1)} %copy-done, bf16[2,384,768]{2,1,0:T(8,128)(2,1)} %copy-done.1, bf16[2,384,768]{2,1,0:T(8,128)(2,1)} %copy-done.1, ...), custom_call_target="tpu_custom_call" | custom-call | flops 905969664 | bytes 4718592 | tf_op jit(solution)/shard_map/pallas_call | solution.py:109
  100.3 1.4 %copy.8 = bf16[384,768]{0,1:T(8,128)(2,1)S(1)} copy(bf16[384,768]{1,0:T(8,128)(2,1)} %shard_map.66) | data formatting | bytes 1179648 | tf_op jit(solution)/shard_map/pallas_call | solution.py:109
  101.7 0.1 constant_dynamic-slice_fusion.1
  101.8 0.9 collective-permute-done.2
  102.7 0.4 fusion.7
  103.1 1.8 %collective-permute-done.3 = bf16[192,1536]{1,0:T(8,128)(2,1)S(1)} collective-permute-done((bf16[192,1536]{1,0:T(8,128)(2,1)}, bf16[192,1536]{1,0:T(8,128)(2,1)S(1)}, u32[]{:S(2)}, u32[]{:S(2)}) %collective-permute-start.3) | collective-permute-done | bytes 589856 | tf_op jit(solution)/shard_map/ppermute | solution.py:161
  105.0 0.4 fusion.5
  105.4 0.0 copy-start.2
  105.4 1.6 %fusion.1 = f32[192,1536]{1,0:T(8,128)} fusion(f32[192,1536]{1,0:T(8,128)S(1)} %fusion.5, f32[192,1536]{1,0:T(8,128)S(1)} %fusion.7, bf16[384,1536]{1,0:T(8,128)(2,1)S(1)} %bitcast.46, bf16[384,384]{0,1:T(8,128)(2,1)S(1)} %bitcast.51, s32[]{:T(128)S(6)} %select_n.60), kind=kOutput, calls=%fused_computation.3 | convolution fusion | flops 227082240 | bytes 4915204 | tf_op jit(solution)/shard_map/dot_general | solution.py:177
  107.0 3.4 %collective-permute-start.4 = (f32[192,1536]{1,0:T(8,128)}, f32[192,1536]{1,0:T(8,128)}, u32[]{:S(2)}, u32[]{:S(2)}) collective-permute-start(f32[192,1536]{1,0:T(8,128)} %fusion.1), channel_id=1, source_target_pairs={{0,1},{1,0},{2,3},{3,2},{4,5},{5,4},{6,7},{7,6},{8,9},{9,8},{10,11... | collective-permute-start | bytes 3538952 | tf_op jit(solution)/shard_map/ppermute | solution.py:182
  110.4 0.0 copy-done.2
  110.5 0.4 fusion.11
  110.9 0.4 fusion.9
  111.3 0.6 fusion
  111.9 1.3 %collective-permute-done.4 = f32[192,1536]{1,0:T(8,128)} collective-permute-done((f32[192,1536]{1,0:T(8,128)}, f32[192,1536]{1,0:T(8,128)}, u32[]{:S(2)}, u32[]{:S(2)}) %collective-permute-start.4) | collective-permute-done | bytes 1179680 | tf_op jit(solution)/shard_map/ppermute | solution.py:182
  113.2 2.3 %fusion.2 = bf16[1,1,1,1,192,1536]{5,4,3,2,1,0:T(8,128)(2,1)} fusion(f32[192,1536]{1,0:T(8,128)S(1)} %fusion, f32[192,1536]{1,0:T(8,128)} %collective-permute-done.4, f32[1536]{0:T(1024)S(1)} %reduce), kind=kLoop, calls=%fused_computation.5 | loop fusion | flops 884736 | bytes 2955264 | tf_op jit(solution)/shard_map/reshape | solution.py:186
  (3 shorter events, 0.1 us)
Async XLA Ops:
  2.1 81.7 %all-to-all-start = ((bf16[12,32,1536]{2,1,0:T(8,128)(2,1)}), bf16[12,32,1536]{2,1,0:T(8,128)(2,1)S(1)}, u32[]{:S(2)}, u32[]{:S(2)}) async-start(bf16[12,32,1536]{2,1,0:T(8,128)(2,1)} %broadcast_in_dim.2), calls=%async_computation | async-start | bytes 2359296 | tf_op jit(solution)/shard_map/all_to_all | solution.py:139
  17.8 10.1 %copy-start.4 = (s32[3]{0:T(128)S(1)}, s32[3]{0:T(128)}, u32[]{:S(2)}) copy-start(s32[3]{0:T(128)} %constant.69.clone) | copy-start | bytes 40
  17.8 10.1 %copy-start.3 = (s32[1,1,1,1,3]{4,3,2,1,0:T(1,128)S(1)}, s32[1,1,1,1,3]{4,3,2,1,0:T(1,128)}, u32[]{:S(2)}) copy-start(s32[1,1,1,1,3]{4,3,2,1,0:T(1,128)} %param.8) | copy-start | bytes 40
  22.3 45.8 %collective-permute-start = (bf16[2,384,768]{2,1,0:T(8,128)(2,1)}, bf16[2,384,768]{2,1,0:T(8,128)(2,1)S(1)}, u32[]{:S(2)}, u32[]{:S(2)}) collective-permute-start(bf16[2,384,768]{2,1,0:T(8,128)(2,1)} %shard_map.64.k_ref.v_ref), channel_id=1, source_target_pairs={{0,2},{2,4},{4,6},{6,8},{8,10},{10,12},{12,14},{14,16},{16,18},{18... | collective-permute-start | bytes 3538952 | tf_op jit(solution)/shard_map/ppermute | solution.py:134
  26.6 57.2 %collective-permute-start.1 = (bf16[2,384,768]{2,1,0:T(8,128)(2,1)}, bf16[2,384,768]{2,1,0:T(8,128)(2,1)S(1)}, u32[]{:S(2)}, u32[]{:S(2)}) collective-permute-start(bf16[2,384,768]{2,1,0:T(8,128)(2,1)} %shard_map.64.k_ref.v_ref), channel_id=1, source_target_pairs={{2,0},{4,2},{6,4},{8,6},{10,8},{12,10},{14,12},{16,14},{18,16},{20... | collective-permute-start | bytes 3538952 | tf_op jit(solution)/shard_map/ppermute | solution.py:135
  68.1 16.9 %copy-start = (bf16[2,384,768]{2,1,0:T(8,128)(2,1)}, bf16[2,384,768]{2,1,0:T(8,128)(2,1)S(1)}, u32[]{:S(2)}) copy-start(bf16[2,384,768]{2,1,0:T(8,128)(2,1)S(1)} %collective-permute-done.kp_ref.vp_ref) | copy-start | bytes 3538948
  83.7 1.4 %copy-start.1 = (bf16[2,384,768]{2,1,0:T(8,128)(2,1)}, bf16[2,384,768]{2,1,0:T(8,128)(2,1)S(1)}, u32[]{:S(2)}) copy-start(bf16[2,384,768]{2,1,0:T(8,128)(2,1)S(1)} %collective-permute-done.1.kn_ref.vn_ref) | copy-start | bytes 3538948
  85.2 17.6 %collective-permute-start.2 = (bf16[192,1536]{1,0:T(8,128)(2,1)}, bf16[192,1536]{1,0:T(8,128)(2,1)S(1)}, u32[]{:S(2)}, u32[]{:S(2)}) collective-permute-start(bf16[192,1536]{1,0:T(8,128)(2,1)} %get-tuple-element.25), channel_id=1, source_target_pairs={{0,32},{32,2},{2,34},{34,4},{4,36},{36,6},{6,38},{38,0},{1,33},{33... | collective-permute-start | bytes 1769480 | tf_op jit(solution)/shard_map/ppermute | solution.py:160
  87.1 17.9 %collective-permute-start.3 = (bf16[192,1536]{1,0:T(8,128)(2,1)}, bf16[192,1536]{1,0:T(8,128)(2,1)S(1)}, u32[]{:S(2)}, u32[]{:S(2)}) collective-permute-start(bf16[192,1536]{1,0:T(8,128)(2,1)} %get-tuple-element.26), channel_id=1, source_target_pairs={{0,38},{32,0},{2,32},{34,2},{4,34},{36,4},{6,36},{38,6},{1,39},{33... | collective-permute-start | bytes 1769480 | tf_op jit(solution)/shard_map/ppermute | solution.py:161
  105.4 5.0 %copy-start.2 = (f32[1,1536]{1,0:T(1,128)S(1)}, f32[1,1536]{1,0:T(1,128)}, u32[]{:S(2)}) copy-start(f32[1,1536]{1,0:T(1,128)} %param.10) | copy-start | bytes 18436
  107.0 6.2 %collective-permute-start.4 = (f32[192,1536]{1,0:T(8,128)}, f32[192,1536]{1,0:T(8,128)}, u32[]{:S(2)}, u32[]{:S(2)}) collective-permute-start(f32[192,1536]{1,0:T(8,128)} %fusion.1), channel_id=1, source_target_pairs={{0,1},{1,0},{2,3},{3,2},{4,5},{5,4},{6,7},{7,6},{8,9},{9,8},{10,11... | collective-permute-start | bytes 3538952 | tf_op jit(solution)/shard_map/ppermute | solution.py:182

commit v9 on v8

--- a/solution.py
+++ b/solution.py
@@ -63,9 +63,8 @@
     tl, _, width = kv.shape
     return pl.pallas_call(
         split_kernel,
-        grid=(width // HD,),
-        in_specs=[pl.BlockSpec((tl, 2, HD), lambda h: (0, 0, h))],
-        out_specs=pl.BlockSpec((2, tl, HD), lambda h: (0, 0, h)),
+        in_specs=[pl.BlockSpec(memory_space=pltpu.VMEM)],
+        out_specs=pl.BlockSpec(memory_space=pltpu.VMEM),
         out_shape=jax.ShapeDtypeStruct((2, tl, width), kv.dtype),
         cost_estimate=pl.CostEstimate(flops=0, transcendentals=0, bytes_accessed=4 * tl * width * 2),
     )(kv)
@@ -136,6 +135,7 @@
 
     zs = lax.axis_size("z")
     spread = jnp.broadcast_to(out_weight[None], (zs,) + out_weight.shape)
+    spread, kv = lax.optimization_barrier((spread, kv))
     own_rows = lax.all_to_all(spread, "z", 0, 0, tiled=True).reshape(-1, out_weight.shape[1])
 
     offsets = window_offsets[0, 0, 0, 0]

time: 116 us -> 113 us (0.974)
  Pallas kernels: 19.9 us -> 18.1 us
  local copies, waits for them, and re-layouts: 4.97 us -> 3.75 us
    pallas_call x1, Pallas kernels: 4.49 us -> 2.64 us  [split_keys_values(): pl.pallas_call(split_kernel, in_specs=[pl.BlockSpec(memory_space=pltpu.VM...]
  transfers between devices with their start and end apart: 6 -> 6, of which waited for: 5 -> 5; matrix products, arithmetic and copies ran while one was open for 4% -> 4% of each run, Pallas kernels for 17% -> 14%
where the time goes in v9:
time: 113 us
  waiting for transfers between devices  52.2 us (46%)
  starting transfers between devices  31.3 us (28%)
  Pallas kernels  18.1 us (16%)
  matrix products  3.87 us (3%)
  local copies, waits for them, and re-layouts  3.75 us (3%)
  other arithmetic  3.12 us (3%)
    ppermute x1, waiting for transfers between devices, local(): kv_prev = lax.ppermute(kv, TM, forward)  32.3 us
    ppermute x1, waiting for transfers between devices, local(): kv_next = lax.ppermute(kv, TM, backward)  15.9 us
    all_to_all x1, starting transfers between devices, local(): lax.all_to_all(spread, 'z', 0, 0, tiled=True)  15.8 us
    pallas_call x1, Pallas kernels, attend_sides(): pl.pallas_call(side_kernel, grid_spec=pltpu.PrefetchScalarGridSpec(num_sc...  8.65 us
    pallas_call x1, Pallas kernels, attend_centre(): pl.pallas_call(centre_kernel, grid_spec=pltpu.PrefetchScalarGridSpec(num_...  6.77 us
    ppermute x1, starting transfers between devices, local(): from_above = lax.ppermute(own_rows[half:], Y, down)  4.57 us
    ppermute x1, starting transfers between devices, local(): kv_prev = lax.ppermute(kv, TM, forward)  4.29 us
    ppermute x1, starting transfers between devices, local(): got = lax.ppermute(sent, ROWS, [(0, 1), (1, 0)])  3.39 us
  transfers between devices with their start and end apart: 6, of which 5 were waited for; matrix products, arithmetic and copies ran while one was open for 4% of the time, Pallas kernels for 14%

profile of v9, /device:TPU:1, one launch (start us, length us, event | category | flops | bytes accessed | tf_op | source)
XLA Modules:
  0.0 112.5 jit_solution(1851156216952211934)
XLA Ops:
  0.0 0.0 copy-start.2
  0.0 2.6 %shard_map.64.k_ref.v_ref = bf16[2,384,768]{2,1,0:T(8,128)(2,1)} custom-call(bf16[384,2,768]{2,1,0:T(2,128)(2,1)} %bitcast.57), custom_call_target="tpu_custom_call" | custom-call | bytes 2359296 | tf_op jit(solution)/shard_map/pallas_call | solution.py:64
  2.6 0.0 copy-done.2
  2.6 1.2 %broadcast_in_dim.2 = bf16[12,32,1536]{2,1,0:T(8,128)(2,1)} broadcast(bf16[32,1536]{1,0:T(8,128)(2,1)S(1)} %copy-done.2), dimensions={1,2} | broadcast | bytes 1277952 | tf_op jit(solution)/shard_map/broadcast_in_dim | solution.py:137
  3.8 0.0 copy-start
  3.8 0.0 copy-start.5
  3.8 0.0 copy-start.4
  3.8 15.8 %all-to-all-start = ((bf16[12,32,1536]{2,1,0:T(8,128)(2,1)}), bf16[12,32,1536]{2,1,0:T(8,128)(2,1)S(1)}, u32[]{:S(2)}, u32[]{:S(2)}) async-start(bf16[12,32,1536]{2,1,0:T(8,128)(2,1)} %broadcast_in_dim.2), calls=%async_computation | async-start | bytes 2359296 | tf_op jit(solution)/shard_map/all_to_all | solution.py:139
  19.7 0.0 copy-done
  19.7 4.3 %collective-permute-start = (bf16[2,384,768]{2,1,0:T(8,128)(2,1)S(1)}, bf16[2,384,768]{2,1,0:T(8,128)(2,1)S(1)}, u32[]{:S(2)}, u32[]{:S(2)}) collective-permute-start(bf16[2,384,768]{2,1,0:T(8,128)(2,1)S(1)} %copy-done), channel_id=1, source_target_pairs={{0,2},{2,4},{4,6},{6,8},{8,10},{10,12},{12,14},{14,16},{16,18},{18... | collective-permute-start | bytes 3538952 | tf_op jit(solution)/shard_map/ppermute | solution.py:133
  24.0 1.3 %collective-permute-start.1 = (bf16[2,384,768]{2,1,0:T(8,128)(2,1)S(1)}, bf16[2,384,768]{2,1,0:T(8,128)(2,1)}, u32[]{:S(2)}, u32[]{:S(2)}) collective-permute-start(bf16[2,384,768]{2,1,0:T(8,128)(2,1)S(1)} %copy-done), channel_id=1, source_target_pairs={{2,0},{4,2},{6,4},{8,6},{10,8},{12,10},{14,12},{16,14},{18,16},{20... | collective-permute-start | bytes 3538952 | tf_op jit(solution)/shard_map/ppermute | solution.py:134
  25.3 0.0 copy-done.5
  25.3 0.0 copy-done.4
  25.3 0.2 and_reduce_fusion
  25.5 0.6 convert_element_type.6.flags_ref
  26.1 6.8 %shard_map.65 = (f32[6,384,1]{2,1,0:T(8,128)}, f32[6,384,1]{2,1,0:T(8,128)}, f32[384,768]{1,0:T(8,128)}) custom-call(s32[3]{0:T(128)} %convert_element_type.6.flags_ref, bf16[384,768]{1,0:T(8,128)(2,1)} %bitcast.48, bf16[2,384,768]{2,1,0:T(8,128)(2,1)} %shard_map.64.k_ref.v_ref, bf16[2,384,768]{2,1,0:T(8,128)(2,1)} %shard_map.64.k_ref.v_ref), custom_call_target="tpu_custom_call" | custom-call | flops 452984832 | bytes 2949120 | tf_op jit(solution)/shard_map/pallas_call | solution.py:82
  32.9 32.3 %collective-permute-done.kp_ref.vp_ref = bf16[2,384,768]{2,1,0:T(8,128)(2,1)S(1)} collective-permute-done((bf16[2,384,768]{2,1,0:T(8,128)(2,1)S(1)}, bf16[2,384,768]{2,1,0:T(8,128)(2,1)S(1)}, u32[]{:S(2)}, u32[]{:S(2)}) %collective-permute-start) | collective-permute-done | bytes 1179680 | tf_op jit(solution)/shard_map/ppermute | solution.py:133
  65.2 0.0 copy-start.1
  65.2 15.9 %collective-permute-done.1.kn_ref.vn_ref = bf16[2,384,768]{2,1,0:T(8,128)(2,1)} collective-permute-done((bf16[2,384,768]{2,1,0:T(8,128)(2,1)S(1)}, bf16[2,384,768]{2,1,0:T(8,128)(2,1)}, u32[]{:S(2)}, u32[]{:S(2)}) %collective-permute-start.1) | collective-permute-done | bytes 1179680 | tf_op jit(solution)/shard_map/ppermute | solution.py:134
  81.0 0.0 all-to-all-done
  81.0 1.1 fusion.19
  82.1 0.0 copy-done.1
  82.1 1.9 %collective-permute-start.2 = (bf16[192,1536]{1,0:T(8,128)(2,1)}, bf16[192,1536]{1,0:T(8,128)(2,1)S(1)}, u32[]{:S(2)}, u32[]{:S(2)}) collective-permute-start(bf16[192,1536]{1,0:T(8,128)(2,1)} %get-tuple-element.29), channel_id=1, source_target_pairs={{0,32},{32,2},{2,34},{34,4},{4,36},{36,6},{6,38},{38,0},{1,33},{33... | collective-permute-start | bytes 1769480 | tf_op jit(solution)/shard_map/ppermute | solution.py:160
  84.0 4.6 %collective-permute-start.3 = (bf16[192,1536]{1,0:T(8,128)(2,1)}, bf16[192,1536]{1,0:T(8,128)(2,1)S(1)}, u32[]{:S(2)}, u32[]{:S(2)}) collective-permute-start(bf16[192,1536]{1,0:T(8,128)(2,1)} %get-tuple-element.30), channel_id=1, source_target_pairs={{0,38},{32,0},{2,32},{34,2},{4,34},{36,4},{6,36},{38,6},{1,39},{33... | collective-permute-start | bytes 1769480 | tf_op jit(solution)/shard_map/ppermute | solution.py:161
  88.6 8.6 %shard_map.66 = bf16[384,768]{1,0:T(8,128)(2,1)} custom-call(s32[3]{0:T(128)} %convert_element_type.6.flags_ref, bf16[384,768]{1,0:T(8,128)(2,1)} %bitcast.49, bf16[2,384,768]{2,1,0:T(8,128)(2,1)} %copy-done.1, bf16[2,384,768]{2,1,0:T(8,128)(2,1)} %copy-done.1, bf16[2,384,768]{2,1,0:T(8,128)(2,1)} %collective-permute-done.1.kn_ref.vn_ref, ...), custom_call_target="tpu_custom_call" | custom-call | flops 905969664 | bytes 4718592 | tf_op jit(solution)/shard_map/pallas_call | solution.py:108
  97.3 1.4 %copy.8 = bf16[384,768]{0,1:T(8,128)(2,1)S(1)} copy(bf16[384,768]{1,0:T(8,128)(2,1)} %shard_map.66) | data formatting | bytes 1179648 | tf_op jit(solution)/shard_map/pallas_call | solution.py:108
  98.7 0.1 constant_dynamic-slice_fusion.1
  98.7 1.0 collective-permute-done.2
  99.7 0.4 fusion.7
  100.1 1.8 %collective-permute-done.3 = bf16[192,1536]{1,0:T(8,128)(2,1)S(1)} collective-permute-done((bf16[192,1536]{1,0:T(8,128)(2,1)}, bf16[192,1536]{1,0:T(8,128)(2,1)S(1)}, u32[]{:S(2)}, u32[]{:S(2)}) %collective-permute-start.3) | collective-permute-done | bytes 589856 | tf_op jit(solution)/shard_map/ppermute | solution.py:161
  102.0 0.4 fusion.5
  102.4 0.0 copy-start.3
  102.4 1.6 %fusion.1 = f32[192,1536]{1,0:T(8,128)} fusion(f32[192,1536]{1,0:T(8,128)S(1)} %fusion.5, f32[192,1536]{1,0:T(8,128)S(1)} %fusion.7, bf16[384,1536]{1,0:T(8,128)(2,1)S(1)} %bitcast.46, bf16[384,384]{0,1:T(8,128)(2,1)S(1)} %bitcast.51, s32[]{:T(128)S(6)} %select_n.60), kind=kOutput, calls=%fused_computation.3 | convolution fusion | flops 227082240 | bytes 4915204 | tf_op jit(solution)/shard_map/dot_general | solution.py:177
  104.0 3.4 %collective-permute-start.4 = (f32[192,1536]{1,0:T(8,128)}, f32[192,1536]{1,0:T(8,128)}, u32[]{:S(2)}, u32[]{:S(2)}) collective-permute-start(f32[192,1536]{1,0:T(8,128)} %fusion.1), channel_id=1, source_target_pairs={{0,1},{1,0},{2,3},{3,2},{4,5},{5,4},{6,7},{7,6},{8,9},{9,8},{10,11... | collective-permute-start | bytes 3538952 | tf_op jit(solution)/shard_map/ppermute | solution.py:182
  107.4 0.0 copy-done.3
  107.4 0.4 fusion.11
  107.9 0.4 fusion.9
  108.3 0.6 fusion
  108.9 1.3 %collective-permute-done.4 = f32[192,1536]{1,0:T(8,128)} collective-permute-done((f32[192,1536]{1,0:T(8,128)}, f32[192,1536]{1,0:T(8,128)}, u32[]{:S(2)}, u32[]{:S(2)}) %collective-permute-start.4) | collective-permute-done | bytes 1179680 | tf_op jit(solution)/shard_map/ppermute | solution.py:182
  110.2 2.3 %fusion.2 = bf16[1,1,1,1,192,1536]{5,4,3,2,1,0:T(8,128)(2,1)} fusion(f32[192,1536]{1,0:T(8,128)S(1)} %fusion, f32[192,1536]{1,0:T(8,128)} %collective-permute-done.4, f32[1536]{0:T(1024)S(1)} %reduce), kind=kLoop, calls=%fused_computation.5 | loop fusion | flops 884736 | bytes 2955264 | tf_op jit(solution)/shard_map/reshape | solution.py:186
  (3 shorter events, 0.1 us)
Async XLA Ops:
  0.0 2.6 %copy-start.2 = (bf16[32,1536]{1,0:T(8,128)(2,1)S(1)}, bf16[32,1536]{1,0:T(8,128)(2,1)}, u32[]{:S(2)}) copy-start(bf16[32,1536]{1,0:T(8,128)(2,1)} %param.9) | copy-start | bytes 294916
  3.8 15.9 %copy-start = (bf16[2,384,768]{2,1,0:T(8,128)(2,1)S(1)}, bf16[2,384,768]{2,1,0:T(8,128)(2,1)}, u32[]{:S(2)}) copy-start(bf16[2,384,768]{2,1,0:T(8,128)(2,1)} %shard_map.64.k_ref.v_ref) | copy-start | bytes 3538948
  3.8 21.5 %copy-start.5 = (s32[3]{0:T(128)S(1)}, s32[3]{0:T(128)}, u32[]{:S(2)}) copy-start(s32[3]{0:T(128)} %constant.69.clone) | copy-start | bytes 40
  3.8 21.5 %copy-start.4 = (s32[1,1,1,1,3]{4,3,2,1,0:T(1,128)S(1)}, s32[1,1,1,1,3]{4,3,2,1,0:T(1,128)}, u32[]{:S(2)}) copy-start(s32[1,1,1,1,3]{4,3,2,1,0:T(1,128)} %param.8) | copy-start | bytes 40
  3.8 77.2 %all-to-all-start = ((bf16[12,32,1536]{2,1,0:T(8,128)(2,1)}), bf16[12,32,1536]{2,1,0:T(8,128)(2,1)S(1)}, u32[]{:S(2)}, u32[]{:S(2)}) async-start(bf16[12,32,1536]{2,1,0:T(8,128)(2,1)} %broadcast_in_dim.2), calls=%async_computation | async-start | bytes 2359296 | tf_op jit(solution)/shard_map/all_to_all | solution.py:139
  19.7 45.5 %collective-permute-start = (bf16[2,384,768]{2,1,0:T(8,128)(2,1)S(1)}, bf16[2,384,768]{2,1,0:T(8,128)(2,1)S(1)}, u32[]{:S(2)}, u32[]{:S(2)}) collective-permute-start(bf16[2,384,768]{2,1,0:T(8,128)(2,1)S(1)} %copy-done), channel_id=1, source_target_pairs={{0,2},{2,4},{4,6},{6,8},{8,10},{10,12},{12,14},{14,16},{16,18},{18... | collective-permute-start | bytes 3538952 | tf_op jit(solution)/shard_map/ppermute | solution.py:133
  24.0 57.0 %collective-permute-start.1 = (bf16[2,384,768]{2,1,0:T(8,128)(2,1)S(1)}, bf16[2,384,768]{2,1,0:T(8,128)(2,1)}, u32[]{:S(2)}, u32[]{:S(2)}) collective-permute-start(bf16[2,384,768]{2,1,0:T(8,128)(2,1)S(1)} %copy-done), channel_id=1, source_target_pairs={{2,0},{4,2},{6,4},{8,6},{10,8},{12,10},{14,12},{16,14},{18,16},{20... | collective-permute-start | bytes 3538952 | tf_op jit(solution)/shard_map/ppermute | solution.py:134
  65.2 17.0 %copy-start.1 = (bf16[2,384,768]{2,1,0:T(8,128)(2,1)}, bf16[2,384,768]{2,1,0:T(8,128)(2,1)S(1)}, u32[]{:S(2)}) copy-start(bf16[2,384,768]{2,1,0:T(8,128)(2,1)S(1)} %collective-permute-done.kp_ref.vp_ref) | copy-start | bytes 3538948
  82.1 17.6 %collective-permute-start.2 = (bf16[192,1536]{1,0:T(8,128)(2,1)}, bf16[192,1536]{1,0:T(8,128)(2,1)S(1)}, u32[]{:S(2)}, u32[]{:S(2)}) collective-permute-start(bf16[192,1536]{1,0:T(8,128)(2,1)} %get-tuple-element.29), channel_id=1, source_target_pairs={{0,32},{32,2},{2,34},{34,4},{4,36},{36,6},{6,38},{38,0},{1,33},{33... | collective-permute-start | bytes 1769480 | tf_op jit(solution)/shard_map/ppermute | solution.py:160
  84.0 17.9 %collective-permute-start.3 = (bf16[192,1536]{1,0:T(8,128)(2,1)}, bf16[192,1536]{1,0:T(8,128)(2,1)S(1)}, u32[]{:S(2)}, u32[]{:S(2)}) collective-permute-start(bf16[192,1536]{1,0:T(8,128)(2,1)} %get-tuple-element.30), channel_id=1, source_target_pairs={{0,38},{32,0},{2,32},{34,2},{4,34},{36,4},{6,36},{38,6},{1,39},{33... | collective-permute-start | bytes 1769480 | tf_op jit(solution)/shard_map/ppermute | solution.py:161
  102.4 5.0 %copy-start.3 = (f32[1,1536]{1,0:T(1,128)S(1)}, f32[1,1536]{1,0:T(1,128)}, u32[]{:S(2)}) copy-start(f32[1,1536]{1,0:T(1,128)} %param.10) | copy-start | bytes 18436
  104.0 6.2 %collective-permute-start.4 = (f32[192,1536]{1,0:T(8,128)}, f32[192,1536]{1,0:T(8,128)}, u32[]{:S(2)}, u32[]{:S(2)}) collective-permute-start(f32[192,1536]{1,0:T(8,128)} %fusion.1), channel_id=1, source_target_pairs={{0,1},{1,0},{2,3},{3,2},{4,5},{5,4},{6,7},{7,6},{8,9},{9,8},{10,11... | collective-permute-start | bytes 3538952 | tf_op jit(solution)/shard_map/ppermute | solution.py:182

commit v10 on v9

--- a/solution.py
+++ b/solution.py
@@ -134,9 +134,7 @@
     kv_next = lax.ppermute(kv, TM, backward)
 
     zs = lax.axis_size("z")
-    spread = jnp.broadcast_to(out_weight[None], (zs,) + out_weight.shape)
-    spread, kv = lax.optimization_barrier((spread, kv))
-    own_rows = lax.all_to_all(spread, "z", 0, 0, tiled=True).reshape(-1, out_weight.shape[1])
+    own_rows = lax.all_gather(out_weight, "z", axis=0, tiled=True)
 
     offsets = window_offsets[0, 0, 0, 0]
     near_t = time_now + offsets // 9 - 1

time: 113 us -> 115 us (1.018)
  between operations: 0.16 us -> 13.6 us
  starting transfers between devices: 31.3 us -> 20.9 us
  waiting for transfers between devices: 52.2 us -> 50.1 us
    all_to_all x1 -> x0, starting transfers between devices: 15.8 us -> none  [local(): lax.all_to_all(spread, 'z', 0, 0, tiled=True)]
    ppermute x1, waiting for transfers between devices: 32.3 us -> 25.2 us  [local(): kv_prev = lax.ppermute(kv, TM, forward)]
    ppermute x1, waiting for transfers between devices: 15.9 us -> 22.9 us  [local(): kv_next = lax.ppermute(kv, TM, backward)]
    ppermute x1, starting transfers between devices: 3.39 us -> 8.01 us  [local(): got = lax.ppermute(sent, ROWS, [(0, 1), (1, 0)])]
    ppermute x1, waiting for transfers between devices: 1.84 us -> 0.01 us  [local(): from_above = lax.ppermute(own_rows[half:], Y, down)]
    slice x1, local copies, waits for them, and re-layouts: 1.11 us -> 2.56 us  [local(): from_below = lax.ppermute(own_rows[:half], Y, up)]
    broadcast_in_dim x1 -> x0, local copies, waits for them, and re-layouts: 1.16 us -> none  [local(): spread = jnp.broadcast_to(out_weight[None], (zs,) + out_weight.shape)]
  transfers between devices with their start and end apart: 6 -> 6, of which waited for: 5 -> 3; matrix products, arithmetic and copies ran while one was open for 4% -> 4% of each run, Pallas kernels for 14% -> 16%
where the time goes in v10:
time: 115 us
  waiting for transfers between devices  50.1 us (44%)
  starting transfers between devices  20.9 us (18%)
  Pallas kernels  18.1 us (16%)
  between operations  13.6 us (12%)
  local copies, waits for them, and re-layouts  4.86 us (4%)
  matrix products  3.9 us (3%)
  other arithmetic  3.08 us (3%)
    ppermute x1, waiting for transfers between devices, local(): kv_prev = lax.ppermute(kv, TM, forward)  25.2 us
    ppermute x1, waiting for transfers between devices, local(): kv_next = lax.ppermute(kv, TM, backward)  22.9 us
    pallas_call x1, Pallas kernels, attend_sides(): pl.pallas_call(side_kernel, grid_spec=pltpu.PrefetchScalarGridSpec(num_sc...  8.66 us
    ppermute x1, starting transfers between devices, local(): got = lax.ppermute(sent, ROWS, [(0, 1), (1, 0)])  8.01 us
    pallas_call x1, Pallas kernels, attend_centre(): pl.pallas_call(centre_kernel, grid_spec=pltpu.PrefetchScalarGridSpec(num_...  6.85 us
    ppermute x1, starting transfers between devices, local(): kv_prev = lax.ppermute(kv, TM, forward)  5.1 us
    ppermute x1, starting transfers between devices, local(): from_above = lax.ppermute(own_rows[half:], Y, down)  4.57 us
    pallas_call x1, Pallas kernels, split_keys_values(): pl.pallas_call(split_kernel, in_specs=[pl.BlockSpec(memory_space=pltpu.VM...  2.63 us
  transfers between devices with their start and end apart: 6, of which 3 were waited for; matrix products, arithmetic and copies ran while one was open for 4% of the time, Pallas kernels for 16%

profile of v10, /device:TPU:1, one launch (start us, length us, event | category | flops | bytes accessed | tf_op | source)
XLA Modules:
  0.0 114.5 jit_solution(653838557944690568)
XLA Ops:
  6.5 0.0 all-gather.2.cloned.1.call-start
  6.5 0.7 all-gather.2.cloned.1.call-update
  7.3 0.0 copy-start.5
  7.3 0.0 copy-start.4
  7.3 2.6 %shard_map.64.k_ref.v_ref = bf16[2,384,768]{2,1,0:T(8,128)(2,1)} custom-call(bf16[384,2,768]{2,1,0:T(2,128)(2,1)} %bitcast.53), custom_call_target="tpu_custom_call" | custom-call | bytes 2359296 | tf_op jit(solution)/shard_map/pallas_call | solution.py:64
  9.9 5.1 %collective-permute-start = (bf16[2,384,768]{2,1,0:T(8,128)(2,1)}, bf16[2,384,768]{2,1,0:T(8,128)(2,1)S(1)}, u32[]{:S(2)}, u32[]{:S(2)}) collective-permute-start(bf16[2,384,768]{2,1,0:T(8,128)(2,1)} %shard_map.64.k_ref.v_ref), channel_id=1, source_target_pairs={{0,2},{2,4},{4,6},{6,8},{8,10},{10,12},{12,14},{14,16},{16,18},{18... | collective-permute-start | bytes 3538952 | tf_op jit(solution)/shard_map/ppermute | solution.py:133
  15.0 1.3 %collective-permute-start.1 = (bf16[2,384,768]{2,1,0:T(8,128)(2,1)}, bf16[2,384,768]{2,1,0:T(8,128)(2,1)S(1)}, u32[]{:S(2)}, u32[]{:S(2)}) collective-permute-start(bf16[2,384,768]{2,1,0:T(8,128)(2,1)} %shard_map.64.k_ref.v_ref), channel_id=1, source_target_pairs={{2,0},{4,2},{6,4},{8,6},{10,8},{12,10},{14,12},{16,14},{18,16},{20... | collective-permute-start | bytes 3538952 | tf_op jit(solution)/shard_map/ppermute | solution.py:134
  16.3 0.0 copy-done.5
  16.4 0.0 copy-done.4
  16.4 0.2 and_reduce_fusion
  16.6 0.5 convert_element_type.6.flags_ref
  17.1 6.9 %shard_map.65 = (f32[6,384,1]{2,1,0:T(8,128)}, f32[6,384,1]{2,1,0:T(8,128)}, f32[384,768]{1,0:T(8,128)}) custom-call(s32[3]{0:T(128)} %convert_element_type.6.flags_ref, bf16[384,768]{1,0:T(8,128)(2,1)} %bitcast.44, bf16[2,384,768]{2,1,0:T(8,128)(2,1)} %shard_map.64.k_ref.v_ref, bf16[2,384,768]{2,1,0:T(8,128)(2,1)} %shard_map.64.k_ref.v_ref), custom_call_target="tpu_custom_call" | custom-call | flops 452984832 | bytes 2949120 | tf_op jit(solution)/shard_map/pallas_call | solution.py:82
  24.0 25.2 %collective-permute-done.kp_ref.vp_ref = bf16[2,384,768]{2,1,0:T(8,128)(2,1)S(1)} collective-permute-done((bf16[2,384,768]{2,1,0:T(8,128)(2,1)}, bf16[2,384,768]{2,1,0:T(8,128)(2,1)S(1)}, u32[]{:S(2)}, u32[]{:S(2)}) %collective-permute-start) | collective-permute-done | bytes 1179680 | tf_op jit(solution)/shard_map/ppermute | solution.py:133
  49.1 0.0 copy-start.1
  49.1 22.9 %collective-permute-done.1.kn_ref.vn_ref = bf16[2,384,768]{2,1,0:T(8,128)(2,1)S(1)} collective-permute-done((bf16[2,384,768]{2,1,0:T(8,128)(2,1)}, bf16[2,384,768]{2,1,0:T(8,128)(2,1)S(1)}, u32[]{:S(2)}, u32[]{:S(2)}) %collective-permute-start.1) | collective-permute-done | bytes 1179680 | tf_op jit(solution)/shard_map/ppermute | solution.py:134
  72.1 0.0 copy-start.2
  72.1 0.0 all-gather.2.cloned.1.call-done
  72.1 2.6 %fusion.19 = (bf16[192,1536]{1,0:T(8,128)(2,1)}, bf16[192,1536]{1,0:T(8,128)(2,1)S(1)}) fusion(bf16[384,1536]{1,0:T(8,128)(2,1)} %all-gather.2.cloned.1.call-done), kind=kLoop, calls=%fused_computation.32 | loop fusion | bytes 2359296 | tf_op jit(solution)/shard_map/slice | solution.py:158
  74.6 0.0 copy-done.1
  74.6 0.0 copy-done.2
  74.6 1.9 %collective-permute-start.2 = (bf16[192,1536]{1,0:T(8,128)(2,1)}, bf16[192,1536]{1,0:T(8,128)(2,1)S(1)}, u32[]{:S(2)}, u32[]{:S(2)}) collective-permute-start(bf16[192,1536]{1,0:T(8,128)(2,1)} %get-tuple-element.25), channel_id=1, source_target_pairs={{0,32},{32,2},{2,34},{34,4},{4,36},{36,6},{6,38},{38,0},{1,33},{33... | collective-permute-start | bytes 1769480 | tf_op jit(solution)/shard_map/ppermute | solution.py:158
  76.5 4.6 %collective-permute-start.3 = (bf16[192,1536]{1,0:T(8,128)(2,1)S(1)}, bf16[192,1536]{1,0:T(8,128)(2,1)S(1)}, u32[]{:S(2)}, u32[]{:S(2)}) collective-permute-start(bf16[192,1536]{1,0:T(8,128)(2,1)S(1)} %get-tuple-element.26), channel_id=1, source_target_pairs={{0,38},{32,0},{2,32},{34,2},{4,34},{36,4},{6,36},{38,6},{1,39},{33... | collective-permute-start | bytes 1769480 | tf_op jit(solution)/shard_map/ppermute | solution.py:159
  81.1 8.7 %shard_map.66 = bf16[384,768]{1,0:T(8,128)(2,1)} custom-call(s32[3]{0:T(128)} %convert_element_type.6.flags_ref, bf16[384,768]{1,0:T(8,128)(2,1)} %bitcast.45, bf16[2,384,768]{2,1,0:T(8,128)(2,1)} %copy-done.1, bf16[2,384,768]{2,1,0:T(8,128)(2,1)} %copy-done.1, bf16[2,384,768]{2,1,0:T(8,128)(2,1)} %copy-done.2, bf16[2,384,768]{2,1,0:T(8,128)(2,1)} %copy-done.2, ...), custom_call_target="tpu_custom_call" | custom-call | flops 905969664 | bytes 4718592 | tf_op jit(solution)/shard_map/pallas_call | solution.py:108
  89.8 1.4 %copy.8 = bf16[384,768]{0,1:T(8,128)(2,1)S(1)} copy(bf16[384,768]{1,0:T(8,128)(2,1)} %shard_map.66) | data formatting | bytes 1179648 | tf_op jit(solution)/shard_map/pallas_call | solution.py:108
  91.2 0.1 constant_dynamic-slice_fusion.1
  91.2 0.0 collective-permute-done.2
  91.3 0.4 fusion.7
  91.7 0.0 copy-start
  91.7 0.0 collective-permute-done.3
  91.7 0.4 fusion.5
  92.1 0.8 copy-done
  93.0 0.0 copy-start.3
  93.0 1.6 %fusion.1 = f32[192,1536]{1,0:T(8,128)} fusion(f32[192,1536]{1,0:T(8,128)S(1)} %fusion.5, f32[192,1536]{1,0:T(8,128)S(1)} %fusion.7, bf16[384,1536]{1,0:T(8,128)(2,1)S(1)} %copy-done, bf16[384,384]{0,1:T(8,128)(2,1)S(1)} %bitcast.47, s32[]{:T(128)S(6)} %select_n.60), kind=kOutput, calls=%fused_computation.3 | convolution fusion | flops 227082240 | bytes 4915204 | tf_op jit(solution)/shard_map/dot_general | solution.py:175
  94.6 8.0 %collective-permute-start.4 = (f32[192,1536]{1,0:T(8,128)}, f32[192,1536]{1,0:T(8,128)}, u32[]{:S(2)}, u32[]{:S(2)}) collective-permute-start(f32[192,1536]{1,0:T(8,128)} %fusion.1), channel_id=1, source_target_pairs={{0,1},{1,0},{2,3},{3,2},{4,5},{5,4},{6,7},{7,6},{8,9},{9,8},{10,11... | collective-permute-start | bytes 3538952 | tf_op jit(solution)/shard_map/ppermute | solution.py:180
  102.6 0.0 copy-done.3
  102.6 0.4 fusion.11
  103.0 0.4 fusion.9
  103.5 0.6 fusion
  104.1 1.3 %collective-permute-done.4 = f32[192,1536]{1,0:T(8,128)} collective-permute-done((f32[192,1536]{1,0:T(8,128)}, f32[192,1536]{1,0:T(8,128)}, u32[]{:S(2)}, u32[]{:S(2)}) %collective-permute-start.4) | collective-permute-done | bytes 1179680 | tf_op jit(solution)/shard_map/ppermute | solution.py:180
  105.4 2.3 %fusion.2 = bf16[1,1,1,1,192,1536]{5,4,3,2,1,0:T(8,128)(2,1)} fusion(f32[192,1536]{1,0:T(8,128)S(1)} %fusion, f32[192,1536]{1,0:T(8,128)} %collective-permute-done.4, f32[1536]{0:T(1024)S(1)} %reduce), kind=kLoop, calls=%fused_computation.5 | loop fusion | flops 884736 | bytes 2955264 | tf_op jit(solution)/shard_map/reshape | solution.py:184
  (3 shorter events, 0.1 us)
Async XLA Ops:
  6.5 65.5 %all-gather.2.cloned.1.call-start = ((), (), s32[]{:S(2)}) async-start(), calls=%async_computation | async-start | bytes 1277952 | tf_op jit(solution)/shard_map/all_gather | solution.py:137
  7.3 9.1 %copy-start.5 = (s32[3]{0:T(128)S(1)}, s32[3]{0:T(128)}, u32[]{:S(2)}) copy-start(s32[3]{0:T(128)} %constant.69.clone) | copy-start | bytes 40
  7.3 9.1 %copy-start.4 = (s32[1,1,1,1,3]{4,3,2,1,0:T(1,128)S(1)}, s32[1,1,1,1,3]{4,3,2,1,0:T(1,128)}, u32[]{:S(2)}) copy-start(s32[1,1,1,1,3]{4,3,2,1,0:T(1,128)} %param.8) | copy-start | bytes 40
  9.9 39.2 %collective-permute-start = (bf16[2,384,768]{2,1,0:T(8,128)(2,1)}, bf16[2,384,768]{2,1,0:T(8,128)(2,1)S(1)}, u32[]{:S(2)}, u32[]{:S(2)}) collective-permute-start(bf16[2,384,768]{2,1,0:T(8,128)(2,1)} %shard_map.64.k_ref.v_ref), channel_id=1, source_target_pairs={{0,2},{2,4},{4,6},{6,8},{8,10},{10,12},{12,14},{14,16},{16,18},{18... | collective-permute-start | bytes 3538952 | tf_op jit(solution)/shard_map/ppermute | solution.py:133
  15.0 57.0 %collective-permute-start.1 = (bf16[2,384,768]{2,1,0:T(8,128)(2,1)}, bf16[2,384,768]{2,1,0:T(8,128)(2,1)S(1)}, u32[]{:S(2)}, u32[]{:S(2)}) collective-permute-start(bf16[2,384,768]{2,1,0:T(8,128)(2,1)} %shard_map.64.k_ref.v_ref), channel_id=1, source_target_pairs={{2,0},{4,2},{6,4},{8,6},{10,8},{12,10},{14,12},{16,14},{18,16},{20... | collective-permute-start | bytes 3538952 | tf_op jit(solution)/shard_map/ppermute | solution.py:134
  49.1 25.5 %copy-start.1 = (bf16[2,384,768]{2,1,0:T(8,128)(2,1)}, bf16[2,384,768]{2,1,0:T(8,128)(2,1)S(1)}, u32[]{:S(2)}) copy-start(bf16[2,384,768]{2,1,0:T(8,128)(2,1)S(1)} %collective-permute-done.kp_ref.vp_ref) | copy-start | bytes 3538948
  72.1 2.6 %copy-start.2 = (bf16[2,384,768]{2,1,0:T(8,128)(2,1)}, bf16[2,384,768]{2,1,0:T(8,128)(2,1)S(1)}, u32[]{:S(2)}) copy-start(bf16[2,384,768]{2,1,0:T(8,128)(2,1)S(1)} %collective-permute-done.1.kn_ref.vn_ref) | copy-start | bytes 3538948
  74.6 16.6 %collective-permute-start.2 = (bf16[192,1536]{1,0:T(8,128)(2,1)}, bf16[192,1536]{1,0:T(8,128)(2,1)S(1)}, u32[]{:S(2)}, u32[]{:S(2)}) collective-permute-start(bf16[192,1536]{1,0:T(8,128)(2,1)} %get-tuple-element.25), channel_id=1, source_target_pairs={{0,32},{32,2},{2,34},{34,4},{4,36},{36,6},{6,38},{38,0},{1,33},{33... | collective-permute-start | bytes 1769480 | tf_op jit(solution)/shard_map/ppermute | solution.py:158
  76.5 15.2 %collective-permute-start.3 = (bf16[192,1536]{1,0:T(8,128)(2,1)S(1)}, bf16[192,1536]{1,0:T(8,128)(2,1)S(1)}, u32[]{:S(2)}, u32[]{:S(2)}) collective-permute-start(bf16[192,1536]{1,0:T(8,128)(2,1)S(1)} %get-tuple-element.26), channel_id=1, source_target_pairs={{0,38},{32,0},{2,32},{34,2},{4,34},{36,4},{6,36},{38,6},{1,39},{33... | collective-permute-start | bytes 1769480 | tf_op jit(solution)/shard_map/ppermute | solution.py:159
  91.7 1.3 %copy-start = (bf16[384,1536]{1,0:T(8,128)(2,1)S(1)}, bf16[384,1536]{1,0:T(8,128)(2,1)}, u32[]{:S(2)}) copy-start(bf16[384,1536]{1,0:T(8,128)(2,1)} %all-gather.2.cloned.1.call-done) | copy-start | bytes 3538948
  93.0 9.6 %copy-start.3 = (f32[1,1536]{1,0:T(1,128)S(1)}, f32[1,1536]{1,0:T(1,128)}, u32[]{:S(2)}) copy-start(f32[1,1536]{1,0:T(1,128)} %param.10) | copy-start | bytes 18436
  94.6 10.8 %collective-permute-start.4 = (f32[192,1536]{1,0:T(8,128)}, f32[192,1536]{1,0:T(8,128)}, u32[]{:S(2)}, u32[]{:S(2)}) collective-permute-start(f32[192,1536]{1,0:T(8,128)} %fusion.1), channel_id=1, source_target_pairs={{0,1},{1,0},{2,3},{3,2},{4,5},{5,4},{6,7},{7,6},{8,9},{9,8},{10,11... | collective-permute-start | bytes 3538952 | tf_op jit(solution)/shard_map/ppermute | solution.py:180
Sparse Core Ops, SparseCore 0:
  9.7 60.4 all-gather.1

commit v11 on v10

--- a/solution.py
+++ b/solution.py
@@ -122,6 +122,28 @@
     )(flags, q, kv_prev, kv_prev, kv_next, kv_next, m_c, l_c, acc_c)
 
 
+def shifted(x, axis, count, shift):
+    return lax.ppermute(x, axis, [(i, (i + shift) % count) for i in range(count)])
+
+
+def gather_two_rounds(piece, axis):
+    count = lax.axis_size(axis)
+    here = lax.axis_index(axis)
+    rows = piece.shape[0]
+    block = jnp.concatenate(
+        [shifted(piece, axis, count, 1), piece, shifted(piece, axis, count, -1)], axis=0
+    )
+    whole = jnp.zeros((count * rows,) + piece.shape[1:], piece.dtype)
+    for shift in (0, 3, -3, 6):
+        moved = block if shift == 0 else shifted(block, axis, count, shift)
+        for j in range(3):
+            at = (here - shift + j - 1 + 2 * count) % count
+            whole = lax.dynamic_update_slice_in_dim(
+                whole, moved[j * rows:(j + 1) * rows], at * rows, axis=0
+            )
+    return whole
+
+
 def local(queries, keys_values, window_offsets, out_weight, gate):
     tl = queries.shape[4]
     all_time = lax.axis_size(TM)
@@ -134,7 +156,8 @@
     kv_next = lax.ppermute(kv, TM, backward)
 
     zs = lax.axis_size("z")
-    own_rows = lax.all_gather(out_weight, "z", axis=0, tiled=True)
+    piece, kv = lax.optimization_barrier((out_weight, kv))
+    own_rows = gather_two_rounds(piece, "z")
 
     offsets = window_offsets[0, 0, 0, 0]
     near_t = time_now + offsets // 9 - 1

time: 115 us -> 120 us (1.043)
  the two profiles are of different devices: /device:TPU:1 before, /device:TPU:223 now
where the time goes in v11:
time: 120 us; the launch traced here: 119 us
  starting transfers between devices  46.6 us (39%)
  waiting for transfers between devices  32.3 us (27%)
  Pallas kernels  18 us (15%)
  local copies, waits for them, and re-layouts  11.2 us (9%)
  matrix products  7.12 us (6%)
  other arithmetic  2.99 us (2%)
    ppermute x5, waiting for transfers between devices, shifted(): lax.ppermute(x, axis, [(i, (i + shift) % count) for i in range(count)])  31.1 us
    ppermute x5, starting transfers between devices, shifted(): lax.ppermute(x, axis, [(i, (i + shift) % count) for i in range(count)])  25.8 us
    pallas_call x1, Pallas kernels, attend_sides(): pl.pallas_call(side_kernel, grid_spec=pltpu.PrefetchScalarGridSpec(num_sc...  8.67 us
    ppermute x1, starting transfers between devices, local(): got = lax.ppermute(sent, ROWS, [(0, 1), (1, 0)])  6.99 us
    pallas_call x1, Pallas kernels, attend_centre(): pl.pallas_call(centre_kernel, grid_spec=pltpu.PrefetchScalarGridSpec(num_...  6.73 us
    ppermute x1, starting transfers between devices, local(): from_below = lax.ppermute(own_rows[:half], Y, up)  5.41 us
    ppermute x1, starting transfers between devices, local(): kv_prev = lax.ppermute(kv, TM, forward)  4.53 us
    unnamed x18, local copies, waits for them, and re-layouts  4.11 us
  transfers between devices with their start and end apart: 10, of which 4 were waited for; matrix products, arithmetic and copies ran while one was open for 12% of the time, Pallas kernels for 13%

profile of v11, /device:TPU:223, one launch (start us, length us, event | category | flops | bytes accessed | tf_op | source)
XLA Modules:
  0.0 118.7 jit_solution(18137156450662477571)
XLA Ops:
  0.0 0.0 copy-start.6
  0.0 2.6 %shard_map.64.k_ref.v_ref = bf16[2,384,768]{2,1,0:T(8,128)(2,1)} custom-call(bf16[384,2,768]{2,1,0:T(2,128)(2,1)} %bitcast.53), custom_call_target="tpu_custom_call" | custom-call | bytes 2359296 | tf_op jit(solution)/shard_map/pallas_call | solution.py:64
  2.6 0.0 copy-start.7
  2.6 5.3 %collective-permute-start = (bf16[32,1536]{1,0:T(8,128)(2,1)}, bf16[32,1536]{1,0:T(8,128)(2,1)}, u32[]{:S(2)}, u32[]{:S(2)}) collective-permute-start(bf16[32,1536]{1,0:T(8,128)(2,1)} %param.9), channel_id=1, source_target_pairs={{0,64},{64,128},{128,192},{192,256},{256,320},{320,384},{384,448},... | collective-permute-start | bytes 294920 | tf_op jit(solution)/shard_map/ppermute | solution.py:126
  8.0 1.9 %collective-permute-start.1 = (bf16[32,1536]{1,0:T(8,128)(2,1)}, bf16[32,1536]{1,0:T(8,128)(2,1)}, u32[]{:S(2)}, u32[]{:S(2)}) collective-permute-start(bf16[32,1536]{1,0:T(8,128)(2,1)} %param.9), channel_id=1, source_target_pairs={{0,704},{64,0},{128,64},{192,128},{256,192},{320,256},{384,320},{4... | collective-permute-start | bytes 294920 | tf_op jit(solution)/shard_map/ppermute | solution.py:126
  9.9 4.5 %collective-permute-start.5 = (bf16[2,384,768]{2,1,0:T(8,128)(2,1)}, bf16[2,384,768]{2,1,0:T(8,128)(2,1)S(1)}, u32[]{:S(2)}, u32[]{:S(2)}) collective-permute-start(bf16[2,384,768]{2,1,0:T(8,128)(2,1)} %shard_map.64.k_ref.v_ref), channel_id=1, source_target_pairs={{0,2},{2,4},{4,6},{6,8},{8,10},{10,12},{12,14},{14,16},{16,18},{18... | collective-permute-start | bytes 3538952 | tf_op jit(solution)/shard_map/ppermute | solution.py:155
  14.4 1.9 %collective-permute-start.6 = (bf16[2,384,768]{2,1,0:T(8,128)(2,1)}, bf16[2,384,768]{2,1,0:T(8,128)(2,1)S(1)}, u32[]{:S(2)}, u32[]{:S(2)}) collective-permute-start(bf16[2,384,768]{2,1,0:T(8,128)(2,1)} %shard_map.64.k_ref.v_ref), channel_id=1, source_target_pairs={{2,0},{4,2},{6,4},{8,6},{10,8},{12,10},{14,12},{16,14},{18,16},{20... | collective-permute-start | bytes 3538952 | tf_op jit(solution)/shard_map/ppermute | solution.py:156
  16.4 0.0 copy-done.6
  16.6 0.0 collective-permute-done
  16.6 0.1 broadcast_in_dim.2
  16.7 1.6 %constant_dynamic-update-slice_fusion.2 = (bf16[96,1536]{1,0:T(8,128)(2,1)}, bf16[384,1536]{1,0:T(8,128)(2,1)S(1)}) fusion(bf16[32,1536]{1,0:T(8,128)(2,1)} %collective-permute-done, bf16[384,1536]{1,0:T(8,128)(2,1)S(1)} %broadcast_in_dim.2, s32[]{:T(128)S(6)} %select_n.144), kind=kLoop, calls=%fused_computation.27 | loop fusion | bytes 294916
  18.3 1.5 %constant_dynamic-update-slice_fusion.1 = (bf16[96,1536]{1,0:T(8,128)(2,1)}, bf16[384,1536]{1,0:T(8,128)(2,1)S(1)}) fusion(bf16[96,1536]{1,0:T(8,128)(2,1)} %get-tuple-element.37, bf16[32,1536]{1,0:T(8,128)(2,1)} %param.9, bf16[384,1536]{1,0:T(8,128)(2,1)S(1)} %get-tuple-element.38, s32[]{:T(128)S(6)} %select_n.146), kind=kLoop, calls=%fused_computation.26 | loop fusion | bytes 294916
  19.8 0.0 collective-permute-done.1
  19.8 1.5 %constant_dynamic-update-slice_fusion = (bf16[96,1536]{1,0:T(8,128)(2,1)}, bf16[384,1536]{1,0:T(8,128)(2,1)S(1)}) fusion(bf16[96,1536]{1,0:T(8,128)(2,1)} %get-tuple-element.35, bf16[32,1536]{1,0:T(8,128)(2,1)} %collective-permute-done.1, bf16[384,1536]{1,0:T(8,128)(2,1)S(1)} %get-tuple-element.36, s32[]{:T(128)S(6)} %select_n.148), kind=kLoop, calls=%fused_computation.25 | loop fusion | bytes 294916 | tf_op jit(solution)/shard_map/concatenate | solution.py:133
  21.4 7.3 %collective-permute-start.2 = (bf16[96,1536]{1,0:T(8,128)(2,1)}, bf16[96,1536]{1,0:T(8,128)(2,1)}, u32[]{:S(2)}, u32[]{:S(2)}) collective-permute-start(bf16[96,1536]{1,0:T(8,128)(2,1)} %get-tuple-element.33), channel_id=1, source_target_pairs={{0,192},{64,256},{128,320},{192,384},{256,448},{320,512},{384,576}... | collective-permute-start | bytes 884744 | tf_op jit(solution)/shard_map/ppermute | solution.py:126
  28.7 0.0 copy-done.7
  28.7 0.2 and_reduce_fusion
  28.9 0.5 convert_element_type.6.flags_ref
  29.4 6.7 %shard_map.65 = (f32[6,384,1]{2,1,0:T(8,128)}, f32[6,384,1]{2,1,0:T(8,128)}, f32[384,768]{1,0:T(8,128)}) custom-call(s32[3]{0:T(128)} %convert_element_type.6.flags_ref, bf16[384,768]{1,0:T(8,128)(2,1)} %bitcast.44, bf16[2,384,768]{2,1,0:T(8,128)(2,1)} %shard_map.64.k_ref.v_ref, bf16[2,384,768]{2,1,0:T(8,128)(2,1)} %shard_map.64.k_ref.v_ref), custom_call_target="tpu_custom_call" | custom-call | flops 452984832 | bytes 2949120 | tf_op jit(solution)/shard_map/pallas_call | solution.py:82
  36.1 3.1 %collective-permute-start.3 = (bf16[96,1536]{1,0:T(8,128)(2,1)}, bf16[96,1536]{1,0:T(8,128)(2,1)S(1)}, u32[]{:S(2)}, u32[]{:S(2)}) collective-permute-start(bf16[96,1536]{1,0:T(8,128)(2,1)} %get-tuple-element.33), channel_id=1, source_target_pairs={{0,576},{64,640},{128,704},{192,0},{256,64},{320,128},{384,192},{4... | collective-permute-start | bytes 884744 | tf_op jit(solution)/shard_map/ppermute | solution.py:126
  39.3 8.1 %collective-permute-start.4 = (bf16[96,1536]{1,0:T(8,128)(2,1)}, bf16[96,1536]{1,0:T(8,128)(2,1)S(1)}, u32[]{:S(2)}, u32[]{:S(2)}) collective-permute-start(bf16[96,1536]{1,0:T(8,128)(2,1)} %get-tuple-element.33), channel_id=1, source_target_pairs={{0,384},{64,448},{128,512},{192,576},{256,640},{320,704},{384,0},{... | collective-permute-start | bytes 884744 | tf_op jit(solution)/shard_map/ppermute | solution.py:126
  47.4 2.0 %collective-permute-done.2 = bf16[96,1536]{1,0:T(8,128)(2,1)} collective-permute-done((bf16[96,1536]{1,0:T(8,128)(2,1)}, bf16[96,1536]{1,0:T(8,128)(2,1)}, u32[]{:S(2)}, u32[]{:S(2)}) %collective-permute-start.2) | collective-permute-done | bytes 294944 | tf_op jit(solution)/shard_map/ppermute | solution.py:126
  49.4 0.9 slice_dynamic-update-slice_fusion.8
  50.3 0.9 slice_dynamic-update-slice_fusion.7
  51.2 0.9 slice_dynamic-update-slice_fusion.6
  52.1 14.7 %collective-permute-done.3 = bf16[96,1536]{1,0:T(8,128)(2,1)S(1)} collective-permute-done((bf16[96,1536]{1,0:T(8,128)(2,1)}, bf16[96,1536]{1,0:T(8,128)(2,1)S(1)}, u32[]{:S(2)}, u32[]{:S(2)}) %collective-permute-start.3) | collective-permute-done | bytes 294944 | tf_op jit(solution)/shard_map/ppermute | solution.py:126
  66.9 14.4 %collective-permute-done.4 = bf16[96,1536]{1,0:T(8,128)(2,1)S(1)} collective-permute-done((bf16[96,1536]{1,0:T(8,128)(2,1)}, bf16[96,1536]{1,0:T(8,128)(2,1)S(1)}, u32[]{:S(2)}, u32[]{:S(2)}) %collective-permute-start.4) | collective-permute-done | bytes 294944 | tf_op jit(solution)/shard_map/ppermute | solution.py:126
  81.3 0.0 collective-permute-done.5.kp_ref.vp_ref
  81.4 0.0 copy-start
  81.4 0.0 collective-permute-done.6.kn_ref.vn_ref
  81.4 0.0 copy-start.1
  81.4 1.2 %fusion.19 = (bf16[192,1536]{1,0:T(8,128)(2,1)}, bf16[192,1536]{1,0:T(8,128)(2,1)}) fusion(bf16[384,1536]{1,0:T(8,128)(2,1)S(1)} %slice_dynamic-update-slice_fusion), kind=kLoop, calls=%fused_computation.47 | loop fusion | bytes 2359296 | tf_op jit(solution)/shard_map/slice | solution.py:181
  82.6 0.1 copy-done
  82.8 0.4 copy-done.1
  83.2 5.4 %collective-permute-start.7 = (bf16[192,1536]{1,0:T(8,128)(2,1)}, bf16[192,1536]{1,0:T(8,128)(2,1)S(1)}, u32[]{:S(2)}, u32[]{:S(2)}) collective-permute-start(bf16[192,1536]{1,0:T(8,128)(2,1)} %get-tuple-element.29), channel_id=1, source_target_pairs={{0,32},{32,2},{2,34},{34,4},{4,36},{36,6},{6,38},{38,0},{1,33},{33... | collective-permute-start | bytes 1769480 | tf_op jit(solution)/shard_map/ppermute | solution.py:181
  88.6 1.9 %collective-permute-start.8 = (bf16[192,1536]{1,0:T(8,128)(2,1)}, bf16[192,1536]{1,0:T(8,128)(2,1)}, u32[]{:S(2)}, u32[]{:S(2)}) collective-permute-start(bf16[192,1536]{1,0:T(8,128)(2,1)} %get-tuple-element.30), channel_id=1, source_target_pairs={{0,38},{32,0},{2,32},{34,2},{4,34},{36,4},{6,36},{38,6},{1,39},{33... | collective-permute-start | bytes 1769480 | tf_op jit(solution)/shard_map/ppermute | solution.py:182
  90.5 8.7 %shard_map.66 = bf16[384,768]{1,0:T(8,128)(2,1)} custom-call(s32[3]{0:T(128)} %convert_element_type.6.flags_ref, bf16[384,768]{1,0:T(8,128)(2,1)} %bitcast.45, bf16[2,384,768]{2,1,0:T(8,128)(2,1)} %copy-done, bf16[2,384,768]{2,1,0:T(8,128)(2,1)} %copy-done, bf16[2,384,768]{2,1,0:T(8,128)(2,1)} %copy-done.1, bf16[2,384,768]{2,1,0:T(8,128)(2,1)} %copy-done.1, ...), custom_call_target="tpu_custom_call" | custom-call | flops 905969664 | bytes 4718592 | tf_op jit(solution)/shard_map/pallas_call | solution.py:108
  99.2 1.4 %copy.8 = bf16[384,768]{0,1:T(8,128)(2,1)S(1)} copy(bf16[384,768]{1,0:T(8,128)(2,1)} %shard_map.66) | data formatting | bytes 1179648 | tf_op jit(solution)/shard_map/pallas_call | solution.py:108
  100.6 0.1 constant_dynamic-slice_fusion.1
  100.7 0.0 copy-start.3
  100.7 0.0 collective-permute-done.7
  100.7 0.0 copy-start.2
  100.7 0.4 fusion.7
  101.1 0.4 copy-done.2
  101.5 1.1 collective-permute-done.8
  102.7 1.5 %fusion.5 = f32[192,1536]{1,0:T(8,128)S(1)} fusion(bf16[192,1536]{1,0:T(8,128)(2,1)} %collective-permute-done.8, bf16[384,384]{0,1:T(8,128)(2,1)S(1)} %bitcast.50, s32[]{:T(128)S(6)} %select_n.170, s32[]{:T(128)S(6)} %add.331), kind=kOutput, calls=%fused_computation.8 | convolution fusion | flops 113246208 | bytes 1867784 | tf_op jit(solution)/shard_map/dot_general | solution.py:200
  104.1 0.0 copy-done.3
  104.1 0.0 copy-start.5
  104.2 1.6 %fusion.1 = f32[192,1536]{1,0:T(8,128)} fusion(f32[192,1536]{1,0:T(8,128)S(1)} %fusion.5, f32[192,1536]{1,0:T(8,128)S(1)} %fusion.7, bf16[384,1536]{1,0:T(8,128)(2,1)S(1)} %slice_dynamic-update-slice_fusion, bf16[384,384]{0,1:T(8,128)(2,1)S(1)} %bitcast.47, s32[]{:T(128)S(6)} %select_n.170), kind=kOutput, calls=%fused_computation.3 | convolution fusion | flops 227082240 | bytes 4915204 | tf_op jit(solution)/shard_map/dot_general | solution.py:198
  105.8 7.0 %collective-permute-start.9 = (f32[192,1536]{1,0:T(8,128)}, f32[192,1536]{1,0:T(8,128)}, u32[]{:S(2)}, u32[]{:S(2)}) collective-permute-start(f32[192,1536]{1,0:T(8,128)} %fusion.1), channel_id=1, source_target_pairs={{0,1},{1,0},{2,3},{3,2},{4,5},{5,4},{6,7},{7,6},{8,9},{9,8},{10,11... | collective-permute-start | bytes 3538952 | tf_op jit(solution)/shard_map/ppermute | solution.py:203
  112.8 0.0 copy-done.5
  112.8 1.5 %fusion.11 = f32[192,1536]{1,0:T(8,128)S(1)} fusion(bf16[192,1536]{1,0:T(8,128)(2,1)} %copy-done.2, bf16[384,384]{0,1:T(8,128)(2,1)S(1)} %bitcast.51, s32[]{:T(128)S(6)} %select_n.168), kind=kOutput, calls=%fused_computation.14 | convolution fusion | flops 113246208 | bytes 1867780 | tf_op jit(solution)/shard_map/dot_general | solution.py:199
  114.3 0.0 copy-start.4
  114.3 1.5 %fusion.9 = f32[192,1536]{1,0:T(8,128)S(1)} fusion(bf16[192,1536]{1,0:T(8,128)(2,1)} %collective-permute-done.8, bf16[384,384]{0,1:T(8,128)(2,1)S(1)} %bitcast.52, s32[]{:T(128)S(6)} %select_n.168, s32[]{:T(128)S(6)} %add.331), kind=kOutput, calls=%fused_computation.12 | convolution fusion | flops 113246208 | bytes 1867784 | tf_op jit(solution)/shard_map/dot_general | solution.py:200
  115.9 0.0 copy-done.4
  115.9 0.6 fusion
  116.5 0.0 collective-permute-done.9
  116.5 2.3 %fusion.2 = bf16[1,1,1,1,192,1536]{5,4,3,2,1,0:T(8,128)(2,1)} fusion(f32[192,1536]{1,0:T(8,128)S(1)} %fusion, f32[192,1536]{1,0:T(8,128)} %collective-permute-done.9, f32[1536]{0:T(1024)S(1)} %reduce), kind=kLoop, calls=%fused_computation.5 | loop fusion | flops 884736 | bytes 2955264 | tf_op jit(solution)/shard_map/reshape | solution.py:207
  (9 shorter events, 0.1 us)
Async XLA Ops:
  0.0 16.4 %copy-start.6 = (s32[1,1,1,1,3]{4,3,2,1,0:T(1,128)S(1)}, s32[1,1,1,1,3]{4,3,2,1,0:T(1,128)}, u32[]{:S(2)}) copy-start(s32[1,1,1,1,3]{4,3,2,1,0:T(1,128)} %param.8) | copy-start | bytes 40
  2.6 26.1 %copy-start.7 = (s32[3]{0:T(128)S(1)}, s32[3]{0:T(128)}, u32[]{:S(2)}) copy-start(s32[3]{0:T(128)} %constant.168.clone) | copy-start | bytes 40
  2.6 14.0 %collective-permute-start = (bf16[32,1536]{1,0:T(8,128)(2,1)}, bf16[32,1536]{1,0:T(8,128)(2,1)}, u32[]{:S(2)}, u32[]{:S(2)}) collective-permute-start(bf16[32,1536]{1,0:T(8,128)(2,1)} %param.9), channel_id=1, source_target_pairs={{0,64},{64,128},{128,192},{192,256},{256,320},{320,384},{384,448},... | collective-permute-start | bytes 294920 | tf_op jit(solution)/shard_map/ppermute | solution.py:126
  8.0 11.9 %collective-permute-start.1 = (bf16[32,1536]{1,0:T(8,128)(2,1)}, bf16[32,1536]{1,0:T(8,128)(2,1)}, u32[]{:S(2)}, u32[]{:S(2)}) collective-permute-start(bf16[32,1536]{1,0:T(8,128)(2,1)} %param.9), channel_id=1, source_target_pairs={{0,704},{64,0},{128,64},{192,128},{256,192},{320,256},{384,320},{4... | collective-permute-start | bytes 294920 | tf_op jit(solution)/shard_map/ppermute | solution.py:126
  9.9 71.5 %collective-permute-start.5 = (bf16[2,384,768]{2,1,0:T(8,128)(2,1)}, bf16[2,384,768]{2,1,0:T(8,128)(2,1)S(1)}, u32[]{:S(2)}, u32[]{:S(2)}) collective-permute-start(bf16[2,384,768]{2,1,0:T(8,128)(2,1)} %shard_map.64.k_ref.v_ref), channel_id=1, source_target_pairs={{0,2},{2,4},{4,6},{6,8},{8,10},{10,12},{12,14},{14,16},{16,18},{18... | collective-permute-start | bytes 3538952 | tf_op jit(solution)/shard_map/ppermute | solution.py:155
  14.4 67.0 %collective-permute-start.6 = (bf16[2,384,768]{2,1,0:T(8,128)(2,1)}, bf16[2,384,768]{2,1,0:T(8,128)(2,1)S(1)}, u32[]{:S(2)}, u32[]{:S(2)}) collective-permute-start(bf16[2,384,768]{2,1,0:T(8,128)(2,1)} %shard_map.64.k_ref.v_ref), channel_id=1, source_target_pairs={{2,0},{4,2},{6,4},{8,6},{10,8},{12,10},{14,12},{16,14},{18,16},{20... | collective-permute-start | bytes 3538952 | tf_op jit(solution)/shard_map/ppermute | solution.py:156
  21.4 28.0 %collective-permute-start.2 = (bf16[96,1536]{1,0:T(8,128)(2,1)}, bf16[96,1536]{1,0:T(8,128)(2,1)}, u32[]{:S(2)}, u32[]{:S(2)}) collective-permute-start(bf16[96,1536]{1,0:T(8,128)(2,1)} %get-tuple-element.33), channel_id=1, source_target_pairs={{0,192},{64,256},{128,320},{192,384},{256,448},{320,512},{384,576}... | collective-permute-start | bytes 884744 | tf_op jit(solution)/shard_map/ppermute | solution.py:126
  36.1 30.7 %collective-permute-start.3 = (bf16[96,1536]{1,0:T(8,128)(2,1)}, bf16[96,1536]{1,0:T(8,128)(2,1)S(1)}, u32[]{:S(2)}, u32[]{:S(2)}) collective-permute-start(bf16[96,1536]{1,0:T(8,128)(2,1)} %get-tuple-element.33), channel_id=1, source_target_pairs={{0,576},{64,640},{128,704},{192,0},{256,64},{320,128},{384,192},{4... | collective-permute-start | bytes 884744 | tf_op jit(solution)/shard_map/ppermute | solution.py:126
  39.3 42.0 %collective-permute-start.4 = (bf16[96,1536]{1,0:T(8,128)(2,1)}, bf16[96,1536]{1,0:T(8,128)(2,1)S(1)}, u32[]{:S(2)}, u32[]{:S(2)}) collective-permute-start(bf16[96,1536]{1,0:T(8,128)(2,1)} %get-tuple-element.33), channel_id=1, source_target_pairs={{0,384},{64,448},{128,512},{192,576},{256,640},{320,704},{384,0},{... | collective-permute-start | bytes 884744 | tf_op jit(solution)/shard_map/ppermute | solution.py:126
  81.4 1.4 %copy-start = (bf16[2,384,768]{2,1,0:T(8,128)(2,1)}, bf16[2,384,768]{2,1,0:T(8,128)(2,1)S(1)}, u32[]{:S(2)}) copy-start(bf16[2,384,768]{2,1,0:T(8,128)(2,1)S(1)} %collective-permute-done.5.kp_ref.vp_ref) | copy-start | bytes 3538948
  81.4 1.8 %copy-start.1 = (bf16[2,384,768]{2,1,0:T(8,128)(2,1)}, bf16[2,384,768]{2,1,0:T(8,128)(2,1)S(1)}, u32[]{:S(2)}) copy-start(bf16[2,384,768]{2,1,0:T(8,128)(2,1)S(1)} %collective-permute-done.6.kn_ref.vn_ref) | copy-start | bytes 3538948
  83.2 17.5 %collective-permute-start.7 = (bf16[192,1536]{1,0:T(8,128)(2,1)}, bf16[192,1536]{1,0:T(8,128)(2,1)S(1)}, u32[]{:S(2)}, u32[]{:S(2)}) collective-permute-start(bf16[192,1536]{1,0:T(8,128)(2,1)} %get-tuple-element.29), channel_id=1, source_target_pairs={{0,32},{32,2},{2,34},{34,4},{4,36},{36,6},{6,38},{38,0},{1,33},{33... | collective-permute-start | bytes 1769480 | tf_op jit(solution)/shard_map/ppermute | solution.py:181
  88.6 14.1 %collective-permute-start.8 = (bf16[192,1536]{1,0:T(8,128)(2,1)}, bf16[192,1536]{1,0:T(8,128)(2,1)}, u32[]{:S(2)}, u32[]{:S(2)}) collective-permute-start(bf16[192,1536]{1,0:T(8,128)(2,1)} %get-tuple-element.30), channel_id=1, source_target_pairs={{0,38},{32,0},{2,32},{34,2},{4,34},{36,4},{6,36},{38,6},{1,39},{33... | collective-permute-start | bytes 1769480 | tf_op jit(solution)/shard_map/ppermute | solution.py:182
  100.7 3.5 %copy-start.3 = (bf16[384,12,1,32]{0,3,2,1:T(8,128)(2,1)}, bf16[384,12,1,32]{0,3,2,1:T(8,128)(2,1)S(1)}, u32[]{:S(2)}) copy-start(bf16[384,12,1,32]{0,3,2,1:T(8,128)(2,1)S(1)} %get-tuple-element.31) | copy-start | bytes 884740
  100.7 0.9 copy-start.2
  104.1 8.7 %copy-start.5 = (f32[1,1536]{1,0:T(1,128)S(1)}, f32[1,1536]{1,0:T(1,128)}, u32[]{:S(2)}) copy-start(f32[1,1536]{1,0:T(1,128)} %param.10) | copy-start | bytes 18436
  105.8 10.7 %collective-permute-start.9 = (f32[192,1536]{1,0:T(8,128)}, f32[192,1536]{1,0:T(8,128)}, u32[]{:S(2)}, u32[]{:S(2)}) collective-permute-start(f32[192,1536]{1,0:T(8,128)} %fusion.1), channel_id=1, source_target_pairs={{0,1},{1,0},{2,3},{3,2},{4,5},{5,4},{6,7},{7,6},{8,9},{9,8},{10,11... | collective-permute-start | bytes 3538952 | tf_op jit(solution)/shard_map/ppermute | solution.py:203
  114.3 1.5 %copy-start.4 = (bf16[384,12,1,32]{0,3,2,1:T(8,128)(2,1)S(1)}, bf16[384,12,1,32]{0,3,2,1:T(8,128)(2,1)}, u32[]{:S(2)}) copy-start(bf16[384,12,1,32]{0,3,2,1:T(8,128)(2,1)} %copy-done.3) | copy-start | bytes 884740

commit v12 on v9

--- a/solution.py
+++ b/solution.py
@@ -178,10 +178,10 @@
         part = part + jnp.dot(far[:, :half], from_below, preferred_element_type=jnp.float32)
         return part + jnp.dot(far[:, half:], from_above, preferred_element_type=jnp.float32)
 
-    sent = project((1 - me) * band)
+    sent = project((1 - me) * band).astype(jnp.bfloat16)
     got = lax.ppermute(sent, ROWS, [(0, 1), (1, 0)])
     kept = lax.optimization_barrier(project(me * band))
-    projection = kept + got
+    projection = kept + got.astype(jnp.float32)
     mixed = (gate[0][None, :] * projection).astype(jnp.bfloat16)
     return mixed.reshape(1, 1, 1, 1, band, DOUT)
 

time: 113 us -> 109 us (0.965)
  waiting for transfers between devices: 52.2 us -> 50.8 us
  other arithmetic: 3.12 us -> 1.78 us
    reshape x1, other arithmetic: 2.3 us -> 0.96 us  [local(): return mixed.reshape(1, 1, 1, 1, band, DOUT)]
where the time goes in v12:
time: 109 us
  waiting for transfers between devices  50.8 us (47%)
  starting transfers between devices  31.3 us (29%)
  Pallas kernels  18.1 us (17%)
  local copies, waits for them, and re-layouts  3.54 us (3%)
  matrix products  2.84 us (3%)
  other arithmetic  1.78 us (2%)
    ppermute x1, waiting for transfers between devices, local(): kv_prev = lax.ppermute(kv, TM, forward)  32.3 us
    ppermute x1, waiting for transfers between devices, local(): kv_next = lax.ppermute(kv, TM, backward)  15.9 us
    all_to_all x1, starting transfers between devices, local(): lax.all_to_all(spread, 'z', 0, 0, tiled=True)  15.8 us
    pallas_call x1, Pallas kernels, attend_sides(): pl.pallas_call(side_kernel, grid_spec=pltpu.PrefetchScalarGridSpec(num_sc...  8.68 us
    pallas_call x1, Pallas kernels, attend_centre(): pl.pallas_call(centre_kernel, grid_spec=pltpu.PrefetchScalarGridSpec(num_...  6.77 us
    ppermute x1, starting transfers between devices, local(): from_above = lax.ppermute(own_rows[half:], Y, down)  4.57 us
    ppermute x1, starting transfers between devices, local(): kv_prev = lax.ppermute(kv, TM, forward)  4.29 us
    ppermute x1, starting transfers between devices, local(): got = lax.ppermute(sent, ROWS, [(0, 1), (1, 0)])  3.39 us
  transfers between devices with their start and end apart: 6, of which 5 were waited for; matrix products, arithmetic and copies ran while one was open for 4% of the time, Pallas kernels for 14%

profile of v12, /device:TPU:1, one launch (start us, length us, event | category | flops | bytes accessed | tf_op | source)
XLA Modules:
  0.0 108.5 jit_solution(17184471656999866306)
XLA Ops:
  0.0 0.0 copy-start.2
  0.0 2.6 %shard_map.64.k_ref.v_ref = bf16[2,384,768]{2,1,0:T(8,128)(2,1)} custom-call(bf16[384,2,768]{2,1,0:T(2,128)(2,1)} %bitcast.57), custom_call_target="tpu_custom_call" | custom-call | bytes 2359296 | tf_op jit(solution)/shard_map/pallas_call | solution.py:64
  2.6 0.0 copy-done.2
  2.6 1.2 %broadcast_in_dim.2 = bf16[12,32,1536]{2,1,0:T(8,128)(2,1)} broadcast(bf16[32,1536]{1,0:T(8,128)(2,1)S(1)} %copy-done.2), dimensions={1,2} | broadcast | bytes 1277952 | tf_op jit(solution)/shard_map/broadcast_in_dim | solution.py:137
  3.8 0.0 copy-start
  3.8 0.0 copy-start.5
  3.8 0.0 copy-start.4
  3.8 15.8 %all-to-all-start = ((bf16[12,32,1536]{2,1,0:T(8,128)(2,1)}), bf16[12,32,1536]{2,1,0:T(8,128)(2,1)S(1)}, u32[]{:S(2)}, u32[]{:S(2)}) async-start(bf16[12,32,1536]{2,1,0:T(8,128)(2,1)} %broadcast_in_dim.2), calls=%async_computation | async-start | bytes 2359296 | tf_op jit(solution)/shard_map/all_to_all | solution.py:139
  19.7 0.0 copy-done
  19.7 4.3 %collective-permute-start = (bf16[2,384,768]{2,1,0:T(8,128)(2,1)S(1)}, bf16[2,384,768]{2,1,0:T(8,128)(2,1)S(1)}, u32[]{:S(2)}, u32[]{:S(2)}) collective-permute-start(bf16[2,384,768]{2,1,0:T(8,128)(2,1)S(1)} %copy-done), channel_id=1, source_target_pairs={{0,2},{2,4},{4,6},{6,8},{8,10},{10,12},{12,14},{14,16},{16,18},{18... | collective-permute-start | bytes 3538952 | tf_op jit(solution)/shard_map/ppermute | solution.py:133
  24.0 1.3 %collective-permute-start.1 = (bf16[2,384,768]{2,1,0:T(8,128)(2,1)S(1)}, bf16[2,384,768]{2,1,0:T(8,128)(2,1)}, u32[]{:S(2)}, u32[]{:S(2)}) collective-permute-start(bf16[2,384,768]{2,1,0:T(8,128)(2,1)S(1)} %copy-done), channel_id=1, source_target_pairs={{2,0},{4,2},{6,4},{8,6},{10,8},{12,10},{14,12},{16,14},{18,16},{20... | collective-permute-start | bytes 3538952 | tf_op jit(solution)/shard_map/ppermute | solution.py:134
  25.3 0.0 copy-done.5
  25.3 0.0 copy-done.4
  25.3 0.2 and_reduce_fusion
  25.5 0.6 convert_element_type.12.flags_ref
  26.1 6.8 %shard_map.65 = (f32[6,384,1]{2,1,0:T(8,128)}, f32[6,384,1]{2,1,0:T(8,128)}, f32[384,768]{1,0:T(8,128)}) custom-call(s32[3]{0:T(128)} %convert_element_type.12.flags_ref, bf16[384,768]{1,0:T(8,128)(2,1)} %bitcast.48, bf16[2,384,768]{2,1,0:T(8,128)(2,1)} %shard_map.64.k_ref.v_ref, bf16[2,384,768]{2,1,0:T(8,128)(2,1)} %shard_map.64.k_ref.v_ref), custom_call_target="tpu_custom_call" | custom-call | flops 452984832 | bytes 2949120 | tf_op jit(solution)/shard_map/pallas_call | solution.py:82
  32.9 32.3 %collective-permute-done.kp_ref.vp_ref = bf16[2,384,768]{2,1,0:T(8,128)(2,1)S(1)} collective-permute-done((bf16[2,384,768]{2,1,0:T(8,128)(2,1)S(1)}, bf16[2,384,768]{2,1,0:T(8,128)(2,1)S(1)}, u32[]{:S(2)}, u32[]{:S(2)}) %collective-permute-start) | collective-permute-done | bytes 1179680 | tf_op jit(solution)/shard_map/ppermute | solution.py:133
  65.2 0.0 copy-start.1
  65.2 15.9 %collective-permute-done.1.kn_ref.vn_ref = bf16[2,384,768]{2,1,0:T(8,128)(2,1)} collective-permute-done((bf16[2,384,768]{2,1,0:T(8,128)(2,1)S(1)}, bf16[2,384,768]{2,1,0:T(8,128)(2,1)}, u32[]{:S(2)}, u32[]{:S(2)}) %collective-permute-start.1) | collective-permute-done | bytes 1179680 | tf_op jit(solution)/shard_map/ppermute | solution.py:134
  81.0 0.0 all-to-all-done
  81.0 0.0 copy-start.3
  81.0 0.9 fusion.20
  81.9 0.0 copy-done.1
  81.9 1.9 %collective-permute-start.2 = (bf16[192,1536]{1,0:T(8,128)(2,1)}, bf16[192,1536]{1,0:T(8,128)(2,1)S(1)}, u32[]{:S(2)}, u32[]{:S(2)}) collective-permute-start(bf16[192,1536]{1,0:T(8,128)(2,1)} %get-tuple-element.29), channel_id=1, source_target_pairs={{0,32},{32,2},{2,34},{34,4},{4,36},{36,6},{6,38},{38,0},{1,33},{33... | collective-permute-start | bytes 1769480 | tf_op jit(solution)/shard_map/ppermute | solution.py:160
  83.8 4.6 %collective-permute-start.3 = (bf16[192,1536]{1,0:T(8,128)(2,1)S(1)}, bf16[192,1536]{1,0:T(8,128)(2,1)S(1)}, u32[]{:S(2)}, u32[]{:S(2)}) collective-permute-start(bf16[192,1536]{1,0:T(8,128)(2,1)S(1)} %get-tuple-element.30), channel_id=1, source_target_pairs={{0,38},{32,0},{2,32},{34,2},{4,34},{36,4},{6,36},{38,6},{1,39},{33... | collective-permute-start | bytes 1769480 | tf_op jit(solution)/shard_map/ppermute | solution.py:161
  88.4 0.0 copy-done.3
  88.5 8.7 %shard_map.66 = bf16[384,768]{1,0:T(8,128)(2,1)} custom-call(s32[3]{0:T(128)} %convert_element_type.12.flags_ref, bf16[384,768]{1,0:T(8,128)(2,1)} %bitcast.49, bf16[2,384,768]{2,1,0:T(8,128)(2,1)} %copy-done.1, bf16[2,384,768]{2,1,0:T(8,128)(2,1)} %copy-done.1, bf16[2,384,768]{2,1,0:T(8,128)(2,1)} %collective-permute-done.1.kn_ref.vn_ref, ...), custom_call_target="tpu_custom_call" | custom-call | flops 905969664 | bytes 4718592 | tf_op jit(solution)/shard_map/pallas_call | solution.py:108
  97.1 1.4 %copy.8 = bf16[384,768]{0,1:T(8,128)(2,1)S(1)} copy(bf16[384,768]{1,0:T(8,128)(2,1)} %shard_map.66) | data formatting | bytes 1179648 | tf_op jit(solution)/shard_map/pallas_call | solution.py:108
  98.5 0.1 constant_dynamic-slice_fusion.1
  98.6 0.9 collective-permute-done.2
  99.5 0.4 fusion.8
  99.9 1.6 %collective-permute-done.3 = bf16[192,1536]{1,0:T(8,128)(2,1)S(1)} collective-permute-done((bf16[192,1536]{1,0:T(8,128)(2,1)S(1)}, bf16[192,1536]{1,0:T(8,128)(2,1)S(1)}, u32[]{:S(2)}, u32[]{:S(2)}) %collective-permute-start.3) | collective-permute-done | bytes 589856 | tf_op jit(solution)/shard_map/ppermute | solution.py:161
  101.5 0.4 fusion.6
  102.0 0.6 fusion.2
  102.6 3.4 %collective-permute-start.4 = (bf16[192,1536]{1,0:T(8,128)(2,1)S(1)}, bf16[192,1536]{1,0:T(8,128)(2,1)S(1)}, u32[]{:S(2)}, u32[]{:S(2)}) collective-permute-start(bf16[192,1536]{1,0:T(8,128)(2,1)S(1)} %fusion.2), channel_id=1, source_target_pairs={{0,1},{1,0},{2,3},{3,2},{4,5},{5,4},{6,7},{7,6},{8,9},{9,8},{10,11... | collective-permute-start | bytes 1769480 | tf_op jit(solution)/shard_map/ppermute | solution.py:182
  106.0 0.4 fusion.12
  106.4 0.4 fusion.10
  106.8 0.6 fusion
  107.4 0.2 collective-permute-done.4
  107.6 1.0 fusion.3
  (3 shorter events, 0.1 us)
Async XLA Ops:
  0.0 2.6 %copy-start.2 = (bf16[32,1536]{1,0:T(8,128)(2,1)S(1)}, bf16[32,1536]{1,0:T(8,128)(2,1)}, u32[]{:S(2)}) copy-start(bf16[32,1536]{1,0:T(8,128)(2,1)} %param.9) | copy-start | bytes 294916
  3.8 15.9 %copy-start = (bf16[2,384,768]{2,1,0:T(8,128)(2,1)S(1)}, bf16[2,384,768]{2,1,0:T(8,128)(2,1)}, u32[]{:S(2)}) copy-start(bf16[2,384,768]{2,1,0:T(8,128)(2,1)} %shard_map.64.k_ref.v_ref) | copy-start | bytes 3538948
  3.8 21.5 %copy-start.5 = (s32[3]{0:T(128)S(1)}, s32[3]{0:T(128)}, u32[]{:S(2)}) copy-start(s32[3]{0:T(128)} %constant.69.clone) | copy-start | bytes 40
  3.8 21.5 %copy-start.4 = (s32[1,1,1,1,3]{4,3,2,1,0:T(1,128)S(1)}, s32[1,1,1,1,3]{4,3,2,1,0:T(1,128)}, u32[]{:S(2)}) copy-start(s32[1,1,1,1,3]{4,3,2,1,0:T(1,128)} %param.8) | copy-start | bytes 40
  3.8 77.2 %all-to-all-start = ((bf16[12,32,1536]{2,1,0:T(8,128)(2,1)}), bf16[12,32,1536]{2,1,0:T(8,128)(2,1)S(1)}, u32[]{:S(2)}, u32[]{:S(2)}) async-start(bf16[12,32,1536]{2,1,0:T(8,128)(2,1)} %broadcast_in_dim.2), calls=%async_computation | async-start | bytes 2359296 | tf_op jit(solution)/shard_map/all_to_all | solution.py:139
  19.7 45.5 %collective-permute-start = (bf16[2,384,768]{2,1,0:T(8,128)(2,1)S(1)}, bf16[2,384,768]{2,1,0:T(8,128)(2,1)S(1)}, u32[]{:S(2)}, u32[]{:S(2)}) collective-permute-start(bf16[2,384,768]{2,1,0:T(8,128)(2,1)S(1)} %copy-done), channel_id=1, source_target_pairs={{0,2},{2,4},{4,6},{6,8},{8,10},{10,12},{12,14},{14,16},{16,18},{18... | collective-permute-start | bytes 3538952 | tf_op jit(solution)/shard_map/ppermute | solution.py:133
  24.0 57.0 %collective-permute-start.1 = (bf16[2,384,768]{2,1,0:T(8,128)(2,1)S(1)}, bf16[2,384,768]{2,1,0:T(8,128)(2,1)}, u32[]{:S(2)}, u32[]{:S(2)}) collective-permute-start(bf16[2,384,768]{2,1,0:T(8,128)(2,1)S(1)} %copy-done), channel_id=1, source_target_pairs={{2,0},{4,2},{6,4},{8,6},{10,8},{12,10},{14,12},{16,14},{18,16},{20... | collective-permute-start | bytes 3538952 | tf_op jit(solution)/shard_map/ppermute | solution.py:134
  65.2 16.8 %copy-start.1 = (bf16[2,384,768]{2,1,0:T(8,128)(2,1)}, bf16[2,384,768]{2,1,0:T(8,128)(2,1)S(1)}, u32[]{:S(2)}) copy-start(bf16[2,384,768]{2,1,0:T(8,128)(2,1)S(1)} %collective-permute-done.kp_ref.vp_ref) | copy-start | bytes 3538948
  81.0 7.4 %copy-start.3 = (f32[1,1536]{1,0:T(1,128)S(1)}, f32[1,1536]{1,0:T(1,128)}, u32[]{:S(2)}) copy-start(f32[1,1536]{1,0:T(1,128)} %param.10) | copy-start | bytes 18436
  81.9 17.6 %collective-permute-start.2 = (bf16[192,1536]{1,0:T(8,128)(2,1)}, bf16[192,1536]{1,0:T(8,128)(2,1)S(1)}, u32[]{:S(2)}, u32[]{:S(2)}) collective-permute-start(bf16[192,1536]{1,0:T(8,128)(2,1)} %get-tuple-element.29), channel_id=1, source_target_pairs={{0,32},{32,2},{2,34},{34,4},{4,36},{36,6},{6,38},{38,0},{1,33},{33... | collective-permute-start | bytes 1769480 | tf_op jit(solution)/shard_map/ppermute | solution.py:160
  83.8 17.7 %collective-permute-start.3 = (bf16[192,1536]{1,0:T(8,128)(2,1)S(1)}, bf16[192,1536]{1,0:T(8,128)(2,1)S(1)}, u32[]{:S(2)}, u32[]{:S(2)}) collective-permute-start(bf16[192,1536]{1,0:T(8,128)(2,1)S(1)} %get-tuple-element.30), channel_id=1, source_target_pairs={{0,38},{32,0},{2,32},{34,2},{4,34},{36,4},{6,36},{38,6},{1,39},{33... | collective-permute-start | bytes 1769480 | tf_op jit(solution)/shard_map/ppermute | solution.py:161
  102.6 5.0 %collective-permute-start.4 = (bf16[192,1536]{1,0:T(8,128)(2,1)S(1)}, bf16[192,1536]{1,0:T(8,128)(2,1)S(1)}, u32[]{:S(2)}, u32[]{:S(2)}) collective-permute-start(bf16[192,1536]{1,0:T(8,128)(2,1)S(1)} %fusion.2), channel_id=1, source_target_pairs={{0,1},{1,0},{2,3},{3,2},{4,5},{5,4},{6,7},{7,6},{8,9},{9,8},{10,11... | collective-permute-start | bytes 1769480 | tf_op jit(solution)/shard_map/ppermute | solution.py:182

commit v13 on v12

--- a/solution.py
+++ b/solution.py
@@ -97,29 +97,54 @@
     return m_c, l_c, acc_c
 
 
-def attend_sides(flags, q, kv_prev, kv_next, m_c, l_c, acc_c):
+def step_kernel(flag_idx, final, flags_ref, q_ref, k_ref, v_ref, m_ref, l_ref, acc_ref, *outs):
+    s = scores_of(q_ref[...], k_ref, flags_ref[flag_idx] > 0)
+    m_c = m_ref[0]
+    top = jnp.maximum(m_c, jnp.max(s, axis=1, keepdims=True))
+    alpha = jnp.exp(m_c - top)
+    p = jnp.exp(s - top)
+    total = alpha * l_ref[0] + p.sum(axis=1, keepdims=True)
+    acc = alpha * acc_ref[...] + jnp.dot(
+        p.astype(jnp.bfloat16), v_ref[...], preferred_element_type=jnp.float32
+    )
+    if final:
+        outs[0][...] = (acc / total).astype(outs[0].dtype)
+    else:
+        outs[0][0] = top
+        outs[1][0] = total
+        outs[2][...] = acc
+
+
+def attend_step(flags, q, kv_side, m_c, l_c, acc_c, flag_idx, final):
     tl, width = q.shape
     heads = width // HD
     k_spec = pl.BlockSpec((None, tl, HD), lambda h, f: (0, 0, h))
     v_spec = pl.BlockSpec((None, tl, HD), lambda h, f: (1, 0, h))
     q_spec = pl.BlockSpec((tl, HD), lambda h, f: (0, h))
     stat_spec = pl.BlockSpec((1, tl, 1), lambda h, f: (h, 0, 0))
+    stat_shape = jax.ShapeDtypeStruct((heads, tl, 1), jnp.float32)
+    if final:
+        out_specs = q_spec
+        out_shape = jax.ShapeDtypeStruct((tl, width), jnp.bfloat16)
+    else:
+        out_specs = [stat_spec, stat_spec, q_spec]
+        out_shape = [stat_shape, stat_shape, jax.ShapeDtypeStruct((tl, width), jnp.float32)]
     tile_flops = heads * 2 * 2 * tl * tl * HD
     return pl.pallas_call(
-        side_kernel,
+        functools.partial(step_kernel, flag_idx, final),
         grid_spec=pltpu.PrefetchScalarGridSpec(
             num_scalar_prefetch=1,
             grid=(heads,),
-            in_specs=[q_spec, k_spec, v_spec, k_spec, v_spec, stat_spec, stat_spec, q_spec],
-            out_specs=q_spec,
-        ),
-        out_shape=jax.ShapeDtypeStruct((tl, width), jnp.bfloat16),
+            in_specs=[q_spec, k_spec, v_spec, stat_spec, stat_spec, q_spec],
+            out_specs=out_specs,
+        ),
+        out_shape=out_shape,
         cost_estimate=pl.CostEstimate(
-            flops=2 * tile_flops,
-            transcendentals=2 * heads * tl * tl,
-            bytes_accessed=tl * width * 2 * 6 + tl * width * 4,
-        ),
-    )(flags, q, kv_prev, kv_prev, kv_next, kv_next, m_c, l_c, acc_c)
+            flops=tile_flops,
+            transcendentals=heads * tl * tl,
+            bytes_accessed=tl * width * 2 * 3 + tl * width * 8,
+        ),
+    )(flags, q, kv_side, kv_side, m_c, l_c, acc_c)
 
 
 def local(queries, keys_values, window_offsets, out_weight, gate):
@@ -154,13 +179,13 @@
     half = own_rows.shape[0] // 2
     q = queries[0, 0, 0, 0]
     centre = attend_centre(flags, q, kv)
-    own_rows, kv_prev, kv_next, centre = lax.optimization_barrier(
-        (own_rows, kv_prev, kv_next, centre)
-    )
+    kv_prev, centre = lax.optimization_barrier((kv_prev, centre))
+    after_prev = attend_step(flags, q, kv_prev, *centre, 0, False)
+    own_rows, kv_next, after_prev = lax.optimization_barrier((own_rows, kv_next, after_prev))
     from_below = lax.ppermute(own_rows[:half], Y, up)
     from_above = lax.ppermute(own_rows[half:], Y, down)
 
-    attended = attend_sides(flags, q, kv_prev, kv_next, *centre)
+    attended = attend_step(flags, q, kv_next, *after_prev, 2, True)
 
     parity = lax.axis_index("ylo")
     split = attended.reshape(tl, zs, 2, -1)

time: 109 us -> 114 us (1.046)
  the two profiles are of different devices: /device:TPU:1 before, /device:TPU:7 now
where the time goes in v13:
time: 114 us; the launch traced here: 113 us
  waiting for transfers between devices  38.7 us (34%)
  starting transfers between devices  37.8 us (33%)
  Pallas kernels  27.9 us (24%)
  local copies, waits for them, and re-layouts  3.89 us (3%)
  matrix products  2.83 us (2%)
  other arithmetic  1.73 us (2%)
    ppermute x1, waiting for transfers between devices, local(): kv_prev = lax.ppermute(kv, TM, forward)  33.3 us
    pallas_call x2, Pallas kernels, attend_step(): pl.pallas_call(functools.partial(step_kernel, flag_idx, final), grid_spec...  18.4 us
    all_to_all x1, starting transfers between devices, local(): lax.all_to_all(spread, 'z', 0, 0, tiled=True)  15 us
    ppermute x1, starting transfers between devices, local(): from_below = lax.ppermute(own_rows[:half], Y, up)  8.6 us
    pallas_call x1, Pallas kernels, attend_centre(): pl.pallas_call(centre_kernel, grid_spec=pltpu.PrefetchScalarGridSpec(num_...  6.94 us
    ppermute x1, starting transfers between devices, local(): kv_prev = lax.ppermute(kv, TM, forward)  4.22 us
    ppermute x1, starting transfers between devices, local(): kv_next = lax.ppermute(kv, TM, backward)  4.07 us
    ppermute x1, starting transfers between devices, local(): got = lax.ppermute(sent, ROWS, [(0, 1), (1, 0)])  3.93 us
  transfers between devices with their start and end apart: 6, of which 4 were waited for; matrix products, arithmetic and copies ran while one was open for 4% of the time, Pallas kernels for 22%

profile of v13, /device:TPU:7, one launch (start us, length us, event | category | flops | bytes accessed | tf_op | source)
XLA Modules:
  0.0 113.0 jit_solution(3904358121611802001)
XLA Ops:
  0.0 0.0 copy-start.2
  0.0 2.6 %shard_map.64.k_ref.v_ref = bf16[2,384,768]{2,1,0:T(8,128)(2,1)} custom-call(bf16[384,2,768]{2,1,0:T(2,128)(2,1)} %bitcast.58), custom_call_target="tpu_custom_call" | custom-call | bytes 2359296 | tf_op jit(solution)/shard_map/pallas_call | solution.py:64
  2.6 0.0 copy-done.2
  2.6 1.1 %broadcast_in_dim.2 = bf16[12,32,1536]{2,1,0:T(8,128)(2,1)} broadcast(bf16[32,1536]{1,0:T(8,128)(2,1)S(1)} %copy-done.2), dimensions={1,2} | broadcast | bytes 1277952 | tf_op jit(solution)/shard_map/broadcast_in_dim | solution.py:162
  3.7 0.0 copy-start
  3.7 0.0 copy-start.5
  3.7 0.0 copy-start.4
  3.7 15.0 %all-to-all-start = ((bf16[12,32,1536]{2,1,0:T(8,128)(2,1)}), bf16[12,32,1536]{2,1,0:T(8,128)(2,1)S(1)}, u32[]{:S(2)}, u32[]{:S(2)}) async-start(bf16[12,32,1536]{2,1,0:T(8,128)(2,1)} %broadcast_in_dim.2), calls=%async_computation | async-start | bytes 2359296 | tf_op jit(solution)/shard_map/all_to_all | solution.py:164
  18.8 0.0 copy-done
  18.8 4.2 %collective-permute-start.1 = (bf16[2,384,768]{2,1,0:T(8,128)(2,1)S(1)}, bf16[2,384,768]{2,1,0:T(8,128)(2,1)}, u32[]{:S(2)}, u32[]{:S(2)}) collective-permute-start(bf16[2,384,768]{2,1,0:T(8,128)(2,1)S(1)} %copy-done), channel_id=1, source_target_pairs={{0,2},{2,4},{4,6},{6,8},{8,10},{10,12},{12,14},{14,16},{16,18},{18... | collective-permute-start | bytes 3538952 | tf_op jit(solution)/shard_map/ppermute | solution.py:158
  23.0 4.1 %collective-permute-start = (bf16[2,384,768]{2,1,0:T(8,128)(2,1)S(1)}, bf16[2,384,768]{2,1,0:T(8,128)(2,1)S(1)}, u32[]{:S(2)}, u32[]{:S(2)}) collective-permute-start(bf16[2,384,768]{2,1,0:T(8,128)(2,1)S(1)} %copy-done), channel_id=1, source_target_pairs={{2,0},{4,2},{6,4},{8,6},{10,8},{12,10},{14,12},{16,14},{18,16},{20... | collective-permute-start | bytes 3538952 | tf_op jit(solution)/shard_map/ppermute | solution.py:159
  27.1 0.0 copy-done.5
  27.1 0.0 copy-done.4
  27.1 0.2 and_reduce_fusion
  27.3 0.5 convert_element_type.12.flags_ref
  27.9 6.9 %shard_map.65 = (f32[6,384,1]{2,1,0:T(8,128)}, f32[6,384,1]{2,1,0:T(8,128)}, f32[384,768]{1,0:T(8,128)}) custom-call(s32[3]{0:T(128)} %convert_element_type.12.flags_ref, bf16[384,768]{1,0:T(8,128)(2,1)} %bitcast.48, bf16[2,384,768]{2,1,0:T(8,128)(2,1)} %shard_map.64.k_ref.v_ref, bf16[2,384,768]{2,1,0:T(8,128)(2,1)} %shard_map.64.k_ref.v_ref), custom_call_target="tpu_custom_call" | custom-call | flops 452984832 | bytes 2949120 | tf_op jit(solution)/shard_map/pallas_call | solution.py:82
  34.8 33.3 %collective-permute-done.1.k_ref.v_ref = bf16[2,384,768]{2,1,0:T(8,128)(2,1)} collective-permute-done((bf16[2,384,768]{2,1,0:T(8,128)(2,1)S(1)}, bf16[2,384,768]{2,1,0:T(8,128)(2,1)}, u32[]{:S(2)}, u32[]{:S(2)}) %collective-permute-start.1) | collective-permute-done | bytes 1179680 | tf_op jit(solution)/shard_map/ppermute | solution.py:158
  68.1 8.9 %shard_map.66 = (f32[6,384,1]{2,1,0:T(8,128)}, f32[6,384,1]{2,1,0:T(8,128)}, f32[384,768]{1,0:T(8,128)}) custom-call(s32[3]{0:T(128)} %convert_element_type.12.flags_ref, bf16[384,768]{1,0:T(8,128)(2,1)} %bitcast.49, bf16[2,384,768]{2,1,0:T(8,128)(2,1)} %collective-permute-done.1.k_ref.v_ref, bf16[2,384,768]{2,1,0:T(8,128)(2,1)} %collective-permute-done.1.k_ref.v_ref, ...), custom_call_target="tpu_custom_call" | custom-call | flops 452984832 | bytes 4128768 | tf_op jit(solution)/shard_map/pallas_call | solution.py:133
  77.0 3.0 %collective-permute-done.k_ref.v_ref = bf16[2,384,768]{2,1,0:T(8,128)(2,1)S(1)} collective-permute-done((bf16[2,384,768]{2,1,0:T(8,128)(2,1)S(1)}, bf16[2,384,768]{2,1,0:T(8,128)(2,1)S(1)}, u32[]{:S(2)}, u32[]{:S(2)}) %collective-permute-start) | collective-permute-done | bytes 1179680 | tf_op jit(solution)/shard_map/ppermute | solution.py:159
  80.0 0.0 copy-start.1
  80.0 0.0 all-to-all-done
  80.0 0.0 copy-start.3
  80.0 1.0 fusion.20
  81.0 0.3 copy-done.1
  81.3 8.6 %collective-permute-start.2 = (bf16[192,1536]{1,0:T(8,128)(2,1)}, bf16[192,1536]{1,0:T(8,128)(2,1)S(1)}, u32[]{:S(2)}, u32[]{:S(2)}) collective-permute-start(bf16[192,1536]{1,0:T(8,128)(2,1)} %get-tuple-element.41), channel_id=1, source_target_pairs={{0,32},{32,2},{2,34},{34,4},{4,36},{36,6},{6,38},{38,0},{1,33},{33... | collective-permute-start | bytes 1769480 | tf_op jit(solution)/shard_map/ppermute | solution.py:185
  89.9 1.9 %collective-permute-start.3 = (bf16[192,1536]{1,0:T(8,128)(2,1)S(1)}, bf16[192,1536]{1,0:T(8,128)(2,1)S(1)}, u32[]{:S(2)}, u32[]{:S(2)}) collective-permute-start(bf16[192,1536]{1,0:T(8,128)(2,1)S(1)} %get-tuple-element.42), channel_id=1, source_target_pairs={{0,38},{32,0},{2,32},{34,2},{4,34},{36,4},{6,36},{38,6},{1,39},{33... | collective-permute-start | bytes 1769480 | tf_op jit(solution)/shard_map/ppermute | solution.py:186
  91.8 0.0 copy-done.3
  91.9 9.5 %shard_map.67 = bf16[384,768]{1,0:T(8,128)(2,1)} custom-call(s32[3]{0:T(128)} %convert_element_type.12.flags_ref, bf16[384,768]{1,0:T(8,128)(2,1)} %bitcast.50, bf16[2,384,768]{2,1,0:T(8,128)(2,1)} %copy-done.1, bf16[2,384,768]{2,1,0:T(8,128)(2,1)} %copy-done.1, f32[6,384,1]{2,1,0:T(8,128)} %get-tuple-element.35.m_ref, ...), custom_call_target="tpu_custom_call" | custom-call | flops 452984832 | bytes 4128768 | tf_op jit(solution)/shard_map/pallas_call | solution.py:133
  101.4 1.4 %copy.8 = bf16[384,768]{0,1:T(8,128)(2,1)S(1)} copy(bf16[384,768]{1,0:T(8,128)(2,1)} %shard_map.67) | data formatting | bytes 1179648 | tf_op jit(solution)/shard_map/pallas_call | solution.py:133
  102.8 0.1 constant_dynamic-slice_fusion.1
  102.9 0.0 collective-permute-done.2
  102.9 0.4 fusion.8
  103.3 2.2 %collective-permute-done.3 = bf16[192,1536]{1,0:T(8,128)(2,1)S(1)} collective-permute-done((bf16[192,1536]{1,0:T(8,128)(2,1)S(1)}, bf16[192,1536]{1,0:T(8,128)(2,1)S(1)}, u32[]{:S(2)}, u32[]{:S(2)}) %collective-permute-start.3) | collective-permute-done | bytes 589856 | tf_op jit(solution)/shard_map/ppermute | solution.py:186
  105.5 0.4 fusion.6
  105.9 0.6 fusion.2
  106.5 3.9 %collective-permute-start.4 = (bf16[192,1536]{1,0:T(8,128)(2,1)S(1)}, bf16[192,1536]{1,0:T(8,128)(2,1)S(1)}, u32[]{:S(2)}, u32[]{:S(2)}) collective-permute-start(bf16[192,1536]{1,0:T(8,128)(2,1)S(1)} %fusion.2), channel_id=1, source_target_pairs={{0,1},{1,0},{2,3},{3,2},{4,5},{5,4},{6,7},{7,6},{8,9},{9,8},{10,11... | collective-permute-start | bytes 1769480 | tf_op jit(solution)/shard_map/ppermute | solution.py:207
  110.5 0.4 fusion.10
  110.9 0.4 fusion.12
  111.3 0.6 fusion
  111.9 0.2 collective-permute-done.4
  112.1 1.0 fusion.3
  (3 shorter events, 0.1 us)
Async XLA Ops:
  0.0 2.6 %copy-start.2 = (bf16[32,1536]{1,0:T(8,128)(2,1)S(1)}, bf16[32,1536]{1,0:T(8,128)(2,1)}, u32[]{:S(2)}) copy-start(bf16[32,1536]{1,0:T(8,128)(2,1)} %param.9) | copy-start | bytes 294916
  3.7 15.0 %copy-start = (bf16[2,384,768]{2,1,0:T(8,128)(2,1)S(1)}, bf16[2,384,768]{2,1,0:T(8,128)(2,1)}, u32[]{:S(2)}) copy-start(bf16[2,384,768]{2,1,0:T(8,128)(2,1)} %shard_map.64.k_ref.v_ref) | copy-start | bytes 3538948
  3.7 23.3 %copy-start.5 = (s32[3]{0:T(128)S(1)}, s32[3]{0:T(128)}, u32[]{:S(2)}) copy-start(s32[3]{0:T(128)} %constant.69.clone) | copy-start | bytes 40
  3.7 23.4 %copy-start.4 = (s32[1,1,1,1,3]{4,3,2,1,0:T(1,128)S(1)}, s32[1,1,1,1,3]{4,3,2,1,0:T(1,128)}, u32[]{:S(2)}) copy-start(s32[1,1,1,1,3]{4,3,2,1,0:T(1,128)} %param.8) | copy-start | bytes 40
  3.7 76.3 %all-to-all-start = ((bf16[12,32,1536]{2,1,0:T(8,128)(2,1)}), bf16[12,32,1536]{2,1,0:T(8,128)(2,1)S(1)}, u32[]{:S(2)}, u32[]{:S(2)}) async-start(bf16[12,32,1536]{2,1,0:T(8,128)(2,1)} %broadcast_in_dim.2), calls=%async_computation | async-start | bytes 2359296 | tf_op jit(solution)/shard_map/all_to_all | solution.py:164
  18.8 49.4 %collective-permute-start.1 = (bf16[2,384,768]{2,1,0:T(8,128)(2,1)S(1)}, bf16[2,384,768]{2,1,0:T(8,128)(2,1)}, u32[]{:S(2)}, u32[]{:S(2)}) collective-permute-start(bf16[2,384,768]{2,1,0:T(8,128)(2,1)S(1)} %copy-done), channel_id=1, source_target_pairs={{0,2},{2,4},{4,6},{6,8},{8,10},{10,12},{12,14},{14,16},{16,18},{18... | collective-permute-start | bytes 3538952 | tf_op jit(solution)/shard_map/ppermute | solution.py:158
  23.0 57.0 %collective-permute-start = (bf16[2,384,768]{2,1,0:T(8,128)(2,1)S(1)}, bf16[2,384,768]{2,1,0:T(8,128)(2,1)S(1)}, u32[]{:S(2)}, u32[]{:S(2)}) collective-permute-start(bf16[2,384,768]{2,1,0:T(8,128)(2,1)S(1)} %copy-done), channel_id=1, source_target_pairs={{2,0},{4,2},{6,4},{8,6},{10,8},{12,10},{14,12},{16,14},{18,16},{20... | collective-permute-start | bytes 3538952 | tf_op jit(solution)/shard_map/ppermute | solution.py:159
  80.0 1.3 %copy-start.1 = (bf16[2,384,768]{2,1,0:T(8,128)(2,1)}, bf16[2,384,768]{2,1,0:T(8,128)(2,1)S(1)}, u32[]{:S(2)}) copy-start(bf16[2,384,768]{2,1,0:T(8,128)(2,1)S(1)} %collective-permute-done.k_ref.v_ref) | copy-start | bytes 3538948
  80.0 11.8 %copy-start.3 = (f32[1,1536]{1,0:T(1,128)S(1)}, f32[1,1536]{1,0:T(1,128)}, u32[]{:S(2)}) copy-start(f32[1,1536]{1,0:T(1,128)} %param.10) | copy-start | bytes 18436
  81.3 21.6 %collective-permute-start.2 = (bf16[192,1536]{1,0:T(8,128)(2,1)}, bf16[192,1536]{1,0:T(8,128)(2,1)S(1)}, u32[]{:S(2)}, u32[]{:S(2)}) collective-permute-start(bf16[192,1536]{1,0:T(8,128)(2,1)} %get-tuple-element.41), channel_id=1, source_target_pairs={{0,32},{32,2},{2,34},{34,4},{4,36},{36,6},{6,38},{38,0},{1,33},{33... | collective-permute-start | bytes 1769480 | tf_op jit(solution)/shard_map/ppermute | solution.py:185
  89.9 15.6 %collective-permute-start.3 = (bf16[192,1536]{1,0:T(8,128)(2,1)S(1)}, bf16[192,1536]{1,0:T(8,128)(2,1)S(1)}, u32[]{:S(2)}, u32[]{:S(2)}) collective-permute-start(bf16[192,1536]{1,0:T(8,128)(2,1)S(1)} %get-tuple-element.42), channel_id=1, source_target_pairs={{0,38},{32,0},{2,32},{34,2},{4,34},{36,4},{6,36},{38,6},{1,39},{33... | collective-permute-start | bytes 1769480 | tf_op jit(solution)/shard_map/ppermute | solution.py:186
  106.5 5.6 %collective-permute-start.4 = (bf16[192,1536]{1,0:T(8,128)(2,1)S(1)}, bf16[192,1536]{1,0:T(8,128)(2,1)S(1)}, u32[]{:S(2)}, u32[]{:S(2)}) collective-permute-start(bf16[192,1536]{1,0:T(8,128)(2,1)S(1)} %fusion.2), channel_id=1, source_target_pairs={{0,1},{1,0},{2,3},{3,2},{4,5},{5,4},{6,7},{7,6},{8,9},{9,8},{10,11... | collective-permute-start | bytes 1769480 | tf_op jit(solution)/shard_map/ppermute | solution.py:207

commit v14 on v12

--- a/solution.py
+++ b/solution.py
@@ -171,16 +171,23 @@
     band = tl // bands
     me = lax.axis_index(ROWS)
 
-    def project(start):
+    def near(start):
         own = lax.dynamic_slice_in_dim(a_own, start, band, axis=0)
-        far = lax.dynamic_slice_in_dim(a_other, start, band, axis=0)
-        part = jnp.dot(own, own_rows, preferred_element_type=jnp.float32)
-        part = part + jnp.dot(far[:, :half], from_below, preferred_element_type=jnp.float32)
-        return part + jnp.dot(far[:, half:], from_above, preferred_element_type=jnp.float32)
-
-    sent = project((1 - me) * band).astype(jnp.bfloat16)
+        return jnp.dot(own, own_rows, preferred_element_type=jnp.float32)
+
+    def far(start, part):
+        other = lax.dynamic_slice_in_dim(a_other, start, band, axis=0)
+        part = part + jnp.dot(other[:, :half], from_below, preferred_element_type=jnp.float32)
+        return part + jnp.dot(other[:, half:], from_above, preferred_element_type=jnp.float32)
+
+    near_sent = near((1 - me) * band)
+    near_kept = near(me * band)
+    near_sent, near_kept, from_below, from_above = lax.optimization_barrier(
+        (near_sent, near_kept, from_below, from_above)
+    )
+    sent = far((1 - me) * band, near_sent).astype(jnp.bfloat16)
     got = lax.ppermute(sent, ROWS, [(0, 1), (1, 0)])
-    kept = lax.optimization_barrier(project(me * band))
+    kept = lax.optimization_barrier(far(me * band, near_kept))
     projection = kept + got.astype(jnp.float32)
     mixed = (gate[0][None, :] * projection).astype(jnp.bfloat16)
     return mixed.reshape(1, 1, 1, 1, band, DOUT)

time: 109 us -> 118 us (1.083)
  waiting for transfers between devices: 50.8 us -> 60.7 us
    ppermute x1, waiting for transfers between devices: 0.89 us -> 9.59 us  [local(): from_below = lax.ppermute(own_rows[:half], Y, up)]
  transfers between devices with their start and end apart: 6 -> 6, of which waited for: 5 -> 5; matrix products, arithmetic and copies ran while one was open for 4% -> 2% of each run, Pallas kernels for 14% -> 6%
where the time goes in v14:
time: 118 us
  waiting for transfers between devices  60.7 us (51%)
  starting transfers between devices  31.3 us (27%)
  Pallas kernels  18 us (15%)
  matrix products  2.85 us (2%)
  local copies, waits for them, and re-layouts  2.67 us (2%)
  other arithmetic  1.78 us (2%)
    ppermute x1, waiting for transfers between devices, local(): kv_prev = lax.ppermute(kv, TM, forward)  32.2 us
    ppermute x1, waiting for transfers between devices, local(): kv_next = lax.ppermute(kv, TM, backward)  15.9 us
    all_to_all x1, starting transfers between devices, local(): lax.all_to_all(spread, 'z', 0, 0, tiled=True)  15.8 us
    ppermute x1, waiting for transfers between devices, local(): from_below = lax.ppermute(own_rows[:half], Y, up)  9.59 us
    pallas_call x1, Pallas kernels, attend_sides(): pl.pallas_call(side_kernel, grid_spec=pltpu.PrefetchScalarGridSpec(num_sc...  8.63 us
    pallas_call x1, Pallas kernels, attend_centre(): pl.pallas_call(centre_kernel, grid_spec=pltpu.PrefetchScalarGridSpec(num_...  6.78 us
    ppermute x1, starting transfers between devices, local(): from_above = lax.ppermute(own_rows[half:], Y, down)  4.57 us
    ppermute x1, starting transfers between devices, local(): kv_prev = lax.ppermute(kv, TM, forward)  4.29 us
  transfers between devices with their start and end apart: 6, of which 5 were waited for; matrix products, arithmetic and copies ran while one was open for 2% of the time, Pallas kernels for 6%

profile of v14, /device:TPU:1, one launch (start us, length us, event | category | flops | bytes accessed | tf_op | source)
XLA Modules:
  0.0 117.5 jit_solution(13810672519490836729)
XLA Ops:
  0.0 0.0 copy-start.2
  0.0 2.6 %shard_map.64.k_ref.v_ref = bf16[2,384,768]{2,1,0:T(8,128)(2,1)} custom-call(bf16[384,2,768]{2,1,0:T(2,128)(2,1)} %bitcast.57), custom_call_target="tpu_custom_call" | custom-call | bytes 2359296 | tf_op jit(solution)/shard_map/pallas_call | solution.py:64
  2.6 0.0 copy-done.2
  2.6 1.1 broadcast_in_dim.2
  3.8 0.0 copy-start
  3.8 0.0 copy-start.5
  3.8 0.0 copy-start.4
  3.8 0.0 copy-start.3
  3.8 15.8 %all-to-all-start = ((bf16[12,32,1536]{2,1,0:T(8,128)(2,1)}), bf16[12,32,1536]{2,1,0:T(8,128)(2,1)S(1)}, u32[]{:S(2)}, u32[]{:S(2)}) async-start(bf16[12,32,1536]{2,1,0:T(8,128)(2,1)} %broadcast_in_dim.2), calls=%async_computation | async-start | bytes 2359296 | tf_op jit(solution)/shard_map/all_to_all | solution.py:139
  19.6 0.0 copy-done
  19.6 4.3 %collective-permute-start = (bf16[2,384,768]{2,1,0:T(8,128)(2,1)S(1)}, bf16[2,384,768]{2,1,0:T(8,128)(2,1)S(1)}, u32[]{:S(2)}, u32[]{:S(2)}) collective-permute-start(bf16[2,384,768]{2,1,0:T(8,128)(2,1)S(1)} %copy-done), channel_id=1, source_target_pairs={{0,2},{2,4},{4,6},{6,8},{8,10},{10,12},{12,14},{14,16},{16,18},{18... | collective-permute-start | bytes 3538952 | tf_op jit(solution)/shard_map/ppermute | solution.py:133
  23.9 1.3 %collective-permute-start.1 = (bf16[2,384,768]{2,1,0:T(8,128)(2,1)S(1)}, bf16[2,384,768]{2,1,0:T(8,128)(2,1)}, u32[]{:S(2)}, u32[]{:S(2)}) collective-permute-start(bf16[2,384,768]{2,1,0:T(8,128)(2,1)S(1)} %copy-done), channel_id=1, source_target_pairs={{2,0},{4,2},{6,4},{8,6},{10,8},{12,10},{14,12},{16,14},{18,16},{20... | collective-permute-start | bytes 3538952 | tf_op jit(solution)/shard_map/ppermute | solution.py:134
  25.2 0.0 copy-done.5
  25.3 0.0 copy-done.4
  25.3 0.2 and_reduce_fusion
  25.5 0.6 convert_element_type.12.flags_ref
  26.1 0.0 copy-done.3
  26.1 6.8 %shard_map.65 = (f32[6,384,1]{2,1,0:T(8,128)}, f32[6,384,1]{2,1,0:T(8,128)}, f32[384,768]{1,0:T(8,128)}) custom-call(s32[3]{0:T(128)} %convert_element_type.12.flags_ref, bf16[384,768]{1,0:T(8,128)(2,1)} %bitcast.48, bf16[2,384,768]{2,1,0:T(8,128)(2,1)} %shard_map.64.k_ref.v_ref, bf16[2,384,768]{2,1,0:T(8,128)(2,1)} %shard_map.64.k_ref.v_ref), custom_call_target="tpu_custom_call" | custom-call | flops 452984832 | bytes 2949120 | tf_op jit(solution)/shard_map/pallas_call | solution.py:82
  32.9 32.2 %collective-permute-done.kp_ref.vp_ref = bf16[2,384,768]{2,1,0:T(8,128)(2,1)S(1)} collective-permute-done((bf16[2,384,768]{2,1,0:T(8,128)(2,1)S(1)}, bf16[2,384,768]{2,1,0:T(8,128)(2,1)S(1)}, u32[]{:S(2)}, u32[]{:S(2)}) %collective-permute-start) | collective-permute-done | bytes 1179680 | tf_op jit(solution)/shard_map/ppermute | solution.py:133
  65.1 0.0 copy-start.1
  65.1 15.9 %collective-permute-done.1.kn_ref.vn_ref = bf16[2,384,768]{2,1,0:T(8,128)(2,1)} collective-permute-done((bf16[2,384,768]{2,1,0:T(8,128)(2,1)S(1)}, bf16[2,384,768]{2,1,0:T(8,128)(2,1)}, u32[]{:S(2)}, u32[]{:S(2)}) %collective-permute-start.1) | collective-permute-done | bytes 1179680 | tf_op jit(solution)/shard_map/ppermute | solution.py:134
  81.0 0.0 all-to-all-done
  81.0 0.0 copy-done.1
  81.0 8.6 %shard_map.66 = bf16[384,768]{1,0:T(8,128)(2,1)} custom-call(s32[3]{0:T(128)} %convert_element_type.12.flags_ref, bf16[384,768]{1,0:T(8,128)(2,1)} %bitcast.49, bf16[2,384,768]{2,1,0:T(8,128)(2,1)} %copy-done.1, bf16[2,384,768]{2,1,0:T(8,128)(2,1)} %copy-done.1, bf16[2,384,768]{2,1,0:T(8,128)(2,1)} %collective-permute-done.1.kn_ref.vn_ref, ...), custom_call_target="tpu_custom_call" | custom-call | flops 905969664 | bytes 4718592 | tf_op jit(solution)/shard_map/pallas_call | solution.py:108
  89.6 1.4 %copy.8 = bf16[384,768]{0,1:T(8,128)(2,1)S(1)} copy(bf16[384,768]{1,0:T(8,128)(2,1)} %shard_map.66) | data formatting | bytes 1179648 | tf_op jit(solution)/shard_map/pallas_call | solution.py:108
  91.0 0.1 fusion.23
  91.1 1.9 %collective-permute-start.2 = (bf16[192,1536]{1,0:T(8,128)(2,1)S(1)}, bf16[192,1536]{1,0:T(8,128)(2,1)S(1)}, u32[]{:S(2)}, u32[]{:S(2)}) collective-permute-start(bf16[192,1536]{1,0:T(8,128)(2,1)S(1)} %get-tuple-element.38), channel_id=1, source_target_pairs={{0,32},{32,2},{2,34},{34,4},{4,36},{36,6},{6,38},{38,0},{1,33},{33... | collective-permute-start | bytes 1769480 | tf_op jit(solution)/shard_map/ppermute | solution.py:160
  93.0 4.6 %collective-permute-start.3 = (bf16[192,1536]{1,0:T(8,128)(2,1)S(1)}, bf16[192,1536]{1,0:T(8,128)(2,1)S(1)}, u32[]{:S(2)}, u32[]{:S(2)}) collective-permute-start(bf16[192,1536]{1,0:T(8,128)(2,1)S(1)} %get-tuple-element.37), channel_id=1, source_target_pairs={{0,38},{32,0},{2,32},{34,2},{4,34},{36,4},{6,36},{38,6},{1,39},{33... | collective-permute-start | bytes 1769480 | tf_op jit(solution)/shard_map/ppermute | solution.py:161
  97.6 0.1 constant_dynamic-slice_fusion
  97.7 0.6 fusion.3
  98.3 0.6 fusion.1
  98.9 9.6 %collective-permute-done.2 = bf16[192,1536]{1,0:T(8,128)(2,1)S(1)} collective-permute-done((bf16[192,1536]{1,0:T(8,128)(2,1)S(1)}, bf16[192,1536]{1,0:T(8,128)(2,1)S(1)}, u32[]{:S(2)}, u32[]{:S(2)}) %collective-permute-start.2) | collective-permute-done | bytes 589856 | tf_op jit(solution)/shard_map/ppermute | solution.py:160
  108.5 2.3 %collective-permute-done.3 = bf16[192,1536]{1,0:T(8,128)(2,1)S(1)} collective-permute-done((bf16[192,1536]{1,0:T(8,128)(2,1)S(1)}, bf16[192,1536]{1,0:T(8,128)(2,1)S(1)}, u32[]{:S(2)}, u32[]{:S(2)}) %collective-permute-start.3) | collective-permute-done | bytes 589856 | tf_op jit(solution)/shard_map/ppermute | solution.py:161
  110.7 0.4 fusion.9
  111.1 0.4 add_convert_fusion
  111.6 3.4 %collective-permute-start.4 = (bf16[192,1536]{1,0:T(8,128)(2,1)S(1)}, bf16[192,1536]{1,0:T(8,128)(2,1)S(1)}, u32[]{:S(2)}, u32[]{:S(2)}) collective-permute-start(bf16[192,1536]{1,0:T(8,128)(2,1)S(1)} %add_convert_fusion), channel_id=1, source_target_pairs={{0,1},{1,0},{2,3},{3,2},{4,5},{5,4},{6,7},{7,6},{8,9},{9,8},{10,11... | collective-permute-start | bytes 1769480 | tf_op jit(solution)/shard_map/ppermute | solution.py:189
  115.0 0.4 fusion.15
  115.4 0.4 add_add_fusion
  115.8 0.8 collective-permute-done.4
  116.6 1.0 fusion
  (3 shorter events, 0.1 us)
Async XLA Ops:
  0.0 2.6 %copy-start.2 = (bf16[32,1536]{1,0:T(8,128)(2,1)S(1)}, bf16[32,1536]{1,0:T(8,128)(2,1)}, u32[]{:S(2)}) copy-start(bf16[32,1536]{1,0:T(8,128)(2,1)} %param.9) | copy-start | bytes 294916
  3.8 15.9 %copy-start = (bf16[2,384,768]{2,1,0:T(8,128)(2,1)S(1)}, bf16[2,384,768]{2,1,0:T(8,128)(2,1)}, u32[]{:S(2)}) copy-start(bf16[2,384,768]{2,1,0:T(8,128)(2,1)} %shard_map.64.k_ref.v_ref) | copy-start | bytes 3538948
  3.8 21.5 %copy-start.5 = (s32[3]{0:T(128)S(1)}, s32[3]{0:T(128)}, u32[]{:S(2)}) copy-start(s32[3]{0:T(128)} %constant.69.clone) | copy-start | bytes 40
  3.8 21.5 %copy-start.4 = (s32[1,1,1,1,3]{4,3,2,1,0:T(1,128)S(1)}, s32[1,1,1,1,3]{4,3,2,1,0:T(1,128)}, u32[]{:S(2)}) copy-start(s32[1,1,1,1,3]{4,3,2,1,0:T(1,128)} %param.8) | copy-start | bytes 40
  3.8 22.3 %copy-start.3 = (f32[1,1536]{1,0:T(1,128)S(1)}, f32[1,1536]{1,0:T(1,128)}, u32[]{:S(2)}) copy-start(f32[1,1536]{1,0:T(1,128)} %param.10) | copy-start | bytes 18436
  3.8 77.2 %all-to-all-start = ((bf16[12,32,1536]{2,1,0:T(8,128)(2,1)}), bf16[12,32,1536]{2,1,0:T(8,128)(2,1)S(1)}, u32[]{:S(2)}, u32[]{:S(2)}) async-start(bf16[12,32,1536]{2,1,0:T(8,128)(2,1)} %broadcast_in_dim.2), calls=%async_computation | async-start | bytes 2359296 | tf_op jit(solution)/shard_map/all_to_all | solution.py:139
  19.6 45.5 %collective-permute-start = (bf16[2,384,768]{2,1,0:T(8,128)(2,1)S(1)}, bf16[2,384,768]{2,1,0:T(8,128)(2,1)S(1)}, u32[]{:S(2)}, u32[]{:S(2)}) collective-permute-start(bf16[2,384,768]{2,1,0:T(8,128)(2,1)S(1)} %copy-done), channel_id=1, source_target_pairs={{0,2},{2,4},{4,6},{6,8},{8,10},{10,12},{12,14},{14,16},{16,18},{18... | collective-permute-start | bytes 3538952 | tf_op jit(solution)/shard_map/ppermute | solution.py:133
  23.9 57.0 %collective-permute-start.1 = (bf16[2,384,768]{2,1,0:T(8,128)(2,1)S(1)}, bf16[2,384,768]{2,1,0:T(8,128)(2,1)}, u32[]{:S(2)}, u32[]{:S(2)}) collective-permute-start(bf16[2,384,768]{2,1,0:T(8,128)(2,1)S(1)} %copy-done), channel_id=1, source_target_pairs={{2,0},{4,2},{6,4},{8,6},{10,8},{12,10},{14,12},{16,14},{18,16},{20... | collective-permute-start | bytes 3538952 | tf_op jit(solution)/shard_map/ppermute | solution.py:134
  65.1 15.9 %copy-start.1 = (bf16[2,384,768]{2,1,0:T(8,128)(2,1)}, bf16[2,384,768]{2,1,0:T(8,128)(2,1)S(1)}, u32[]{:S(2)}) copy-start(bf16[2,384,768]{2,1,0:T(8,128)(2,1)S(1)} %collective-permute-done.kp_ref.vp_ref) | copy-start | bytes 3538948
  91.1 17.4 %collective-permute-start.2 = (bf16[192,1536]{1,0:T(8,128)(2,1)S(1)}, bf16[192,1536]{1,0:T(8,128)(2,1)S(1)}, u32[]{:S(2)}, u32[]{:S(2)}) collective-permute-start(bf16[192,1536]{1,0:T(8,128)(2,1)S(1)} %get-tuple-element.38), channel_id=1, source_target_pairs={{0,32},{32,2},{2,34},{34,4},{4,36},{36,6},{6,38},{38,0},{1,33},{33... | collective-permute-start | bytes 1769480 | tf_op jit(solution)/shard_map/ppermute | solution.py:160
  93.0 17.7 %collective-permute-start.3 = (bf16[192,1536]{1,0:T(8,128)(2,1)S(1)}, bf16[192,1536]{1,0:T(8,128)(2,1)S(1)}, u32[]{:S(2)}, u32[]{:S(2)}) collective-permute-start(bf16[192,1536]{1,0:T(8,128)(2,1)S(1)} %get-tuple-element.37), channel_id=1, source_target_pairs={{0,38},{32,0},{2,32},{34,2},{4,34},{36,4},{6,36},{38,6},{1,39},{33... | collective-permute-start | bytes 1769480 | tf_op jit(solution)/shard_map/ppermute | solution.py:161
  111.6 5.0 %collective-permute-start.4 = (bf16[192,1536]{1,0:T(8,128)(2,1)S(1)}, bf16[192,1536]{1,0:T(8,128)(2,1)S(1)}, u32[]{:S(2)}, u32[]{:S(2)}) collective-permute-start(bf16[192,1536]{1,0:T(8,128)(2,1)S(1)} %add_convert_fusion), channel_id=1, source_target_pairs={{0,1},{1,0},{2,3},{3,2},{4,5},{5,4},{6,7},{7,6},{8,9},{9,8},{10,11... | collective-permute-start | bytes 1769480 | tf_op jit(solution)/shard_map/ppermute | solution.py:189
